TPU v7x, 256 devices: a whole 4x4x8 slice. The times are simulated.
256 devices in a mesh: row: 4 (over y), col: 64 (over z, x, core).
Axes of the slice: x: 4, y: 4, z: 8, core: 2. Of those that a mesh axis runs over, the one named last changes fastest.
Arguments:
- tokens: bfloat16 [32768, 4096], P(('row', 'col')), may hold values from -6 to 6
- expert_ids: int32 [32768, 2], P(('row', 'col')), may hold values from 0 to 63, all different within a row; in each aligned block of 128 rows (0 to 127, 128 to 255, ...) at most 5 rows name the same one
- gate_weights: float32 [32768, 2], P(('row', 'col')), may hold values from 0.1 to 1
- w_gate: bfloat16 [64, 4096, 1536], P('col', None, 'row'), may hold values from -0.09375 to 0.09375
- w_up: bfloat16 [64, 4096, 1536], P('col', None, 'row'), may hold values from -0.09375 to 0.09375
- w_down: bfloat16 [64, 1536, 4096], P('col', None, 'row'), may hold values from -0.15625 to 0.15625
Outputs:
- moe_out: bfloat16 [32768, 4096], P(('row', 'col'))
Inputs may be any that keep to these rules, and one draw needn't show every extreme that they name: `expert_ids`: each row names 2 different experts. Among the 128 rows of one device no expert is named by more than 5 rows, and in every draw some expert is named by exactly 5 rows of some device.
All inputs are finite; a program needn't handle non-finite values.
Results may differ from a plain program's by a relative error of at most 0.0058.
Values may be sent and summed in bfloat16 or wider, within the bound.
No kernel may reach another device: no remote copies, remote signals or barrier semaphores. Data moves between devices by JAX's collectives and lax.ppermute only.
A program may use at most 128 MiB of HBM per device.

v0:
```python
import jax
import jax.numpy as jnp
from jax import lax
from jax.sharding import PartitionSpec as P

CHUNKS = ((0, 3), (3, 5))


def local(tokens, expert_ids, gate_weights, w_gate, w_up, w_down):
    token_count, top_count = expert_ids.shape
    width = tokens.shape[1]
    unit_count = w_gate.shape[2]
    quarter = w_down.shape[2]
    columns = lax.axis_size("col")
    groups = lax.axis_size("row")
    experts = w_gate.shape[0] * columns
    capacity = max(2, token_count * top_count * 5 // (4 * experts))
    flat_ids = expert_ids.reshape(-1)
    onehot = (flat_ids[:, None] == jnp.arange(experts, dtype=jnp.int32)[None, :]).astype(jnp.int32)
    earlier = jnp.cumsum(onehot, axis=0) - onehot
    position = jnp.sum(earlier * onehot, axis=1)
    slot_ids = (flat_ids * capacity + position).reshape(token_count, top_count)
    shares = gate_weights / jnp.sum(gate_weights, axis=1, keepdims=True)

    meta = jnp.concatenate([slot_ids.astype(jnp.float32), shares], axis=1)
    meta = lax.all_gather(meta, "row", axis=0, tiled=False)
    all_slots = meta[:, :, :top_count]
    all_shares = meta[:, :, top_count:]

    w_down_parts = w_down[0].reshape(groups, unit_count, quarter)
    combined = jnp.zeros((groups, token_count, quarter), jnp.float32)
    for lo, hi in CHUNKS:
        span = hi - lo
        wanted = (
            jnp.arange(experts, dtype=jnp.int32)[:, None] * capacity
            + jnp.arange(lo, hi, dtype=jnp.int32)[None, :]
        ).reshape(-1)
        chooser = jnp.any(
            wanted[:, None, None] == slot_ids[None, :, :], axis=2
        ).astype(jnp.bfloat16)
        outgoing = jnp.dot(chooser, tokens, preferred_element_type=jnp.float32).astype(jnp.bfloat16)
        outgoing = outgoing.reshape(columns, span, width)
        arrived = lax.all_to_all(outgoing, "col", split_axis=0, concat_axis=0, tiled=True)
        rows = lax.all_gather(arrived, "row", axis=0, tiled=False)
        rows = rows.transpose(2, 0, 1, 3).reshape(span * groups * columns, width)
        gate_part = jnp.dot(rows, w_gate[0], preferred_element_type=jnp.float32)
        up_part = jnp.dot(rows, w_up[0], preferred_element_type=jnp.float32)
        hidden = (jax.nn.silu(gate_part) * up_part).astype(jnp.bfloat16)
        hidden_all = lax.all_gather(hidden, "row", axis=0, tiled=False)
        result = jnp.einsum(
            "jnu,juf->nf", hidden_all, w_down_parts, preferred_element_type=jnp.float32
        ).astype(jnp.bfloat16)
        result = result.reshape(span, groups, columns, quarter).transpose(2, 1, 0, 3)
        back = lax.all_to_all(result, "col", split_axis=0, concat_axis=0, tiled=True)
        match = (all_slots[:, :, :, None] == wanted.astype(jnp.float32)[None, None, None, :])
        weights = jnp.sum(jnp.where(match, all_shares[:, :, :, None], 0.0), axis=2)
        weights = weights.reshape(groups, token_count, experts, span)
        combined = combined + jnp.einsum(
            "rtep,erpf->rtf", weights, back.astype(jnp.float32),
            precision=lax.Precision.HIGHEST, preferred_element_type=jnp.float32,
        )
    combined = combined.astype(jnp.bfloat16)
    home = lax.all_to_all(combined, "row", split_axis=0, concat_axis=0, tiled=True)
    return home.transpose(1, 0, 2).reshape(token_count, width)


def solution(mesh):
    placed = (
        P(("row", "col"), None),
        P(("row", "col"), None),
        P(("row", "col"), None),
        P("col", None, "row"),
        P("col", None, "row"),
        P("col", None, "row"),
    )
    return jax.shard_map(
        local, mesh=mesh, in_specs=placed, out_specs=P(("row", "col"), None), check_vma=False
    )
```

profile of v0, /device:TPU:4, one launch (start us, length us, event | category | flops | bytes accessed | tf_op | source)
XLA Modules:
  0.0 368.6 jit_solution(17993576208528898447)
XLA Ops:
  6.5 0.9 copy.94
  7.5 0.1 eq.81
  7.6 0.1 eq.77
  7.8 0.1 add.96
  8.0 0.6 reduce-window.6
  8.6 0.2 slice_reduce_fusion
  8.8 0.1 fusion.28
  8.9 0.1 reduce_sum.39
  9.2 0.7 fusion.30
  9.9 0.1 compare_reduce_fusion
  10.0 2.9 convolution_convert_fusion
  12.9 4.1 %reshape.121 = bf16[64,3,4096]{2,1,0:T(4,128)(2,1)} reshape(bf16[192,4096]{1,0:T(8,128)(2,1)} %convolution_convert_fusion) | data formatting | bytes 3145728 | tf_op jit(solution)/shard_map/reshape | solution.py:42
  17.0 63.3 %all_to_all.25 = bf16[64,3,4096]{2,1,0:T(4,128)(2,1)S(1)} all-to-all(bf16[64,3,4096]{2,1,0:T(4,128)(2,1)} %reshape.121), channel_id=1, replica_groups=mesh['row'=4,'col'=64] {'col'}, dimensions={0} | all-to-all | bytes 3145728 | tf_op jit(solution)/shard_map/all_to_all | solution.py:43
  80.3 2.3 copy.101
  82.6 0.1 broadcast_add_fusion
  82.7 0.1 add.102
  82.8 0.1 compare_reduce_fusion.1
  82.9 2.6 convolution_convert_fusion.1
  85.6 2.5 reshape.125
  88.1 34.3 %all_to_all.26 = bf16[64,2,4096]{2,1,0:T(2,128)(2,1)} all-to-all(bf16[64,2,4096]{2,1,0:T(2,128)(2,1)} %reshape.125), channel_id=1, replica_groups=mesh['row'=4,'col'=64] {'col'}, dimensions={0} | all-to-all | bytes 2097152 | tf_op jit(solution)/shard_map/all_to_all | solution.py:43
  122.5 0.2 all-gather.12.cloned.1.call-start
  122.7 24.6 %all-gather.10.cloned.1.call-done = bf16[256,3,4096]{2,0,1:T(8,128)(2,1)} async-done(((bf16[64,3,4096]{2,0,1:T(8,128)(2,1)}), bf16[256,3,4096]{2,0,1:T(8,128)(2,1)}) %all-gather.10.cloned.1.call-update) | async-done | bytes 6291472 | tf_op jit(solution)/shard_map/all_gather | solution.py:44
  147.3 6.6 %fusion.6 = f32[768,384]{1,0:T(8,128)S(1)} fusion(bf16[768,4096]{1,0:T(8,128)(2,1)} %bitcast.100, bf16[1,4096,384]{2,1,0:T(8,128)(2,1)} %param.9), kind=kOutput, calls=%fused_computation.9 | convolution fusion | flops 2415919104 | bytes 10616832 | tf_op jit(solution)/shard_map/dot_general | solution.py:46
  153.9 4.3 %fusion.14 = bf16[768,384]{1,0:T(8,128)(2,1)} fusion(bf16[768,4096]{1,0:T(8,128)(2,1)S(1)} %bitcast.101, bf16[1,4096,384]{2,1,0:T(8,128)(2,1)S(1)} %copy-done.5, f32[768,384]{1,0:T(8,128)S(1)} %fusion.6), kind=kOutput, calls=%fused_computation.18 | convolution fusion | flops 2417688576 | bytes 11206656 | tf_op jit(solution)/shard_map/dot_general | solution.py:47
  158.2 42.5 %all-gather.14.cloned.1.call-done = bf16[256,2,4096]{2,1,0:T(2,128)(2,1)} async-done(((bf16[64,2,4096]{2,1,0:T(2,128)(2,1)}), bf16[256,2,4096]{2,1,0:T(2,128)(2,1)}) %all-gather.14.cloned.1.call-update) | async-done | bytes 4194320 | tf_op jit(solution)/shard_map/all_gather | solution.py:44
  200.7 5.3 %copy.108 = bf16[256,2,4096]{2,0,1:T(8,128)(2,1)S(1)} copy(bf16[256,2,4096]{2,1,0:T(2,128)(2,1)} %all-gather.14.cloned.1.call-done) | data formatting | bytes 8388608 | tf_op jit(solution)/shard_map/all_gather | solution.py:44
  206.0 1.9 copy-done.1
  207.9 3.2 fusion.4
  211.1 27.4 %all-gather.12.cloned.1.call-done = bf16[3072,384]{1,0:T(8,128)(2,1)} async-done(((bf16[768,384]{1,0:T(8,128)(2,1)}), bf16[3072,384]{1,0:T(8,128)(2,1)}) %all-gather.12.cloned.1.call-update) | async-done | bytes 2359312 | tf_op jit(solution)/shard_map/all_gather | solution.py:49
  238.5 4.3 %bitcast_convert_fusion = bf16[768,1024]{1,0:T(8,128)(2,1)S(1)} fusion(bf16[4,768,384]{2,1,0:T(8,128)(2,1)} %bitcast.102, bf16[4,384,1024]{2,1,0:T(8,128)(2,1)S(1)} %bitcast.88), kind=kOutput, calls=%fused_computation.2 | convolution fusion | flops 2416705536 | bytes 7077888 | tf_op jit(solution)/shard_map/jnu,juf->nf/dot_general | solution.py:50
  242.7 2.4 copy.128
  245.2 10.7 %all-to-all-start.1 = ((bf16[64,4,3,1024]{3,1,2,0:T(4,128)(2,1)}), bf16[64,4,3,1024]{3,1,2,0:T(4,128)(2,1)}, u32[]{:S(2)}, u32[]{:S(2)}) async-start(bf16[64,4,3,1024]{3,1,2,0:T(4,128)(2,1)} %bitcast.90), calls=%async_computation.1 | async-start | bytes 3145728 | tf_op jit(solution)/shard_map/all_to_all | solution.py:54
  255.9 6.4 %fusion.20 = bf16[512,384]{1,0:T(8,128)(2,1)} fusion(bf16[512,4096]{1,0:T(8,128)(2,1)} %bitcast.92, bf16[1,4096,384]{2,1,0:T(8,128)(2,1)} %param.10, f32[512,384]{1,0:T(8,128)} %fusion.4), kind=kOutput, calls=%fused_computation.20 | convolution fusion | flops 1611792384 | bytes 8519680 | tf_op jit(solution)/shard_map/dot_general | solution.py:47
  262.3 29.1 %all-gather.16.cloned.1.call-done = bf16[2048,384]{1,0:T(8,128)(2,1)} async-done(((bf16[512,384]{1,0:T(8,128)(2,1)}), bf16[2048,384]{1,0:T(8,128)(2,1)}) %all-gather.16.cloned.1.call-update) | async-done | bytes 1572880 | tf_op jit(solution)/shard_map/all_gather | solution.py:49
  291.4 3.2 bitcast_convert_fusion.1
  294.6 2.1 copy.129
  296.7 10.7 %all-to-all-start.3 = ((bf16[64,4,2,1024]{3,2,1,0:T(2,128)(2,1)}), bf16[64,4,2,1024]{3,2,1,0:T(2,128)(2,1)}, u32[]{:S(2)}, u32[]{:S(2)}) async-start(bf16[64,4,2,1024]{3,2,1,0:T(2,128)(2,1)} %bitcast.93), calls=%async_computation.3 | async-start | bytes 2097152 | tf_op jit(solution)/shard_map/all_to_all | solution.py:54
  307.5 10.4 %all-gather = f32[512,4]{0,1:T(4,128)S(1)} all-gather(f32[128,4]{0,1:T(4,128)S(1)} %pad_maximum_fusion), channel_id=2, replica_groups=mesh['row'=4,'col'=64] {'row'}, dimensions={0}, use_global_device_ids=true | all-gather | bytes 10240 | tf_op jit(solution)/shard_map/all_gather | solution.py:26
  317.9 1.1 select_reduce_fusion.1
  319.0 1.1 copy.107
  320.1 0.1 select_reduce_fusion
  320.2 0.3 copy.100
  320.5 4.5 %fusion.9 = f32[4,128,1024,1]{2,1,3,0:T(8,128)} fusion(bf16[64,4,3,1024]{3,1,2,0:T(4,128)(2,1)} %all-to-all-done.1, f32[4,128,64,3]{1,0,3,2:T(4,128)S(1)} %bitcast.97), kind=kOutput, calls=%fused_computation.14 | convolution fusion | flops 1207959552 | bytes 4063232 | tf_op jit(solution)/shard_map/rtep,erpf->rtf/dot_general | solution.py:58
  325.0 11.1 %all-to-all-done.3 = bf16[64,4,2,1024]{3,2,1,0:T(2,128)(2,1)} async-done(((bf16[64,4,2,1024]{3,2,1,0:T(2,128)(2,1)}), bf16[64,4,2,1024]{3,2,1,0:T(2,128)(2,1)}, u32[]{:S(2)}, u32[]{:S(2)}) %all-to-all-start.3) | async-done | bytes 1048608 | tf_op jit(solution)/shard_map/all_to_all | solution.py:54
  336.1 3.9 %fusion.8 = bf16[4,128,1024]{2,1,0:T(8,128)(2,1)S(1)} fusion(f32[4,128,1024,1]{2,1,3,0:T(8,128)} %fusion.9, bf16[64,4,2,1024]{3,2,1,0:T(2,128)(2,1)} %all-to-all-done.3, f32[4,128,64,2]{1,3,2,0:T(2,128)S(1)} %bitcast.98), kind=kOutput, calls=%fused_computation.12 | convolution fusion | flops 806354944 | bytes 4456448 | tf_op jit(solution)/shard_map/rtep,erpf->rtf/dot_general | solution.py:58
  340.1 17.4 %all_to_all.27 = bf16[4,128,1024]{2,1,0:T(8,128)(2,1)} all-to-all(bf16[4,128,1024]{2,1,0:T(8,128)(2,1)S(1)} %fusion.8), channel_id=1, replica_groups=mesh['row'=4,'col'=64] {'row'}, dimensions={0} | all-to-all | bytes 2097152 | tf_op jit(solution)/shard_map/all_to_all | solution.py:63
  357.5 2.3 copy.112
  359.8 2.3 copy.113
  (35 shorter events, 0.4 us)
Async XLA Ops:
  6.5 231.9 %copy-start = (bf16[1,1536,1024]{2,1,0:T(8,128)(2,1)S(1)}, bf16[1,1536,1024]{2,1,0:T(8,128)(2,1)}, u32[]{:S(2)}) copy-start(bf16[1,1536,1024]{2,1,0:T(8,128)(2,1)} %param.11) | copy-start | bytes 9437188
  6.5 140.8 %all-gather.10.cloned.1.call-start = ((), (), s32[]{:S(2)}) async-start(), calls=%async_computation.5 | async-start | bytes 7864320 | tf_op jit(solution)/shard_map/all_gather | solution.py:44
  82.6 118.1 %all-gather.14.cloned.1.call-start = ((), (), s32[]{:S(2)}) async-start(), calls=%async_computation.7 | async-start | bytes 5242880 | tf_op jit(solution)/shard_map/all_gather | solution.py:44
  122.5 116.0 %all-gather.12.cloned.1.call-start = ((), (), s32[]{:S(2)}) async-start(), calls=%async_computation.6 | async-start | bytes 2949120 | tf_op jit(solution)/shard_map/all_gather | solution.py:49
  147.3 6.6 %copy-start.3 = (bf16[256,3,4096]{2,0,1:T(8,128)(2,1)S(1)}, bf16[256,3,4096]{2,0,1:T(8,128)(2,1)}, u32[]{:S(2)}) copy-start(bf16[256,3,4096]{2,0,1:T(8,128)(2,1)} %all-gather.10.cloned.1.call-done) | copy-start | bytes 18874372
  147.3 6.6 %copy-start.5 = (bf16[1,4096,384]{2,1,0:T(8,128)(2,1)S(1)}, bf16[1,4096,384]{2,1,0:T(8,128)(2,1)}, u32[]{:S(2)}) copy-start(bf16[1,4096,384]{2,1,0:T(8,128)(2,1)} %param.10) | copy-start | bytes 9437188
  200.7 7.2 %copy-start.4 = (bf16[1,4096,384]{2,1,0:T(8,128)(2,1)S(1)}, bf16[1,4096,384]{2,1,0:T(8,128)(2,1)}, u32[]{:S(2)}) copy-start(bf16[1,4096,384]{2,1,0:T(8,128)(2,1)} %param.9) | copy-start | bytes 9437188
  206.0 1.9 copy-start.1
  245.2 51.5 %all-to-all-start.1 = ((bf16[64,4,3,1024]{3,1,2,0:T(4,128)(2,1)}), bf16[64,4,3,1024]{3,1,2,0:T(4,128)(2,1)}, u32[]{:S(2)}, u32[]{:S(2)}) async-start(bf16[64,4,3,1024]{3,1,2,0:T(4,128)(2,1)} %bitcast.90), calls=%async_computation.1 | async-start | bytes 3145728 | tf_op jit(solution)/shard_map/all_to_all | solution.py:54
  255.9 35.5 %all-gather.16.cloned.1.call-start = ((), (), s32[]{:S(2)}) async-start(), calls=%async_computation.8 | async-start | bytes 1966080 | tf_op jit(solution)/shard_map/all_gather | solution.py:49
  294.6 12.8 %copy-start.2 = (f32[128,2]{0,1:T(2,128)S(1)}, f32[128,2]{0,1:T(2,128)}, u32[]{:S(2)}) copy-start(f32[128,2]{0,1:T(2,128)} %param.8) | copy-start | bytes 3076
  296.7 39.5 %all-to-all-start.3 = ((bf16[64,4,2,1024]{3,2,1,0:T(2,128)(2,1)}), bf16[64,4,2,1024]{3,2,1,0:T(2,128)(2,1)}, u32[]{:S(2)}, u32[]{:S(2)}) async-start(bf16[64,4,2,1024]{3,2,1,0:T(2,128)(2,1)} %bitcast.93), calls=%async_computation.3 | async-start | bytes 2097152 | tf_op jit(solution)/shard_map/all_to_all | solution.py:54
Sparse Core Ops, SparseCore 0:
  82.7 64.5 all-gather.9
  149.1 51.5 all-gather.13
  202.5 35.9 all-gather.11
  262.4 28.9 all-gather.15
where the time goes:
time: 370 us; the launch traced here: 369 us
  waiting for transfers between devices  135 us (36%)
  blocking collectives  125 us (34%)
  matrix products  41.9 us (11%)
  local copies, waits for them, and re-layouts  28.4 us (8%)
  starting transfers between devices  21.7 us (6%)
  between operations  13.3 us (4%)
    all_to_all x2, blocking collectives, local(): lax.all_to_all(outgoing, 'col', split_axis=0, concat_axis=0, tiled=True)  97.6 us
    all_gather x2, waiting for transfers between devices, local(): rows = lax.all_gather(arrived, 'row', axis=0, tiled=False)  67.1 us
    all_gather x2, waiting for transfers between devices, local(): hidden_all = lax.all_gather(hidden, 'row', axis=0, tiled=False)  56.5 us
    all_to_all x2, starting transfers between devices, local(): lax.all_to_all(result, 'col', split_axis=0, concat_axis=0, tiled=True)  21.4 us
    all_to_all x1, blocking collectives, local(): lax.all_to_all(combined, 'row', split_axis=0, concat_axis=0, tiled=True)  17.4 us
    all_to_all x2, waiting for transfers between devices, local(): lax.all_to_all(result, 'col', split_axis=0, concat_axis=0, tiled=True)  11.1 us
    dot_general x2, matrix products, local(): up_part = jnp.dot(rows, w_up[0], preferred_element_type=jnp.float32)  10.7 us
    all_gather x1, blocking collectives, local(): meta = lax.all_gather(meta, 'row', axis=0, tiled=False)  10.4 us
  transfers between devices with their start and end apart: 6, of which 5 were waited for; matrix products, arithmetic and copies ran while one was open for 12% of the time, Pallas kernels for 0%

commit v1 on v0

--- a/solution.py
+++ b/solution.py
@@ -3,7 +3,7 @@
 from jax import lax
 from jax.sharding import PartitionSpec as P
 
-CHUNKS = ((0, 3), (3, 5))
+CHUNKS = ((0, 2), (2, 5))
 
 
 def local(tokens, expert_ids, gate_weights, w_gate, w_up, w_down):
@@ -23,12 +23,20 @@
     shares = gate_weights / jnp.sum(gate_weights, axis=1, keepdims=True)
 
     meta = jnp.concatenate([slot_ids.astype(jnp.float32), shares], axis=1)
-    meta = lax.all_gather(meta, "row", axis=0, tiled=False)
+    my_row = lax.axis_index("row")
+    shifted = [meta]
+    for step in range(1, groups):
+        pairs = [(i, (i + step) % groups) for i in range(groups)]
+        shifted.append(lax.ppermute(meta, "row", pairs))
+    order = jnp.stack([shifted[(-s) % groups] for s in range(groups)])
+    meta = jnp.roll(order, my_row, axis=0)
     all_slots = meta[:, :, :top_count]
     all_shares = meta[:, :, top_count:]
 
     w_down_parts = w_down[0].reshape(groups, unit_count, quarter)
     combined = jnp.zeros((groups, token_count, quarter), jnp.float32)
+    previous = None
+    stages = []
     for lo, hi in CHUNKS:
         span = hi - lo
         wanted = (
@@ -40,13 +48,22 @@
         ).astype(jnp.bfloat16)
         outgoing = jnp.dot(chooser, tokens, preferred_element_type=jnp.float32).astype(jnp.bfloat16)
         outgoing = outgoing.reshape(columns, span, width)
+        if previous is not None:
+            outgoing, _ = lax.optimization_barrier((outgoing, previous))
         arrived = lax.all_to_all(outgoing, "col", split_axis=0, concat_axis=0, tiled=True)
+        previous = arrived
         rows = lax.all_gather(arrived, "row", axis=0, tiled=False)
         rows = rows.transpose(2, 0, 1, 3).reshape(span * groups * columns, width)
         gate_part = jnp.dot(rows, w_gate[0], preferred_element_type=jnp.float32)
         up_part = jnp.dot(rows, w_up[0], preferred_element_type=jnp.float32)
         hidden = (jax.nn.silu(gate_part) * up_part).astype(jnp.bfloat16)
+        stages.append((span, wanted, hidden))
+
+    combined = jnp.zeros((groups, token_count, quarter), jnp.float32)
+    for index, (span, wanted, hidden) in enumerate(stages):
         hidden_all = lax.all_gather(hidden, "row", axis=0, tiled=False)
+        if index + 1 < len(stages):
+            hidden_all, _ = lax.optimization_barrier((hidden_all, stages[index + 1][2]))
         result = jnp.einsum(
             "jnu,juf->nf", hidden_all, w_down_parts, preferred_element_type=jnp.float32
         ).astype(jnp.bfloat16)
@@ -60,8 +77,8 @@
             precision=lax.Precision.HIGHEST, preferred_element_type=jnp.float32,
         )
     combined = combined.astype(jnp.bfloat16)
-    home = lax.all_to_all(combined, "row", split_axis=0, concat_axis=0, tiled=True)
-    return home.transpose(1, 0, 2).reshape(token_count, width)
+    home = lax.all_to_all(combined, "row", split_axis=0, concat_axis=2, tiled=True)
+    return home.reshape(token_count, width)
 
 
 def solution(mesh):

time: 370 us -> 347 us (0.938)
  blocking collectives: 125 us -> 115 us
  waiting for transfers between devices: 135 us -> 127 us
  matrix products: 41.9 us -> 37.9 us
    all_to_all x2, waiting for transfers between devices: 11.1 us -> 26.8 us  [local(): lax.all_to_all(result, 'col', split_axis=0, concat_axis=0, tiled=True)]
    all_gather x2, waiting for transfers between devices: 56.5 us -> 42.1 us  [local(): hidden_all = lax.all_gather(hidden, 'row', axis=0, tiled=False)]
    all_gather x2, waiting for transfers between devices: 67.1 us -> 53.5 us  [local(): rows = lax.all_gather(arrived, 'row', axis=0, tiled=False)]
    all_gather x1 -> x0, blocking collectives: 10.4 us -> none  [local(): meta = lax.all_gather(meta, 'row', axis=0, tiled=False)]
    ppermute x0 -> x3, waiting for transfers between devices: none -> 4.2 us  [local(): shifted.append(lax.ppermute(meta, 'row', pairs))]
  transfers between devices with their start and end apart: 6 -> 9, of which waited for: 5 -> 8; matrix products, arithmetic and copies ran while one was open for 12% -> 14% of each run, Pallas kernels for 0% -> 0%
where the time goes in v1:
time: 347 us
  waiting for transfers between devices  127 us (37%)
  blocking collectives  115 us (33%)
  matrix products  37.9 us (11%)
  local copies, waits for them, and re-layouts  26.2 us (8%)
  starting transfers between devices  24.7 us (7%)
  between operations  13.4 us (4%)
    all_to_all x2, blocking collectives, local(): lax.all_to_all(outgoing, 'col', split_axis=0, concat_axis=0, tiled=True)  97.8 us
    all_gather x2, waiting for transfers between devices, local(): rows = lax.all_gather(arrived, 'row', axis=0, tiled=False)  53.5 us
    all_gather x2, waiting for transfers between devices, local(): hidden_all = lax.all_gather(hidden, 'row', axis=0, tiled=False)  42.1 us
    all_to_all x2, waiting for transfers between devices, local(): lax.all_to_all(result, 'col', split_axis=0, concat_axis=0, tiled=True)  26.8 us
    all_to_all x2, starting transfers between devices, local(): lax.all_to_all(result, 'col', split_axis=0, concat_axis=0, tiled=True)  20.9 us
    all_to_all x1, blocking collectives, local(): lax.all_to_all(combined, 'row', split_axis=0, concat_axis=2, tiled=True)  17.6 us
    dot_general x2, matrix products, local(): gate_part = jnp.dot(rows, w_gate[0], preferred_element_type=jnp.float32)  8.9 us
    dot_general x2, matrix products, local(): jnp.einsum('rtep,erpf->rtf', weights, back.astype(jnp.float32), precision...  8.57 us
  transfers between devices with their start and end apart: 9, of which 8 were waited for; matrix products, arithmetic and copies ran while one was open for 14% of the time, Pallas kernels for 0%

profile of v1, /device:TPU:4, one launch (start us, length us, event | category | flops | bytes accessed | tf_op | source)
XLA Modules:
  0.0 346.6 jit_solution(861350598635539021)
XLA Ops:
  6.5 0.9 copy.118
  7.5 0.1 eq.84
  7.6 0.1 eq.80
  7.8 0.6 reduce-window.6
  8.4 0.2 slice_reduce_fusion
  8.7 0.1 reduce_sum.39
  8.9 0.7 fusion.30
  9.7 0.1 add.108
  10.0 2.6 convolution_convert_fusion.1
  12.6 2.5 reshape.122
  15.1 40.9 %all_to_all.35 = bf16[64,2,4096]{2,1,0:T(2,128)(2,1)} all-to-all(bf16[64,2,4096]{2,1,0:T(2,128)(2,1)} %reshape.122), channel_id=1, replica_groups=mesh['row'=4,'col'=64] {'col'}, dimensions={0} | all-to-all | bytes 2097152 | tf_op jit(solution)/shard_map/all_to_all | solution.py:53
  56.2 0.1 add.114
  56.4 2.9 convolution_convert_fusion
  59.4 4.1 %reshape.124 = bf16[64,3,4096]{2,1,0:T(4,128)(2,1)} reshape(bf16[192,4096]{1,0:T(8,128)(2,1)} %convolution_convert_fusion) | data formatting | bytes 3145728 | tf_op jit(solution)/shard_map/reshape | solution.py:50
  63.5 56.9 %all_to_all.36 = bf16[64,3,4096]{2,1,0:T(4,128)(2,1)S(1)} all-to-all(bf16[64,3,4096]{2,1,0:T(4,128)(2,1)} %reshape.124), channel_id=1, replica_groups=mesh['row'=4,'col'=64] {'col'}, dimensions={0} | all-to-all | bytes 3145728 | tf_op jit(solution)/shard_map/all_to_all | solution.py:53
  120.4 2.3 copy.134
  122.7 0.2 all-gather.11.cloned.1.call-start
  123.0 5.3 %copy.133 = bf16[256,2,4096]{2,0,1:T(8,128)(2,1)S(1)} copy(bf16[256,2,4096]{2,1,0:T(2,128)(2,1)} %all-gather.9.cloned.1.call-done) | data formatting | bytes 8388608 | tf_op jit(solution)/shard_map/all_gather | solution.py:55
  128.2 2.3 fusion.6
  130.6 3.1 fusion.19
  133.7 0.3 all-gather.15.cloned.1.call-start
  134.0 53.5 %all-gather.13.cloned.1.call-done = bf16[256,3,4096]{2,0,1:T(8,128)(2,1)} async-done(((bf16[64,3,4096]{2,0,1:T(8,128)(2,1)}), bf16[256,3,4096]{2,0,1:T(8,128)(2,1)}) %all-gather.13.cloned.1.call-update) | async-done | bytes 6291472 | tf_op jit(solution)/shard_map/all_gather | solution.py:55
  187.4 6.6 %fusion.4 = f32[768,384]{1,0:T(8,128)S(1)} fusion(bf16[768,4096]{1,0:T(8,128)(2,1)} %bitcast.124, bf16[1,4096,384]{2,1,0:T(8,128)(2,1)} %param.9), kind=kOutput, calls=%fused_computation.7 | convolution fusion | flops 2415919104 | bytes 10616832 | tf_op jit(solution)/shard_map/dot_general | solution.py:57
  194.0 4.3 %fusion.13 = bf16[768,384]{1,0:T(8,128)(2,1)} fusion(bf16[768,4096]{1,0:T(8,128)(2,1)S(1)} %bitcast.125, bf16[1,4096,384]{2,1,0:T(8,128)(2,1)S(1)} %copy-done.5, f32[768,384]{1,0:T(8,128)S(1)} %fusion.4), kind=kOutput, calls=%fused_computation.17 | convolution fusion | flops 2417688576 | bytes 11206656 | tf_op jit(solution)/shard_map/dot_general | solution.py:58
  198.4 20.7 %all-gather.11.cloned.1.call-done = bf16[2048,384]{1,0:T(8,128)(2,1)} async-done(((bf16[512,384]{1,0:T(8,128)(2,1)}), bf16[2048,384]{1,0:T(8,128)(2,1)}) %all-gather.11.cloned.1.call-update) | async-done | bytes 1572880 | tf_op jit(solution)/shard_map/all_gather | solution.py:64
  219.1 3.2 bitcast_convert_fusion.1
  222.3 2.1 copy.161
  224.3 10.7 %all-to-all-start.2 = ((bf16[64,4,2,1024]{3,2,1,0:T(2,128)(2,1)}), bf16[64,4,2,1024]{3,2,1,0:T(2,128)(2,1)}, u32[]{:S(2)}, u32[]{:S(2)}) async-start(bf16[64,4,2,1024]{3,2,1,0:T(2,128)(2,1)} %bitcast.109), calls=%async_computation.2 | async-start | bytes 2097152 | tf_op jit(solution)/shard_map/all_to_all | solution.py:71
  235.1 21.4 %all-gather.15.cloned.1.call-done = bf16[3072,384]{1,0:T(8,128)(2,1)} async-done(((bf16[768,384]{1,0:T(8,128)(2,1)}), bf16[3072,384]{1,0:T(8,128)(2,1)}) %all-gather.15.cloned.1.call-update) | async-done | bytes 2359312 | tf_op jit(solution)/shard_map/all_gather | solution.py:64
  256.4 4.3 %bitcast_convert_fusion = bf16[768,1024]{1,0:T(8,128)(2,1)S(1)} fusion(bf16[4,768,384]{2,1,0:T(8,128)(2,1)} %bitcast.126, bf16[4,384,1024]{2,1,0:T(8,128)(2,1)S(1)} %bitcast.105), kind=kOutput, calls=%fused_computation.2 | convolution fusion | flops 2416705536 | bytes 7077888 | tf_op jit(solution)/shard_map/jnu,juf->nf/dot_general | solution.py:67
  260.7 2.4 copy.160
  263.1 0.7 all-to-all-done.2
  263.8 10.1 %all-to-all-start.3 = ((bf16[64,4,3,1024]{3,1,2,0:T(4,128)(2,1)}), bf16[64,4,3,1024]{3,1,2,0:T(4,128)(2,1)}, u32[]{:S(2)}, u32[]{:S(2)}) async-start(bf16[64,4,3,1024]{3,1,2,0:T(4,128)(2,1)} %bitcast.106), calls=%async_computation.3 | async-start | bytes 3145728 | tf_op jit(solution)/shard_map/all_to_all | solution.py:71
  274.0 0.9 collective-permute-start
  274.9 1.8 collective-permute-start.1
  276.7 0.6 collective-permute-start.2
  277.3 0.4 collective-permute-done
  277.7 2.3 collective-permute-done.1
  280.0 1.5 collective-permute-done.2
  281.6 0.3 select_reduce_fusion.1
  281.9 0.8 copy.132
  282.9 0.3 copy.140
  283.2 4.7 %fusion.22 = f32[4,128,1024,1]{2,1,3,0:T(8,128)} fusion(bf16[64,4,2,1024]{3,2,1,0:T(2,128)(2,1)} %all-to-all-done.2, f32[4,128,64,2]{1,3,2,0:T(2,128)} %bitcast.115), kind=kOutput, calls=%fused_computation.20 | convolution fusion | flops 805306368 | bytes 3407872 | tf_op jit(solution)/shard_map/rtep,erpf->rtf/dot_general | solution.py:75
  287.8 26.1 %all-to-all-done.3 = bf16[64,4,3,1024]{3,1,2,0:T(4,128)(2,1)} async-done(((bf16[64,4,3,1024]{3,1,2,0:T(4,128)(2,1)}), bf16[64,4,3,1024]{3,1,2,0:T(4,128)(2,1)}, u32[]{:S(2)}, u32[]{:S(2)}) %all-to-all-start.3) | async-done | bytes 1572896 | tf_op jit(solution)/shard_map/all_to_all | solution.py:71
  313.9 3.9 %fusion.8 = bf16[4,128,1024]{2,1,0:T(8,128)(2,1)S(1)} fusion(f32[4,128,1024,1]{2,1,3,0:T(8,128)} %fusion.22, bf16[64,4,3,1024]{3,1,2,0:T(4,128)(2,1)} %all-to-all-done.3, f32[4,128,64,3]{1,0,3,2:T(4,128)S(1)} %bitcast.113), kind=kOutput, calls=%fused_computation.12 | convolution fusion | flops 1209008128 | bytes 5111808 | tf_op jit(solution)/shard_map/rtep,erpf->rtf/dot_general | solution.py:75
  317.8 17.6 %all_to_all.37 = bf16[4,128,1024]{2,1,0:T(8,128)(2,1)} all-to-all(bf16[4,128,1024]{2,1,0:T(8,128)(2,1)S(1)} %fusion.8), channel_id=1, replica_groups=mesh['row'=4,'col'=64] {'row'}, dimensions={0} | all-to-all | bytes 2097152 | tf_op jit(solution)/shard_map/all_to_all | solution.py:80
  335.5 2.3 copy.144
  337.8 2.3 copy.145
  (40 shorter events, 0.9 us)
Async XLA Ops:
  6.5 212.5 %copy-start = (bf16[1,1536,1024]{2,1,0:T(8,128)(2,1)S(1)}, bf16[1,1536,1024]{2,1,0:T(8,128)(2,1)}, u32[]{:S(2)}) copy-start(bf16[1,1536,1024]{2,1,0:T(8,128)(2,1)} %param.11) | copy-start | bytes 9437188
  6.5 116.4 %all-gather.9.cloned.1.call-start = ((), (), s32[]{:S(2)}) async-start(), calls=%async_computation.5 | async-start | bytes 5242880 | tf_op jit(solution)/shard_map/all_gather | solution.py:55
  56.1 131.4 %all-gather.13.cloned.1.call-start = ((), (), s32[]{:S(2)}) async-start(), calls=%async_computation.7 | async-start | bytes 7864320 | tf_op jit(solution)/shard_map/all_gather | solution.py:55
  122.7 96.4 %all-gather.11.cloned.1.call-start = ((), (), s32[]{:S(2)}) async-start(), calls=%async_computation.6 | async-start | bytes 1966080 | tf_op jit(solution)/shard_map/all_gather | solution.py:64
  122.9 5.3 %copy-start.3 = (bf16[1,4096,384]{2,1,0:T(8,128)(2,1)S(1)}, bf16[1,4096,384]{2,1,0:T(8,128)(2,1)}, u32[]{:S(2)}) copy-start(bf16[1,4096,384]{2,1,0:T(8,128)(2,1)} %param.9) | copy-start | bytes 9437188
  128.2 2.3 copy-start.4
  133.7 122.7 %all-gather.15.cloned.1.call-start = ((), (), s32[]{:S(2)}) async-start(), calls=%async_computation.8 | async-start | bytes 2949120 | tf_op jit(solution)/shard_map/all_gather | solution.py:64
  187.4 6.6 %copy-start.2 = (bf16[256,3,4096]{2,0,1:T(8,128)(2,1)S(1)}, bf16[256,3,4096]{2,0,1:T(8,128)(2,1)}, u32[]{:S(2)}) copy-start(bf16[256,3,4096]{2,0,1:T(8,128)(2,1)} %all-gather.13.cloned.1.call-done) | copy-start | bytes 18874372
  187.4 6.6 %copy-start.5 = (bf16[1,4096,384]{2,1,0:T(8,128)(2,1)S(1)}, bf16[1,4096,384]{2,1,0:T(8,128)(2,1)}, u32[]{:S(2)}) copy-start(bf16[1,4096,384]{2,1,0:T(8,128)(2,1)} %param.10) | copy-start | bytes 9437188
  224.3 39.5 %all-to-all-start.2 = ((bf16[64,4,2,1024]{3,2,1,0:T(2,128)(2,1)}), bf16[64,4,2,1024]{3,2,1,0:T(2,128)(2,1)}, u32[]{:S(2)}, u32[]{:S(2)}) async-start(bf16[64,4,2,1024]{3,2,1,0:T(2,128)(2,1)} %bitcast.109), calls=%async_computation.2 | async-start | bytes 2097152 | tf_op jit(solution)/shard_map/all_to_all | solution.py:71
  263.1 10.9 %copy-start.1 = (f32[128,2]{0,1:T(2,128)S(1)}, f32[128,2]{0,1:T(2,128)}, u32[]{:S(2)}) copy-start(f32[128,2]{0,1:T(2,128)} %param.8) | copy-start | bytes 3076
  263.8 50.1 %all-to-all-start.3 = ((bf16[64,4,3,1024]{3,1,2,0:T(4,128)(2,1)}), bf16[64,4,3,1024]{3,1,2,0:T(4,128)(2,1)}, u32[]{:S(2)}, u32[]{:S(2)}) async-start(bf16[64,4,3,1024]{3,1,2,0:T(4,128)(2,1)} %bitcast.106), calls=%async_computation.3 | async-start | bytes 3145728 | tf_op jit(solution)/shard_map/all_to_all | solution.py:71
  274.0 3.7 %collective-permute-start = (f32[128,4]{0,1:T(4,128)S(1)}, f32[128,4]{0,1:T(4,128)S(1)}, u32[]{:S(2)}, u32[]{:S(2)}) collective-permute-start(f32[128,4]{0,1:T(4,128)S(1)} %pad_maximum_fusion), channel_id=1, source_target_pairs={{0,192},{64,0},{128,64},{192,128},{1,193},{65,1},{129,65},{193,129... | collective-permute-start | bytes 6152 | tf_op jit(solution)/shard_map/ppermute | solution.py:30
  274.9 5.1 %collective-permute-start.1 = (f32[128,4]{0,1:T(4,128)S(1)}, f32[128,4]{0,1:T(4,128)S(1)}, u32[]{:S(2)}, u32[]{:S(2)}) collective-permute-start(f32[128,4]{0,1:T(4,128)S(1)} %pad_maximum_fusion), channel_id=1, source_target_pairs={{0,128},{64,192},{128,0},{192,64},{1,129},{65,193},{129,1},{193,65... | collective-permute-start | bytes 6152 | tf_op jit(solution)/shard_map/ppermute | solution.py:30
  276.7 4.8 %collective-permute-start.2 = (f32[128,4]{0,1:T(4,128)S(1)}, f32[128,4]{0,1:T(4,128)S(1)}, u32[]{:S(2)}, u32[]{:S(2)}) collective-permute-start(f32[128,4]{0,1:T(4,128)S(1)} %pad_maximum_fusion), channel_id=1, source_target_pairs={{0,64},{64,128},{128,192},{192,0},{1,65},{65,129},{129,193},{193,1... | collective-permute-start | bytes 6152 | tf_op jit(solution)/shard_map/ppermute | solution.py:30
Sparse Core Ops, SparseCore 0:
  56.2 47.4 all-gather.8
  122.8 64.5 all-gather.12
  189.2 29.7 all-gather.10
  220.7 35.6 all-gather.14

commit v2 on v1

--- a/solution.py
+++ b/solution.py
@@ -47,11 +47,12 @@
             wanted[:, None, None] == slot_ids[None, :, :], axis=2
         ).astype(jnp.bfloat16)
         outgoing = jnp.dot(chooser, tokens, preferred_element_type=jnp.float32).astype(jnp.bfloat16)
-        outgoing = outgoing.reshape(columns, span, width)
+        outgoing = outgoing.reshape(columns, span * width // 128, 128)
         if previous is not None:
             outgoing, _ = lax.optimization_barrier((outgoing, previous))
         arrived = lax.all_to_all(outgoing, "col", split_axis=0, concat_axis=0, tiled=True)
         previous = arrived
+        arrived = arrived.reshape(columns, span, width)
         rows = lax.all_gather(arrived, "row", axis=0, tiled=False)
         rows = rows.transpose(2, 0, 1, 3).reshape(span * groups * columns, width)
         gate_part = jnp.dot(rows, w_gate[0], preferred_element_type=jnp.float32)
@@ -68,7 +69,9 @@
             "jnu,juf->nf", hidden_all, w_down_parts, preferred_element_type=jnp.float32
         ).astype(jnp.bfloat16)
         result = result.reshape(span, groups, columns, quarter).transpose(2, 1, 0, 3)
+        result = result.reshape(columns, groups * span * quarter // 128, 128)
         back = lax.all_to_all(result, "col", split_axis=0, concat_axis=0, tiled=True)
+        back = back.reshape(experts, groups, span, quarter)
         match = (all_slots[:, :, :, None] == wanted.astype(jnp.float32)[None, None, None, :])
         weights = jnp.sum(jnp.where(match, all_shares[:, :, :, None], 0.0), axis=2)
         weights = weights.reshape(groups, token_count, experts, span)

time: 347 us -> 359 us (1.035)
  local copies, waits for them, and re-layouts: 26.2 us -> 54.1 us
  blocking collectives: 115 us -> 104 us
  waiting for transfers between devices: 127 us -> 123 us
    reshape x2 -> x6, local copies, waits for them, and re-layouts: 6.61 us -> 21 us  [the longest x2 7.65 us: local(): result = result.reshape(columns, groups * span * quarter // 128, 128)]
    another operation x1 -> x5, local copies, waits for them, and re-layouts: 0.01 us -> 13.9 us  [the longest x4 13.9 us: local(): rows = lax.all_gather(arrived, 'row', axis=0, tiled=False)]
    all_to_all x2, blocking collectives: 97.8 us -> 86.7 us  [local(): lax.all_to_all(outgoing, 'col', split_axis=0, concat_axis=0, tiled=True)]
  transfers between devices with their start and end apart: 9 -> 9, of which waited for: 8 -> 7; matrix products, arithmetic and copies ran while one was open for 14% -> 18% of each run, Pallas kernels for 0% -> 0%
where the time goes in v2:
time: 359 us; the launch traced here: 358 us
  waiting for transfers between devices  123 us (34%)
  blocking collectives  104 us (29%)
  local copies, waits for them, and re-layouts  54.1 us (15%)
  matrix products  35.7 us (10%)
  starting transfers between devices  25.2 us (7%)
  between operations  13.4 us (4%)
    all_to_all x2, blocking collectives, local(): lax.all_to_all(outgoing, 'col', split_axis=0, concat_axis=0, tiled=True)  86.7 us
    all_gather x2, waiting for transfers between devices, local(): rows = lax.all_gather(arrived, 'row', axis=0, tiled=False)  55.9 us
    all_gather x2, waiting for transfers between devices, local(): hidden_all = lax.all_gather(hidden, 'row', axis=0, tiled=False)  39 us
    all_to_all x2, waiting for transfers between devices, local(): lax.all_to_all(result, 'col', split_axis=0, concat_axis=0, tiled=True)  24 us
    all_to_all x2, starting transfers between devices, local(): lax.all_to_all(result, 'col', split_axis=0, concat_axis=0, tiled=True)  21.6 us
    all_to_all x1, blocking collectives, local(): lax.all_to_all(combined, 'row', split_axis=0, concat_axis=2, tiled=True)  17.7 us
    another operation x4, local copies, waits for them, and re-layouts, local(): rows = lax.all_gather(arrived, 'row', axis=0, tiled=False)  13.9 us
    dot_general x2, matrix products, local(): jnp.einsum('rtep,erpf->rtf', weights, back.astype(jnp.float32), precision...  9.51 us
  transfers between devices with their start and end apart: 9, of which 7 were waited for; matrix products, arithmetic and copies ran while one was open for 18% of the time, Pallas kernels for 0%

profile of v2, /device:TPU:4, one launch (start us, length us, event | category | flops | bytes accessed | tf_op | source)
XLA Modules:
  0.0 358.1 jit_solution(3848216792533036995)
XLA Ops:
  6.5 0.9 copy.110
  7.8 0.6 reduce-window.6
  8.9 0.7 fusion.30
  10.0 2.6 convolution_convert_fusion.1
  12.6 2.3 reshape.134
  14.9 40.9 %all_to_all.35 = bf16[64,64,128]{2,1,0:T(8,128)(2,1)} all-to-all(bf16[64,64,128]{2,1,0:T(8,128)(2,1)} %reshape.134), channel_id=1, replica_groups=mesh['row'=4,'col'=64] {'col'}, dimensions={0} | all-to-all | bytes 2097152 | tf_op jit(solution)/shard_map/all_to_all | solution.py:53
  55.8 2.1 all_gather_reshape.6
  58.0 2.8 copy.125
  61.2 2.9 convolution_convert_fusion
  64.1 3.8 %reshape.136 = bf16[64,96,128]{2,1,0:T(8,128)(2,1)} reshape(bf16[192,4096]{1,0:T(8,128)(2,1)} %convolution_convert_fusion) | data formatting | bytes 3145728 | tf_op jit(solution)/shard_map/reshape | solution.py:50
  67.9 45.8 %all_to_all.36 = bf16[64,96,128]{2,1,0:T(8,128)(2,1)} all-to-all(bf16[64,96,128]{2,1,0:T(8,128)(2,1)} %reshape.136), channel_id=1, replica_groups=mesh['row'=4,'col'=64] {'col'}, dimensions={0} | all-to-all | bytes 3145728 | tf_op jit(solution)/shard_map/all_to_all | solution.py:53
  113.7 5.1 %all_gather_reshape.7 = bf16[1,64,3,4096]{3,2,1,0:T(4,128)(2,1)} reshape(bf16[64,96,128]{2,1,0:T(8,128)(2,1)} %all_to_all.36) | data formatting | bytes 3145728 | tf_op jit(solution)/shard_map/all_gather;reshape | solution.py:56
  118.8 3.9 %copy.127 = bf16[1,64,3,4096]{3,1,2,0:T(8,128)(2,1)} copy(bf16[1,64,3,4096]{3,2,1,0:T(4,128)(2,1)} %all_gather_reshape.7) | data formatting | bytes 3145728 | tf_op jit(solution)/shard_map/all_gather;reshape | solution.py:56
  122.8 2.6 copy.126
  125.4 0.5 copy-done.2
  125.9 2.3 fusion.6
  128.2 3.1 fusion.19
  131.6 55.9 %all-gather.9.cloned.1.call-done = bf16[4,64,3,4096]{3,1,2,0:T(8,128)(2,1)} async-done(((bf16[1,64,3,4096]{3,1,2,0:T(8,128)(2,1)}), bf16[4,64,3,4096]{3,1,2,0:T(8,128)(2,1)}) %all-gather.9.cloned.1.call-update) | async-done | bytes 6291472 | tf_op jit(solution)/shard_map/all_gather | solution.py:56
  187.5 3.4 copy.128
  190.8 0.3 copy-done.3
  191.2 3.4 fusion.4
  194.6 4.3 %fusion.13 = bf16[768,384]{1,0:T(8,128)(2,1)} fusion(bf16[768,4096]{1,0:T(8,128)(2,1)S(1)} %bitcast.104, bf16[1,4096,384]{2,1,0:T(8,128)(2,1)S(1)} %copy-done.5, f32[768,384]{1,0:T(8,128)S(1)} %fusion.4), kind=kOutput, calls=%fused_computation.17 | convolution fusion | flops 2417688576 | bytes 11206656 | tf_op jit(solution)/shard_map/dot_general | solution.py:59
  198.9 20.2 %all-gather.11.cloned.1.call-done = bf16[2048,384]{1,0:T(8,128)(2,1)} async-done(((bf16[512,384]{1,0:T(8,128)(2,1)}), bf16[2048,384]{1,0:T(8,128)(2,1)}) %all-gather.11.cloned.1.call-update) | async-done | bytes 1572880 | tf_op jit(solution)/shard_map/all_gather | solution.py:65
  219.1 3.2 bitcast_convert_fusion.1
  222.3 2.1 copy.155
  224.3 2.5 reshape.139
  226.8 10.7 %all-to-all-start.2 = ((bf16[64,64,128]{2,1,0:T(8,128)(2,1)}), bf16[64,64,128]{2,1,0:T(8,128)(2,1)}, u32[]{:S(2)}, u32[]{:S(2)}) async-start(bf16[64,64,128]{2,1,0:T(8,128)(2,1)} %reshape.139), calls=%async_computation.2 | async-start | bytes 2097152 | tf_op jit(solution)/shard_map/all_to_all | solution.py:73
  237.6 18.8 %all-gather.13.cloned.1.call-done = bf16[3072,384]{1,0:T(8,128)(2,1)} async-done(((bf16[768,384]{1,0:T(8,128)(2,1)}), bf16[3072,384]{1,0:T(8,128)(2,1)}) %all-gather.13.cloned.1.call-update) | async-done | bytes 2359312 | tf_op jit(solution)/shard_map/all_gather | solution.py:65
  256.4 4.3 %bitcast_convert_fusion = bf16[768,1024]{1,0:T(8,128)(2,1)S(1)} fusion(bf16[4,768,384]{2,1,0:T(8,128)(2,1)} %bitcast.122, bf16[4,384,1024]{2,1,0:T(8,128)(2,1)S(1)} %bitcast.101), kind=kOutput, calls=%fused_computation.2 | convolution fusion | flops 2416705536 | bytes 7077888 | tf_op jit(solution)/shard_map/jnu,juf->nf/dot_general | solution.py:68
  260.7 2.7 copy.154
  263.4 5.1 %reshape.143 = bf16[64,96,128]{2,1,0:T(8,128)(2,1)} reshape(bf16[64,4,3,1024]{3,2,1,0:T(4,128)(2,1)} %bitcast.102) | data formatting | bytes 3145728 | tf_op jit(solution)/shard_map/reshape | solution.py:72
  268.5 10.8 %all-to-all-start.3 = ((bf16[64,96,128]{2,1,0:T(8,128)(2,1)}), bf16[64,96,128]{2,1,0:T(8,128)(2,1)}, u32[]{:S(2)}, u32[]{:S(2)}) async-start(bf16[64,96,128]{2,1,0:T(8,128)(2,1)} %reshape.143), calls=%async_computation.3 | async-start | bytes 3145728 | tf_op jit(solution)/shard_map/all_to_all | solution.py:73
  279.4 0.9 collective-permute-start
  280.4 1.8 collective-permute-start.1
  282.1 0.6 collective-permute-start.2
  282.7 0.4 collective-permute-done
  283.1 2.3 collective-permute-done.1
  285.4 1.5 collective-permute-done.2
  287.0 0.3 select_reduce_fusion.1
  287.4 0.8 copy.124
  288.6 2.1 reshape.140
  290.7 4.6 %fusion.22 = f32[4,128,1024,1]{2,1,3,0:T(8,128)} fusion(bf16[64,4,2,1024]{3,2,1,0:T(2,128)(2,1)} %reshape.140, f32[4,128,64,2]{1,3,2,0:T(2,128)} %bitcast.113), kind=kOutput, calls=%fused_computation.20 | convolution fusion | flops 805306368 | bytes 3407872 | tf_op jit(solution)/shard_map/rtep,erpf->rtf/dot_general | solution.py:78
  295.4 24.0 %all-to-all-done.3 = bf16[64,96,128]{2,1,0:T(8,128)(2,1)} async-done(((bf16[64,96,128]{2,1,0:T(8,128)(2,1)}), bf16[64,96,128]{2,1,0:T(8,128)(2,1)}, u32[]{:S(2)}, u32[]{:S(2)}) %all-to-all-start.3) | async-done | bytes 1572896 | tf_op jit(solution)/shard_map/all_to_all | solution.py:73
  319.4 5.1 %reshape.144 = bf16[64,4,3,1024]{3,2,1,0:T(4,128)(2,1)} reshape(bf16[64,96,128]{2,1,0:T(8,128)(2,1)} %all-to-all-done.3) | data formatting | bytes 3145728 | tf_op jit(solution)/shard_map/reshape | solution.py:74
  324.5 4.9 %fusion.8 = bf16[4,128,1024]{2,1,0:T(8,128)(2,1)S(1)} fusion(f32[4,128,1024,1]{2,1,3,0:T(8,128)} %fusion.22, bf16[64,4,3,1024]{3,2,1,0:T(4,128)(2,1)} %reshape.144, f32[4,128,64,3]{1,0,3,2:T(4,128)S(1)} %bitcast.111), kind=kOutput, calls=%fused_computation.12 | convolution fusion | flops 1209008128 | bytes 5111808 | tf_op jit(solution)/shard_map/rtep,erpf->rtf/dot_general | solution.py:78
  329.4 17.7 %all_to_all.37 = bf16[4,128,1024]{2,1,0:T(8,128)(2,1)} all-to-all(bf16[4,128,1024]{2,1,0:T(8,128)(2,1)S(1)} %fusion.8), channel_id=1, replica_groups=mesh['row'=4,'col'=64] {'row'}, dimensions={0} | all-to-all | bytes 2097152 | tf_op jit(solution)/shard_map/all_to_all | solution.py:83
  347.0 2.3 copy.138
  349.3 2.3 copy.139
  (48 shorter events, 2.3 us)
Async XLA Ops:
  6.5 212.5 %copy-start = (bf16[1,1536,1024]{2,1,0:T(8,128)(2,1)S(1)}, bf16[1,1536,1024]{2,1,0:T(8,128)(2,1)}, u32[]{:S(2)}) copy-start(bf16[1,1536,1024]{2,1,0:T(8,128)(2,1)} %param.11) | copy-start | bytes 9437188
  6.5 116.2 %all-gather.7.cloned.1.call-start = ((), (), s32[]{:S(2)}) async-start(), calls=%async_computation.5 | async-start | bytes 5242880 | tf_op jit(solution)/shard_map/all_gather | solution.py:56
  60.8 126.7 %all-gather.9.cloned.1.call-start = ((), (), s32[]{:S(2)}) async-start(), calls=%async_computation.6 | async-start | bytes 7864320 | tf_op jit(solution)/shard_map/all_gather | solution.py:56
  122.7 96.4 %all-gather.11.cloned.1.call-start = ((), (), s32[]{:S(2)}) async-start(), calls=%async_computation.7 | async-start | bytes 1966080 | tf_op jit(solution)/shard_map/all_gather | solution.py:65
  122.8 3.2 copy-start.2
  125.9 2.3 copy-start.4
  131.4 125.1 %all-gather.13.cloned.1.call-start = ((), (), s32[]{:S(2)}) async-start(), calls=%async_computation.8 | async-start | bytes 2949120 | tf_op jit(solution)/shard_map/all_gather | solution.py:65
  187.5 3.7 %copy-start.3 = (bf16[1,4096,384]{2,1,0:T(8,128)(2,1)S(1)}, bf16[1,4096,384]{2,1,0:T(8,128)(2,1)}, u32[]{:S(2)}) copy-start(bf16[1,4096,384]{2,1,0:T(8,128)(2,1)} %param.9) | copy-start | bytes 9437188
  191.2 3.4 copy-start.5
  226.8 41.7 %all-to-all-start.2 = ((bf16[64,64,128]{2,1,0:T(8,128)(2,1)}), bf16[64,64,128]{2,1,0:T(8,128)(2,1)}, u32[]{:S(2)}, u32[]{:S(2)}) async-start(bf16[64,64,128]{2,1,0:T(8,128)(2,1)} %reshape.139), calls=%async_computation.2 | async-start | bytes 2097152 | tf_op jit(solution)/shard_map/all_to_all | solution.py:73
  268.5 10.8 %copy-start.1 = (f32[128,2]{0,1:T(2,128)S(1)}, f32[128,2]{0,1:T(2,128)}, u32[]{:S(2)}) copy-start(f32[128,2]{0,1:T(2,128)} %param.8) | copy-start | bytes 3076
  268.5 50.8 %all-to-all-start.3 = ((bf16[64,96,128]{2,1,0:T(8,128)(2,1)}), bf16[64,96,128]{2,1,0:T(8,128)(2,1)}, u32[]{:S(2)}, u32[]{:S(2)}) async-start(bf16[64,96,128]{2,1,0:T(8,128)(2,1)} %reshape.143), calls=%async_computation.3 | async-start | bytes 3145728 | tf_op jit(solution)/shard_map/all_to_all | solution.py:73
  279.4 3.7 %collective-permute-start = (f32[128,4]{0,1:T(4,128)S(1)}, f32[128,4]{0,1:T(4,128)S(1)}, u32[]{:S(2)}, u32[]{:S(2)}) collective-permute-start(f32[128,4]{0,1:T(4,128)S(1)} %pad_maximum_fusion), channel_id=1, source_target_pairs={{0,192},{64,0},{128,64},{192,128},{1,193},{65,1},{129,65},{193,129... | collective-permute-start | bytes 6152 | tf_op jit(solution)/shard_map/ppermute | solution.py:30
  280.4 5.1 %collective-permute-start.1 = (f32[128,4]{0,1:T(4,128)S(1)}, f32[128,4]{0,1:T(4,128)S(1)}, u32[]{:S(2)}, u32[]{:S(2)}) collective-permute-start(f32[128,4]{0,1:T(4,128)S(1)} %pad_maximum_fusion), channel_id=1, source_target_pairs={{0,128},{64,192},{128,0},{192,64},{1,129},{65,193},{129,1},{193,65... | collective-permute-start | bytes 6152 | tf_op jit(solution)/shard_map/ppermute | solution.py:30
  282.1 4.8 %collective-permute-start.2 = (f32[128,4]{0,1:T(4,128)S(1)}, f32[128,4]{0,1:T(4,128)S(1)}, u32[]{:S(2)}, u32[]{:S(2)}) collective-permute-start(f32[128,4]{0,1:T(4,128)S(1)} %pad_maximum_fusion), channel_id=1, source_target_pairs={{0,64},{64,128},{128,192},{192,0},{1,65},{65,129},{129,193},{193,1... | collective-permute-start | bytes 6152 | tf_op jit(solution)/shard_map/ppermute | solution.py:30
Sparse Core Ops, SparseCore 0:
  60.9 47.4 all-gather.6
  122.8 64.6 all-gather.8
  189.3 29.7 all-gather.10
  220.7 35.6 all-gather.12

commit v3 on v1

--- a/solution.py
+++ b/solution.py
@@ -47,15 +47,19 @@
             wanted[:, None, None] == slot_ids[None, :, :], axis=2
         ).astype(jnp.bfloat16)
         outgoing = jnp.dot(chooser, tokens, preferred_element_type=jnp.float32).astype(jnp.bfloat16)
-        outgoing = outgoing.reshape(columns, span, width)
+        outgoing = outgoing.reshape(columns, span * width // 128, 128)
         if previous is not None:
             outgoing, _ = lax.optimization_barrier((outgoing, previous))
         arrived = lax.all_to_all(outgoing, "col", split_axis=0, concat_axis=0, tiled=True)
         previous = arrived
         rows = lax.all_gather(arrived, "row", axis=0, tiled=False)
-        rows = rows.transpose(2, 0, 1, 3).reshape(span * groups * columns, width)
-        gate_part = jnp.dot(rows, w_gate[0], preferred_element_type=jnp.float32)
-        up_part = jnp.dot(rows, w_up[0], preferred_element_type=jnp.float32)
+        rows = rows.reshape(groups * columns, span, width // 128, 128)
+        gate_w = w_gate[0].reshape(width // 128, 128, unit_count)
+        up_w = w_up[0].reshape(width // 128, 128, unit_count)
+        gate_part = jnp.einsum("npak,aku->npu", rows, gate_w, preferred_element_type=jnp.float32)
+        up_part = jnp.einsum("npak,aku->npu", rows, up_w, preferred_element_type=jnp.float32)
+        gate_part = gate_part.reshape(groups * columns * span, unit_count)
+        up_part = up_part.reshape(groups * columns * span, unit_count)
         hidden = (jax.nn.silu(gate_part) * up_part).astype(jnp.bfloat16)
         stages.append((span, wanted, hidden))
 
@@ -67,7 +71,7 @@
         result = jnp.einsum(
             "jnu,juf->nf", hidden_all, w_down_parts, preferred_element_type=jnp.float32
         ).astype(jnp.bfloat16)
-        result = result.reshape(span, groups, columns, quarter).transpose(2, 1, 0, 3)
+        result = result.reshape(groups, columns, span, quarter).transpose(1, 0, 2, 3)
         back = lax.all_to_all(result, "col", split_axis=0, concat_axis=0, tiled=True)
         match = (all_slots[:, :, :, None] == wanted.astype(jnp.float32)[None, None, None, :])
         weights = jnp.sum(jnp.where(match, all_shares[:, :, :, None], 0.0), axis=2)

time: 347 us -> 343 us (0.988)
  blocking collectives: 115 us -> 104 us
  matrix products: 37.9 us -> 43.5 us
    all_to_all x2, blocking collectives: 97.8 us -> 86.7 us  [local(): lax.all_to_all(outgoing, 'col', split_axis=0, concat_axis=0, tiled=True)]
    reshape x4 -> x5, local copies, waits for them, and re-layouts: 11.1 us -> 16.9 us  [the longest x3 10.8 us: local(): result.reshape(groups, columns, span, quarter).transpose(1, 0, 2, 3)]
    all_gather x1 -> x0, local copies, waits for them, and re-layouts: 5.25 us -> none  [local(): rows = lax.all_gather(arrived, 'row', axis=0, tiled=False)]
    all_gather x2, waiting for transfers between devices: 42.1 us -> 37.3 us  [local(): hidden_all = lax.all_gather(hidden, 'row', axis=0, tiled=False)]
    transpose x0 -> x1, local copies, waits for them, and re-layouts: none -> 4.77 us  [local(): result.reshape(groups, columns, span, quarter).transpose(1, 0, 2, 3)]
    dot_general x4, matrix products: 16.3 us -> 19.8 us  [the longest x2 12.3 us: local(): jnp.einsum('npak,aku->npu', rows, gate_w, preferred_element_type=jnp.floa...]
  transfers between devices with their start and end apart: 9 -> 9, of which waited for: 8 -> 7; matrix products, arithmetic and copies ran while one was open for 14% -> 17% of each run, Pallas kernels for 0% -> 0%
where the time goes in v3:
time: 343 us; the launch traced here: 342 us
  waiting for transfers between devices  124 us (36%)
  blocking collectives  104 us (30%)
  matrix products  43.5 us (13%)
  local copies, waits for them, and re-layouts  29.2 us (9%)
  starting transfers between devices  25 us (7%)
  between operations  13.4 us (4%)
    all_to_all x2, blocking collectives, local(): lax.all_to_all(outgoing, 'col', split_axis=0, concat_axis=0, tiled=True)  86.7 us
    all_gather x2, waiting for transfers between devices, local(): rows = lax.all_gather(arrived, 'row', axis=0, tiled=False)  56 us
    all_gather x2, waiting for transfers between devices, local(): hidden_all = lax.all_gather(hidden, 'row', axis=0, tiled=False)  37.3 us
    all_to_all x2, waiting for transfers between devices, local(): lax.all_to_all(result, 'col', split_axis=0, concat_axis=0, tiled=True)  26.1 us
    all_to_all x2, starting transfers between devices, local(): lax.all_to_all(result, 'col', split_axis=0, concat_axis=0, tiled=True)  21.4 us
    all_to_all x1, blocking collectives, local(): lax.all_to_all(combined, 'row', split_axis=0, concat_axis=2, tiled=True)  17.7 us
    dot_general x2, matrix products, local(): jnp.einsum('npak,aku->npu', rows, gate_w, preferred_element_type=jnp.floa...  12.3 us
    reshape x3, local copies, waits for them, and re-layouts, local(): result.reshape(groups, columns, span, quarter).transpose(1, 0, 2, 3)  10.8 us
  transfers between devices with their start and end apart: 9, of which 7 were waited for; matrix products, arithmetic and copies ran while one was open for 17% of the time, Pallas kernels for 0%

profile of v3, /device:TPU:4, one launch (start us, length us, event | category | flops | bytes accessed | tf_op | source)
XLA Modules:
  0.0 341.5 jit_solution(10410554504399542658)
XLA Ops:
  6.5 0.9 copy.126
  7.5 0.1 eq.84
  7.6 0.1 eq.80
  7.8 0.6 reduce-window.6
  8.4 0.2 slice_reduce_fusion
  8.6 0.1 fusion.40
  8.7 0.1 reduce_sum.39
  8.9 0.7 fusion.42
  9.7 0.1 add.108
  10.0 2.6 convolution_convert_fusion.1
  12.6 2.3 reshape.130
  14.9 40.9 %all_to_all.35 = bf16[64,64,128]{2,1,0:T(8,128)(2,1)} all-to-all(bf16[64,64,128]{2,1,0:T(8,128)(2,1)} %reshape.130), channel_id=1, replica_groups=mesh['row'=4,'col'=64] {'col'}, dimensions={0} | all-to-all | bytes 2097152 | tf_op jit(solution)/shard_map/all_to_all | solution.py:53
  56.0 0.1 add.114
  56.2 2.9 convolution_convert_fusion
  59.2 3.8 %reshape.131 = bf16[64,96,128]{2,1,0:T(8,128)(2,1)} reshape(bf16[192,4096]{1,0:T(8,128)(2,1)} %convolution_convert_fusion) | data formatting | bytes 3145728 | tf_op jit(solution)/shard_map/reshape | solution.py:50
  63.0 45.8 %all_to_all.36 = bf16[64,96,128]{2,1,0:T(8,128)(2,1)} all-to-all(bf16[64,96,128]{2,1,0:T(8,128)(2,1)} %reshape.131), channel_id=1, replica_groups=mesh['row'=4,'col'=64] {'col'}, dimensions={0} | all-to-all | bytes 3145728 | tf_op jit(solution)/shard_map/all_to_all | solution.py:53
  108.9 5.6 %fusion.22 = f32[512,384]{1,0:T(8,128)S(1)} fusion(bf16[32,128,384]{2,1,0:T(8,128)(2,1)} %bitcast.112, bf16[512,32,128]{2,1,0:T(8,128)(2,1)} %bitcast.110), kind=kOutput, calls=%fused_computation.19 | convolution fusion | flops 1610612736 | bytes 8126464 | tf_op jit(solution)/shard_map/npak,aku->npu/dot_general | solution.py:59
  114.5 3.1 fusion.31
  117.7 0.2 all-gather.15.cloned.1.call-start
  117.9 56.0 %all-gather.13.cloned.1.call-done = bf16[256,96,128]{2,1,0:T(8,128)(2,1)} async-done(((bf16[64,96,128]{2,1,0:T(8,128)(2,1)}), bf16[256,96,128]{2,1,0:T(8,128)(2,1)}) %all-gather.13.cloned.1.call-update) | async-done | bytes 6291472 | tf_op jit(solution)/shard_map/all_gather | solution.py:55
  173.9 6.7 %fusion.10 = f32[768,384]{1,0:T(8,128)S(1)} fusion(bf16[32,128,384]{2,1,0:T(8,128)(2,1)} %bitcast.113, bf16[768,32,128]{2,1,0:T(8,128)(2,1)} %bitcast.108), kind=kOutput, calls=%fused_computation.15 | convolution fusion | flops 2415919104 | bytes 10616832 | tf_op jit(solution)/shard_map/npak,aku->npu/dot_general | solution.py:59
  180.6 4.4 %fusion.19 = bf16[768,384]{1,0:T(8,128)(2,1)} fusion(bf16[32,128,384]{2,1,0:T(8,128)(2,1)S(1)} %bitcast.115, bf16[768,32,128]{2,1,0:T(8,128)(2,1)S(1)} %bitcast.109, f32[768,384]{1,0:T(8,128)S(1)} %fusion.10), kind=kOutput, calls=%fused_computation.18 | convolution fusion | flops 2417688576 | bytes 11206656 | tf_op jit(solution)/shard_map/npak,aku->npu/dot_general | solution.py:60
  185.0 20.5 %all-gather.11.cloned.1.call-done = bf16[2048,384]{1,0:T(8,128)(2,1)} async-done(((bf16[512,384]{1,0:T(8,128)(2,1)}), bf16[2048,384]{1,0:T(8,128)(2,1)}) %all-gather.11.cloned.1.call-update) | async-done | bytes 1572880 | tf_op jit(solution)/shard_map/all_gather | solution.py:68
  205.5 4.2 %bitcast_convert_fusion.1 = bf16[512,1024]{1,0:T(8,128)(2,1)} fusion(bf16[4,512,384]{2,1,0:T(8,128)(2,1)} %bitcast.117, bf16[4,384,1024]{2,1,0:T(8,128)(2,1)S(1)} %bitcast.92), kind=kOutput, calls=%fused_computation.13 | convolution fusion | flops 1611137024 | bytes 5767168 | tf_op jit(solution)/shard_map/jnu,juf->nf/dot_general | solution.py:71
  209.7 2.3 reshape.132
  211.9 3.4 copy.193
  215.3 10.7 %all-to-all-start.2 = ((bf16[64,4,2,1024]{3,2,1,0:T(2,128)(2,1)}), bf16[64,4,2,1024]{3,2,1,0:T(2,128)(2,1)}, u32[]{:S(2)}, u32[]{:S(2)}) async-start(bf16[64,4,2,1024]{3,2,1,0:T(2,128)(2,1)} %bitcast.95), calls=%async_computation.2 | async-start | bytes 2097152 | tf_op jit(solution)/shard_map/all_to_all | solution.py:75
  226.0 16.8 %all-gather.15.cloned.1.call-done = bf16[3072,384]{1,0:T(8,128)(2,1)} async-done(((bf16[768,384]{1,0:T(8,128)(2,1)}), bf16[3072,384]{1,0:T(8,128)(2,1)}) %all-gather.15.cloned.1.call-update) | async-done | bytes 2359312 | tf_op jit(solution)/shard_map/all_gather | solution.py:68
  242.9 5.4 %bitcast_convert_fusion = bf16[768,1024]{1,0:T(8,128)(2,1)} fusion(bf16[4,768,384]{2,1,0:T(8,128)(2,1)} %bitcast.116, bf16[4,384,1024]{2,1,0:T(8,128)(2,1)S(1)} %bitcast.93), kind=kOutput, calls=%fused_computation.10 | convolution fusion | flops 2416705536 | bytes 7077888 | tf_op jit(solution)/shard_map/jnu,juf->nf/dot_general | solution.py:71
  248.3 5.1 %reshape.134 = bf16[4,64,3,1024]{3,2,1,0:T(4,128)(2,1)} reshape(bf16[768,1024]{1,0:T(8,128)(2,1)} %bitcast_convert_fusion) | data formatting | bytes 3145728 | tf_op jit(solution)/shard_map/reshape | solution.py:74
  253.4 4.8 %copy.151 = bf16[64,4,3,1024]{3,1,2,0:T(4,128)(2,1)} copy(bf16[64,4,3,1024]{3,2,0,1:T(4,128)(2,1)} %bitcast.94) | data formatting | bytes 3145728 | tf_op jit(solution)/shard_map/transpose | solution.py:74
  258.2 10.7 %all-to-all-start.3 = ((bf16[64,4,3,1024]{3,1,2,0:T(4,128)(2,1)}), bf16[64,4,3,1024]{3,1,2,0:T(4,128)(2,1)}, u32[]{:S(2)}, u32[]{:S(2)}) async-start(bf16[64,4,3,1024]{3,1,2,0:T(4,128)(2,1)} %copy.151), calls=%async_computation.3 | async-start | bytes 3145728 | tf_op jit(solution)/shard_map/all_to_all | solution.py:75
  269.0 0.9 collective-permute-start
  269.9 1.8 collective-permute-start.1
  271.7 0.6 collective-permute-start.2
  272.3 0.4 collective-permute-done
  272.6 2.3 collective-permute-done.1
  275.0 1.5 collective-permute-done.2
  276.5 0.3 select_reduce_fusion.1
  276.9 0.8 copy.140
  277.7 0.1 select_reduce_fusion
  277.8 0.3 copy.150
  278.1 4.7 %fusion.34 = f32[4,128,1024,1]{2,1,3,0:T(8,128)} fusion(bf16[64,4,2,1024]{3,2,1,0:T(2,128)(2,1)} %all-to-all-done.2, f32[4,128,64,2]{1,3,2,0:T(2,128)} %bitcast.99), kind=kOutput, calls=%fused_computation.23 | convolution fusion | flops 805306368 | bytes 3407872 | tf_op jit(solution)/shard_map/rtep,erpf->rtf/dot_general | solution.py:79
  282.8 26.1 %all-to-all-done.3 = bf16[64,4,3,1024]{3,1,2,0:T(4,128)(2,1)} async-done(((bf16[64,4,3,1024]{3,1,2,0:T(4,128)(2,1)}), bf16[64,4,3,1024]{3,1,2,0:T(4,128)(2,1)}, u32[]{:S(2)}, u32[]{:S(2)}) %all-to-all-start.3) | async-done | bytes 1572896 | tf_op jit(solution)/shard_map/all_to_all | solution.py:75
  308.9 3.9 %fusion.8 = bf16[4,128,1024]{2,1,0:T(8,128)(2,1)S(1)} fusion(f32[4,128,1024,1]{2,1,3,0:T(8,128)} %fusion.34, bf16[64,4,3,1024]{3,1,2,0:T(4,128)(2,1)} %all-to-all-done.3, f32[4,128,64,3]{1,0,3,2:T(4,128)S(1)} %bitcast.98), kind=kOutput, calls=%fused_computation.12 | convolution fusion | flops 1209008128 | bytes 5111808 | tf_op jit(solution)/shard_map/rtep,erpf->rtf/dot_general | solution.py:79
  312.8 17.7 %all_to_all.37 = bf16[4,128,1024]{2,1,0:T(8,128)(2,1)} all-to-all(bf16[4,128,1024]{2,1,0:T(8,128)(2,1)S(1)} %fusion.8), channel_id=1, replica_groups=mesh['row'=4,'col'=64] {'row'}, dimensions={0} | all-to-all | bytes 2097152 | tf_op jit(solution)/shard_map/all_to_all | solution.py:84
  330.4 2.3 copy.154
  332.7 2.3 copy.155
  (40 shorter events, 0.8 us)
Async XLA Ops:
  6.5 199.0 %copy-start = (bf16[1,1536,1024]{2,1,0:T(8,128)(2,1)S(1)}, bf16[1,1536,1024]{2,1,0:T(8,128)(2,1)}, u32[]{:S(2)}) copy-start(bf16[1,1536,1024]{2,1,0:T(8,128)(2,1)} %param.11) | copy-start | bytes 9437188
  6.5 102.3 %all-gather.9.cloned.1.call-start = ((), (), s32[]{:S(2)}) async-start(), calls=%async_computation.5 | async-start | bytes 5242880 | tf_op jit(solution)/shard_map/all_gather | solution.py:55
  55.9 118.0 %all-gather.13.cloned.1.call-start = ((), (), s32[]{:S(2)}) async-start(), calls=%async_computation.7 | async-start | bytes 7864320 | tf_op jit(solution)/shard_map/all_gather | solution.py:55
  108.8 96.7 %all-gather.11.cloned.1.call-start = ((), (), s32[]{:S(2)}) async-start(), calls=%async_computation.6 | async-start | bytes 1966080 | tf_op jit(solution)/shard_map/all_gather | solution.py:68
  108.8 5.7 %copy-start.3 = (bf16[256,64,128]{2,1,0:T(8,128)(2,1)S(1)}, bf16[256,64,128]{2,1,0:T(8,128)(2,1)}, u32[]{:S(2)}) copy-start(bf16[256,64,128]{2,1,0:T(8,128)(2,1)} %all-gather.9.cloned.1.call-done) | copy-start | bytes 12582916
  108.9 5.7 %copy-start.4 = (bf16[1,4096,384]{2,1,0:T(8,128)(2,1)S(1)}, bf16[1,4096,384]{2,1,0:T(8,128)(2,1)}, u32[]{:S(2)}) copy-start(bf16[1,4096,384]{2,1,0:T(8,128)(2,1)} %param.10) | copy-start | bytes 9437188
  117.7 125.2 %all-gather.15.cloned.1.call-start = ((), (), s32[]{:S(2)}) async-start(), calls=%async_computation.8 | async-start | bytes 2949120 | tf_op jit(solution)/shard_map/all_gather | solution.py:68
  173.9 6.7 %copy-start.2 = (bf16[256,96,128]{2,1,0:T(8,128)(2,1)S(1)}, bf16[256,96,128]{2,1,0:T(8,128)(2,1)}, u32[]{:S(2)}) copy-start(bf16[256,96,128]{2,1,0:T(8,128)(2,1)} %all-gather.13.cloned.1.call-done) | copy-start | bytes 18874372
  173.9 6.7 %copy-start.5 = (bf16[1,4096,384]{2,1,0:T(8,128)(2,1)S(1)}, bf16[1,4096,384]{2,1,0:T(8,128)(2,1)}, u32[]{:S(2)}) copy-start(bf16[1,4096,384]{2,1,0:T(8,128)(2,1)} %param.10) | copy-start | bytes 9437188
  215.3 42.9 %all-to-all-start.2 = ((bf16[64,4,2,1024]{3,2,1,0:T(2,128)(2,1)}), bf16[64,4,2,1024]{3,2,1,0:T(2,128)(2,1)}, u32[]{:S(2)}, u32[]{:S(2)}) async-start(bf16[64,4,2,1024]{3,2,1,0:T(2,128)(2,1)} %bitcast.95), calls=%async_computation.2 | async-start | bytes 2097152 | tf_op jit(solution)/shard_map/all_to_all | solution.py:75
  253.4 15.5 %copy-start.1 = (f32[128,2]{0,1:T(2,128)S(1)}, f32[128,2]{0,1:T(2,128)}, u32[]{:S(2)}) copy-start(f32[128,2]{0,1:T(2,128)} %param.8) | copy-start | bytes 3076
  258.2 50.7 %all-to-all-start.3 = ((bf16[64,4,3,1024]{3,1,2,0:T(4,128)(2,1)}), bf16[64,4,3,1024]{3,1,2,0:T(4,128)(2,1)}, u32[]{:S(2)}, u32[]{:S(2)}) async-start(bf16[64,4,3,1024]{3,1,2,0:T(4,128)(2,1)} %copy.151), calls=%async_computation.3 | async-start | bytes 3145728 | tf_op jit(solution)/shard_map/all_to_all | solution.py:75
  269.0 3.7 %collective-permute-start = (f32[128,4]{0,1:T(4,128)S(1)}, f32[128,4]{0,1:T(4,128)S(1)}, u32[]{:S(2)}, u32[]{:S(2)}) collective-permute-start(f32[128,4]{0,1:T(4,128)S(1)} %pad_maximum_fusion), channel_id=1, source_target_pairs={{0,192},{64,0},{128,64},{192,128},{1,193},{65,1},{129,65},{193,129... | collective-permute-start | bytes 6152 | tf_op jit(solution)/shard_map/ppermute | solution.py:30
  269.9 5.1 %collective-permute-start.1 = (f32[128,4]{0,1:T(4,128)S(1)}, f32[128,4]{0,1:T(4,128)S(1)}, u32[]{:S(2)}, u32[]{:S(2)}) collective-permute-start(f32[128,4]{0,1:T(4,128)S(1)} %pad_maximum_fusion), channel_id=1, source_target_pairs={{0,128},{64,192},{128,0},{192,64},{1,129},{65,193},{129,1},{193,65... | collective-permute-start | bytes 6152 | tf_op jit(solution)/shard_map/ppermute | solution.py:30
  271.7 4.8 %collective-permute-start.2 = (f32[128,4]{0,1:T(4,128)S(1)}, f32[128,4]{0,1:T(4,128)S(1)}, u32[]{:S(2)}, u32[]{:S(2)}) collective-permute-start(f32[128,4]{0,1:T(4,128)S(1)} %pad_maximum_fusion), channel_id=1, source_target_pairs={{0,64},{64,128},{128,192},{192,0},{1,65},{65,129},{129,193},{193,1... | collective-permute-start | bytes 6152 | tf_op jit(solution)/shard_map/ppermute | solution.py:30
Sparse Core Ops, SparseCore 0:
  56.0 47.4 all-gather.8
  108.9 64.9 all-gather.12
  175.7 29.7 all-gather.10
  207.2 35.6 all-gather.14

commit v4 on v3

--- a/solution.py
+++ b/solution.py
@@ -30,11 +30,8 @@
         shifted.append(lax.ppermute(meta, "row", pairs))
     order = jnp.stack([shifted[(-s) % groups] for s in range(groups)])
     meta = jnp.roll(order, my_row, axis=0)
-    all_slots = meta[:, :, :top_count]
-    all_shares = meta[:, :, top_count:]
 
     w_down_parts = w_down[0].reshape(groups, unit_count, quarter)
-    combined = jnp.zeros((groups, token_count, quarter), jnp.float32)
     previous = None
     stages = []
     for lo, hi in CHUNKS:
@@ -49,7 +46,7 @@
         outgoing = jnp.dot(chooser, tokens, preferred_element_type=jnp.float32).astype(jnp.bfloat16)
         outgoing = outgoing.reshape(columns, span * width // 128, 128)
         if previous is not None:
-            outgoing, _ = lax.optimization_barrier((outgoing, previous))
+            outgoing, _, meta = lax.optimization_barrier((outgoing, previous, meta))
         arrived = lax.all_to_all(outgoing, "col", split_axis=0, concat_axis=0, tiled=True)
         previous = arrived
         rows = lax.all_gather(arrived, "row", axis=0, tiled=False)
@@ -63,23 +60,26 @@
         hidden = (jax.nn.silu(gate_part) * up_part).astype(jnp.bfloat16)
         stages.append((span, wanted, hidden))
 
-    combined = jnp.zeros((groups, token_count, quarter), jnp.float32)
-    for index, (span, wanted, hidden) in enumerate(stages):
-        hidden_all = lax.all_gather(hidden, "row", axis=0, tiled=False)
-        if index + 1 < len(stages):
-            hidden_all, _ = lax.optimization_barrier((hidden_all, stages[index + 1][2]))
-        result = jnp.einsum(
-            "jnu,juf->nf", hidden_all, w_down_parts, preferred_element_type=jnp.float32
-        ).astype(jnp.bfloat16)
-        result = result.reshape(groups, columns, span, quarter).transpose(1, 0, 2, 3)
-        back = lax.all_to_all(result, "col", split_axis=0, concat_axis=0, tiled=True)
-        match = (all_slots[:, :, :, None] == wanted.astype(jnp.float32)[None, None, None, :])
-        weights = jnp.sum(jnp.where(match, all_shares[:, :, :, None], 0.0), axis=2)
-        weights = weights.reshape(groups, token_count, experts, span)
-        combined = combined + jnp.einsum(
-            "rtep,erpf->rtf", weights, back.astype(jnp.float32),
-            precision=lax.Precision.HIGHEST, preferred_element_type=jnp.float32,
-        )
+    all_slots = meta[:, :, :top_count]
+    all_shares = meta[:, :, top_count:]
+    joined = jnp.concatenate(
+        [h.reshape(groups, columns, span, unit_count).transpose(1, 0, 2, 3) for span, _, h in stages],
+        axis=2,
+    ).reshape(columns * groups * capacity, unit_count)
+    hidden_all = lax.all_gather(joined, "row", axis=0, tiled=False)
+    result = jnp.einsum(
+        "jnu,juf->nf", hidden_all, w_down_parts, preferred_element_type=jnp.float32
+    ).astype(jnp.bfloat16)
+    result = result.reshape(columns, groups, capacity, quarter)
+    back = lax.all_to_all(result, "col", split_axis=0, concat_axis=0, tiled=True)
+    wanted = jnp.arange(experts * capacity, dtype=jnp.float32)
+    match = (all_slots[:, :, :, None] == wanted[None, None, None, :])
+    weights = jnp.sum(jnp.where(match, all_shares[:, :, :, None], 0.0), axis=2)
+    weights = weights.reshape(groups, token_count, experts, capacity)
+    combined = jnp.einsum(
+        "rtep,erpf->rtf", weights, back.astype(jnp.float32),
+        precision=lax.Precision.HIGHEST, preferred_element_type=jnp.float32,
+    )
     combined = combined.astype(jnp.bfloat16)
     home = lax.all_to_all(combined, "row", split_axis=0, concat_axis=2, tiled=True)
     return home.reshape(token_count, width)

time: 343 us -> 376 us (1.096)
  waiting for transfers between devices: 124 us -> 163 us
  starting transfers between devices: 25 us -> 16.9 us
  local copies, waits for them, and re-layouts: 29.2 us -> 36.5 us
  matrix products: 43.5 us -> 38 us
    all_to_all x2 -> x1, waiting for transfers between devices: 26.1 us -> 61 us  [local(): lax.all_to_all(result, 'col', split_axis=0, concat_axis=0, tiled=True)]
    all_gather x2 -> x1, waiting for transfers between devices: 37.3 us -> 49.5 us  [local(): hidden_all = lax.all_gather(joined, 'row', axis=0, tiled=False)]
    all_to_all x2 -> x1, starting transfers between devices: 21.4 us -> 10.7 us  [local(): lax.all_to_all(result, 'col', split_axis=0, concat_axis=0, tiled=True)]
    reshape x3 -> x4, local copies, waits for them, and re-layouts: 10.8 us -> 18.1 us  [the longest x2 14.9 us: local(): result = result.reshape(columns, groups, capacity, quarter)]
    transpose x1 -> x0, local copies, waits for them, and re-layouts: 4.77 us -> none  [local(): result.reshape(groups, columns, span, quarter).transpose(1, 0, 2, 3)]
    ppermute x3, waiting for transfers between devices: 4.2 us -> 0.01 us  [local(): shifted.append(lax.ppermute(meta, 'row', pairs))]
    all_gather x2, waiting for transfers between devices: 56 us -> 52.1 us  [local(): rows = lax.all_gather(arrived, 'row', axis=0, tiled=False)]
    dot_general x2 -> x1, matrix products: 8.57 us -> 4.93 us  [local(): jnp.einsum('rtep,erpf->rtf', weights, back.astype(jnp.float32), precision...]
  transfers between devices with their start and end apart: 9 -> 7, of which waited for: 7 -> 3; matrix products, arithmetic and copies ran while one was open for 17% -> 5% of each run, Pallas kernels for 0% -> 0%
where the time goes in v4:
time: 376 us; the launch traced here: 375 us
  waiting for transfers between devices  163 us (43%)
  blocking collectives  104 us (28%)
  matrix products  38 us (10%)
  local copies, waits for them, and re-layouts  36.5 us (10%)
  starting transfers between devices  16.9 us (4%)
  between operations  13.3 us (4%)
  other arithmetic  3.95 us (1%)
    all_to_all x2, blocking collectives, local(): lax.all_to_all(outgoing, 'col', split_axis=0, concat_axis=0, tiled=True)  86.7 us
    all_to_all x1, waiting for transfers between devices, local(): lax.all_to_all(result, 'col', split_axis=0, concat_axis=0, tiled=True)  61 us
    all_gather x2, waiting for transfers between devices, local(): rows = lax.all_gather(arrived, 'row', axis=0, tiled=False)  52.1 us
    all_gather x1, waiting for transfers between devices, local(): hidden_all = lax.all_gather(joined, 'row', axis=0, tiled=False)  49.5 us
    all_to_all x1, blocking collectives, local(): lax.all_to_all(combined, 'row', split_axis=0, concat_axis=2, tiled=True)  17.2 us
    reshape x2, local copies, waits for them, and re-layouts, local(): result = result.reshape(columns, groups, capacity, quarter)  14.9 us
    dot_general x2, matrix products, local(): jnp.einsum('npak,aku->npu', rows, gate_w, preferred_element_type=jnp.floa...  12.3 us
    all_to_all x1, starting transfers between devices, local(): lax.all_to_all(result, 'col', split_axis=0, concat_axis=0, tiled=True)  10.7 us
  transfers between devices with their start and end apart: 7, of which 3 were waited for; matrix products, arithmetic and copies ran while one was open for 5% of the time, Pallas kernels for 0%

profile of v4, /device:TPU:4, one launch (start us, length us, event | category | flops | bytes accessed | tf_op | source)
XLA Modules:
  0.0 375.2 jit_solution(10077592479357608019)
XLA Ops:
  6.5 0.9 copy.109
  7.5 0.1 eq.72
  7.6 0.1 eq.68
  7.8 0.1 iota_add_fusion
  7.8 0.1 add.80
  8.0 0.6 reduce-window.6
  8.6 0.2 slice_reduce_fusion
  8.8 0.1 fusion.39
  8.9 0.1 reduce_sum.30
  9.1 0.1 copy.112
  9.2 0.7 fusion.41
  9.9 0.1 compare_reduce_fusion.1
  10.0 2.6 convolution_convert_fusion.1
  12.6 2.4 reshape.104
  14.9 40.9 %all_to_all.30 = bf16[64,64,128]{2,1,0:T(8,128)(2,1)} all-to-all(bf16[64,64,128]{2,1,0:T(8,128)(2,1)} %reshape.104), channel_id=1, replica_groups=mesh['row'=4,'col'=64] {'col'}, dimensions={0} | all-to-all | bytes 2097152 | tf_op jit(solution)/shard_map/all_to_all | solution.py:50
  55.9 0.0 all-gather.10.cloned.1.call-start
  56.0 1.6 collective-permute-start.2
  57.6 2.9 collective-permute-start.1
  60.5 1.3 collective-permute-start
  61.9 0.1 broadcast_add_fusion
  62.0 0.1 add.75
  62.1 0.1 compare_reduce_fusion
  62.2 2.9 convolution_convert_fusion
  65.1 3.8 %reshape.103 = bf16[64,96,128]{2,1,0:T(8,128)(2,1)} reshape(bf16[192,4096]{1,0:T(8,128)(2,1)} %convolution_convert_fusion) | data formatting | bytes 3145728 | tf_op jit(solution)/shard_map/reshape | solution.py:47
  69.1 45.8 %all_to_all.31 = bf16[64,96,128]{2,1,0:T(8,128)(2,1)} all-to-all(bf16[64,96,128]{2,1,0:T(8,128)(2,1)} %reshape.103), channel_id=1, replica_groups=mesh['row'=4,'col'=64] {'col'}, dimensions={0} | all-to-all | bytes 3145728 | tf_op jit(solution)/shard_map/all_to_all | solution.py:50
  114.9 0.2 all-gather.6.cloned.1.call-start
  115.2 5.6 %fusion.24 = f32[512,384]{1,0:T(8,128)S(1)} fusion(bf16[32,128,384]{2,1,0:T(8,128)(2,1)} %bitcast.96, bf16[512,32,128]{2,1,0:T(8,128)(2,1)} %bitcast.94), kind=kOutput, calls=%fused_computation.21 | convolution fusion | flops 1610612736 | bytes 8126464 | tf_op jit(solution)/shard_map/npak,aku->npu/dot_general | solution.py:56
  120.8 3.1 fusion.33
  123.9 1.2 reshape.106
  125.1 52.1 %all-gather.10.cloned.1.call-done = bf16[256,96,128]{2,1,0:T(8,128)(2,1)} async-done(((bf16[64,96,128]{2,1,0:T(8,128)(2,1)}), bf16[256,96,128]{2,1,0:T(8,128)(2,1)}) %all-gather.10.cloned.1.call-update) | async-done | bytes 6291472 | tf_op jit(solution)/shard_map/all_gather | solution.py:52
  177.2 6.7 %fusion.12 = f32[768,384]{1,0:T(8,128)S(1)} fusion(bf16[32,128,384]{2,1,0:T(8,128)(2,1)} %bitcast.97, bf16[768,32,128]{2,1,0:T(8,128)(2,1)} %bitcast.92), kind=kOutput, calls=%fused_computation.15 | convolution fusion | flops 2415919104 | bytes 10616832 | tf_op jit(solution)/shard_map/npak,aku->npu/dot_general | solution.py:56
  183.9 4.4 %fusion.21 = bf16[768,384]{1,0:T(8,128)(2,1)} fusion(bf16[32,128,384]{2,1,0:T(8,128)(2,1)S(1)} %bitcast.99, bf16[768,32,128]{2,1,0:T(8,128)(2,1)S(1)} %bitcast.93, f32[768,384]{1,0:T(8,128)S(1)} %fusion.12), kind=kOutput, calls=%fused_computation.18 | convolution fusion | flops 2417688576 | bytes 11206656 | tf_op jit(solution)/shard_map/npak,aku->npu/dot_general | solution.py:57
  188.3 2.0 reshape.107
  190.3 1.9 pad_maximum_fusion
  192.2 1.3 copy.128
  193.5 3.1 all_gather_reshape.3
  196.6 49.5 %all-gather.6.cloned.1.call-done = bf16[4,1280,384]{2,1,0:T(8,128)(2,1)} async-done(((bf16[1,1280,384]{2,1,0:T(8,128)(2,1)}), bf16[4,1280,384]{2,1,0:T(8,128)(2,1)}) %all-gather.6.cloned.1.call-update) | async-done | bytes 3932176 | tf_op jit(solution)/shard_map/all_gather | solution.py:69
  246.1 7.7 %bitcast_convert_fusion = bf16[1280,1024]{1,0:T(8,128)(2,1)} fusion(bf16[4,1280,384]{2,1,0:T(8,128)(2,1)} %all-gather.6.cloned.1.call-done, bf16[4,384,1024]{2,1,0:T(8,128)(2,1)S(1)} %bitcast.78), kind=kOutput, calls=%fused_computation.4 | convolution fusion | flops 4027842560 | bytes 9699328 | tf_op jit(solution)/shard_map/jnu,juf->nf/dot_general | solution.py:70
  253.9 6.0 %reshape.108 = bf16[64,4,5,1024]{3,2,1,0:T(8,128)(2,1)} reshape(bf16[1280,1024]{1,0:T(8,128)(2,1)} %bitcast_convert_fusion) | data formatting | bytes 5242880 | tf_op jit(solution)/shard_map/reshape | solution.py:73
  259.9 8.9 %copy.129 = bf16[64,4,5,1024]{3,1,2,0:T(4,128)(2,1)} copy(bf16[64,4,5,1024]{3,2,1,0:T(8,128)(2,1)} %reshape.108) | data formatting | bytes 5242880 | tf_op jit(solution)/shard_map/reshape | solution.py:73
  268.8 10.7 %all-to-all-start.2 = ((bf16[64,4,5,1024]{3,1,2,0:T(4,128)(2,1)}), bf16[64,4,5,1024]{3,1,2,0:T(4,128)(2,1)}, u32[]{:S(2)}, u32[]{:S(2)}) async-start(bf16[64,4,5,1024]{3,1,2,0:T(4,128)(2,1)} %copy.129), calls=%async_computation.2 | async-start | bytes 5242880 | tf_op jit(solution)/shard_map/all_to_all | solution.py:74
  279.5 0.2 select_reduce_fusion
  279.7 1.3 copy.123
  281.0 61.0 %all-to-all-done.2 = bf16[64,4,5,1024]{3,1,2,0:T(4,128)(2,1)} async-done(((bf16[64,4,5,1024]{3,1,2,0:T(4,128)(2,1)}), bf16[64,4,5,1024]{3,1,2,0:T(4,128)(2,1)}, u32[]{:S(2)}, u32[]{:S(2)}) %all-to-all-start.2) | async-done | bytes 2621472 | tf_op jit(solution)/shard_map/all_to_all | solution.py:74
  341.9 4.9 %bitcast_convert_fusion.1 = bf16[4,128,1024]{2,1,0:T(8,128)(2,1)S(1)} fusion(bf16[64,4,5,1024]{3,1,2,0:T(4,128)(2,1)} %all-to-all-done.2, f32[4,128,64,5]{1,0,3,2:T(4,128)} %bitcast.82), kind=kOutput, calls=%fused_computation.13 | convolution fusion | flops 2013790208 | bytes 4325376 | tf_op jit(solution)/shard_map/rtep,erpf->rtf/dot_general | solution.py:79
  346.9 17.2 %all_to_all.32 = bf16[4,128,1024]{2,1,0:T(8,128)(2,1)} all-to-all(bf16[4,128,1024]{2,1,0:T(8,128)(2,1)S(1)} %bitcast_convert_fusion.1), channel_id=1, replica_groups=mesh['row'=4,'col'=64] {'row'}, dimensions={0} | all-to-all | bytes 2097152 | tf_op jit(solution)/shard_map/all_to_all | solution.py:84
  364.1 2.3 copy.132
  366.4 2.3 copy.133
  (33 shorter events, 0.3 us)
Async XLA Ops:
  6.5 239.6 %copy-start = (bf16[1,1536,1024]{2,1,0:T(8,128)(2,1)S(1)}, bf16[1,1536,1024]{2,1,0:T(8,128)(2,1)}, u32[]{:S(2)}) copy-start(bf16[1,1536,1024]{2,1,0:T(8,128)(2,1)} %param.11) | copy-start | bytes 9437188
  6.5 108.6 %all-gather.8.cloned.1.call-start = ((), (), s32[]{:S(2)}) async-start(), calls=%async_computation.5 | async-start | bytes 5242880 | tf_op jit(solution)/shard_map/all_gather | solution.py:52
  12.6 43.3 %copy-start.1 = (f32[128,2]{0,1:T(2,128)S(1)}, f32[128,2]{0,1:T(2,128)}, u32[]{:S(2)}) copy-start(f32[128,2]{0,1:T(2,128)} %param.8) | copy-start | bytes 3076
  55.9 121.3 %all-gather.10.cloned.1.call-start = ((), (), s32[]{:S(2)}) async-start(), calls=%async_computation.6 | async-start | bytes 7864320 | tf_op jit(solution)/shard_map/all_gather | solution.py:52
  56.0 13.0 %collective-permute-start.2 = (f32[128,4]{0,1:T(4,128)S(1)}, f32[128,4]{0,1:T(4,128)S(1)}, u32[]{:S(2)}, u32[]{:S(2)}) collective-permute-start(f32[128,4]{0,1:T(4,128)S(1)} %pad_maximum_fusion.1), channel_id=1, source_target_pairs={{0,64},{64,128},{128,192},{192,0},{1,65},{65,129},{129,193},{193,1... | collective-permute-start | bytes 6152 | tf_op jit(solution)/shard_map/ppermute | solution.py:30
  57.6 11.4 %collective-permute-start.1 = (f32[128,4]{0,1:T(4,128)S(1)}, f32[128,4]{0,1:T(4,128)S(1)}, u32[]{:S(2)}, u32[]{:S(2)}) collective-permute-start(f32[128,4]{0,1:T(4,128)S(1)} %pad_maximum_fusion.1), channel_id=1, source_target_pairs={{0,128},{64,192},{128,0},{192,64},{1,129},{65,193},{129,1},{193,65... | collective-permute-start | bytes 6152 | tf_op jit(solution)/shard_map/ppermute | solution.py:30
  60.5 8.5 %collective-permute-start = (f32[128,4]{0,1:T(4,128)S(1)}, f32[128,4]{0,1:T(4,128)S(1)}, u32[]{:S(2)}, u32[]{:S(2)}) collective-permute-start(f32[128,4]{0,1:T(4,128)S(1)} %pad_maximum_fusion.1), channel_id=1, source_target_pairs={{0,192},{64,0},{128,64},{192,128},{1,193},{65,1},{129,65},{193,129... | collective-permute-start | bytes 6152 | tf_op jit(solution)/shard_map/ppermute | solution.py:30
  114.9 131.3 %all-gather.6.cloned.1.call-start = ((), (), s32[]{:S(2)}) async-start(), calls=%async_computation.4 | async-start | bytes 4915200 | tf_op jit(solution)/shard_map/all_gather | solution.py:69
  115.1 5.7 %copy-start.3 = (bf16[256,64,128]{2,1,0:T(8,128)(2,1)S(1)}, bf16[256,64,128]{2,1,0:T(8,128)(2,1)}, u32[]{:S(2)}) copy-start(bf16[256,64,128]{2,1,0:T(8,128)(2,1)} %all-gather.8.cloned.1.call-done) | copy-start | bytes 12582916
  115.1 5.7 %copy-start.4 = (bf16[1,4096,384]{2,1,0:T(8,128)(2,1)S(1)}, bf16[1,4096,384]{2,1,0:T(8,128)(2,1)}, u32[]{:S(2)}) copy-start(bf16[1,4096,384]{2,1,0:T(8,128)(2,1)} %param.10) | copy-start | bytes 9437188
  177.2 6.7 %copy-start.2 = (bf16[256,96,128]{2,1,0:T(8,128)(2,1)S(1)}, bf16[256,96,128]{2,1,0:T(8,128)(2,1)}, u32[]{:S(2)}) copy-start(bf16[256,96,128]{2,1,0:T(8,128)(2,1)} %all-gather.10.cloned.1.call-done) | copy-start | bytes 18874372
  177.2 6.7 %copy-start.5 = (bf16[1,4096,384]{2,1,0:T(8,128)(2,1)S(1)}, bf16[1,4096,384]{2,1,0:T(8,128)(2,1)}, u32[]{:S(2)}) copy-start(bf16[1,4096,384]{2,1,0:T(8,128)(2,1)} %param.10) | copy-start | bytes 9437188
  268.8 73.2 %all-to-all-start.2 = ((bf16[64,4,5,1024]{3,1,2,0:T(4,128)(2,1)}), bf16[64,4,5,1024]{3,1,2,0:T(4,128)(2,1)}, u32[]{:S(2)}, u32[]{:S(2)}) async-start(bf16[64,4,5,1024]{3,1,2,0:T(4,128)(2,1)} %copy.129), calls=%async_computation.2 | async-start | bytes 5242880 | tf_op jit(solution)/shard_map/all_to_all | solution.py:74
Sparse Core Ops, SparseCore 0:
  56.0 47.4 all-gather.7
  115.0 62.1 all-gather.9
  196.8 49.3 all-gather.5

commit v5 on v3

--- a/solution.py
+++ b/solution.py
@@ -30,8 +30,6 @@
         shifted.append(lax.ppermute(meta, "row", pairs))
     order = jnp.stack([shifted[(-s) % groups] for s in range(groups)])
     meta = jnp.roll(order, my_row, axis=0)
-    all_slots = meta[:, :, :top_count]
-    all_shares = meta[:, :, top_count:]
 
     w_down_parts = w_down[0].reshape(groups, unit_count, quarter)
     combined = jnp.zeros((groups, token_count, quarter), jnp.float32)
@@ -49,7 +47,7 @@
         outgoing = jnp.dot(chooser, tokens, preferred_element_type=jnp.float32).astype(jnp.bfloat16)
         outgoing = outgoing.reshape(columns, span * width // 128, 128)
         if previous is not None:
-            outgoing, _ = lax.optimization_barrier((outgoing, previous))
+            outgoing, _, meta = lax.optimization_barrier((outgoing, previous, meta))
         arrived = lax.all_to_all(outgoing, "col", split_axis=0, concat_axis=0, tiled=True)
         previous = arrived
         rows = lax.all_gather(arrived, "row", axis=0, tiled=False)
@@ -63,14 +61,20 @@
         hidden = (jax.nn.silu(gate_part) * up_part).astype(jnp.bfloat16)
         stages.append((span, wanted, hidden))
 
+    all_slots = meta[:, :, :top_count]
+    all_shares = meta[:, :, top_count:]
+    down_blocks = [
+        lax.dynamic_index_in_dim(w_down_parts, (my_row - step) % groups, axis=0, keepdims=False)
+        for step in range(groups)
+    ]
     combined = jnp.zeros((groups, token_count, quarter), jnp.float32)
     for index, (span, wanted, hidden) in enumerate(stages):
-        hidden_all = lax.all_gather(hidden, "row", axis=0, tiled=False)
-        if index + 1 < len(stages):
-            hidden_all, _ = lax.optimization_barrier((hidden_all, stages[index + 1][2]))
-        result = jnp.einsum(
-            "jnu,juf->nf", hidden_all, w_down_parts, preferred_element_type=jnp.float32
-        ).astype(jnp.bfloat16)
+        total = jnp.dot(hidden, down_blocks[0], preferred_element_type=jnp.float32)
+        for step in range(1, groups):
+            pairs = [(i, (i + step) % groups) for i in range(groups)]
+            moved = lax.ppermute(hidden, "row", pairs)
+            total = total + jnp.dot(moved, down_blocks[step], preferred_element_type=jnp.float32)
+        result = total.astype(jnp.bfloat16)
         result = result.reshape(groups, columns, span, quarter).transpose(1, 0, 2, 3)
         back = lax.all_to_all(result, "col", split_axis=0, concat_axis=0, tiled=True)
         match = (all_slots[:, :, :, None] == wanted.astype(jnp.float32)[None, None, None, :])

time: 343 us -> 326 us (0.950)
  waiting for transfers between devices: 124 us -> 105 us
    ppermute x0 -> x6, waiting for transfers between devices: none -> 51.1 us  [local(): moved = lax.ppermute(hidden, 'row', pairs)]
    all_gather x2 -> x0, waiting for transfers between devices: 37.3 us -> none  [local(): hidden_all = lax.all_gather(hidden, 'row', axis=0, tiled=False)]
    all_gather x2, waiting for transfers between devices: 56 us -> 20.5 us  [local(): rows = lax.all_gather(arrived, 'row', axis=0, tiled=False)]
    ppermute x0 -> x6, starting transfers between devices: none -> 11.1 us  [local(): moved = lax.ppermute(hidden, 'row', pairs)]
    all_to_all x2, starting transfers between devices: 21.4 us -> 11.9 us  [local(): lax.all_to_all(result, 'col', split_axis=0, concat_axis=0, tiled=True)]
    all_to_all x2, waiting for transfers between devices: 26.1 us -> 33.7 us  [local(): lax.all_to_all(result, 'col', split_axis=0, concat_axis=0, tiled=True)]
    ppermute x3, waiting for transfers between devices: 4.2 us -> 0.01 us  [local(): shifted.append(lax.ppermute(meta, 'row', pairs))]
    dot_general x2 -> x8, matrix products: 9.56 us -> 9.97 us  [the longest x6 8.28 us: local(): jnp.dot(moved, down_blocks[step], preferred_element_type=jnp.float32)]
  transfers between devices with their start and end apart: 9 -> 13, of which waited for: 7 -> 6; matrix products, arithmetic and copies ran while one was open for 17% -> 18% of each run, Pallas kernels for 0% -> 0%
where the time goes in v5:
time: 326 us; the launch traced here: 325 us
  waiting for transfers between devices  105 us (32%)
  blocking collectives  104 us (32%)
  matrix products  42.4 us (13%)
  local copies, waits for them, and re-layouts  29.3 us (9%)
  starting transfers between devices  27.7 us (8%)
  between operations  13.7 us (4%)
    all_to_all x2, blocking collectives, local(): lax.all_to_all(outgoing, 'col', split_axis=0, concat_axis=0, tiled=True)  86.7 us
    ppermute x6, waiting for transfers between devices, local(): moved = lax.ppermute(hidden, 'row', pairs)  51.1 us
    all_to_all x2, waiting for transfers between devices, local(): lax.all_to_all(result, 'col', split_axis=0, concat_axis=0, tiled=True)  33.7 us
    all_gather x2, waiting for transfers between devices, local(): rows = lax.all_gather(arrived, 'row', axis=0, tiled=False)  20.5 us
    all_to_all x1, blocking collectives, local(): lax.all_to_all(combined, 'row', split_axis=0, concat_axis=2, tiled=True)  17.6 us
    dot_general x2, matrix products, local(): jnp.einsum('npak,aku->npu', rows, gate_w, preferred_element_type=jnp.floa...  12.3 us
    all_to_all x2, starting transfers between devices, local(): lax.all_to_all(result, 'col', split_axis=0, concat_axis=0, tiled=True)  11.9 us
    ppermute x6, starting transfers between devices, local(): moved = lax.ppermute(hidden, 'row', pairs)  11.1 us
  transfers between devices with their start and end apart: 13, of which 6 were waited for; matrix products, arithmetic and copies ran while one was open for 18% of the time, Pallas kernels for 0%

profile of v5, /device:TPU:4, one launch (start us, length us, event | category | flops | bytes accessed | tf_op | source)
XLA Modules:
  0.0 325.2 jit_solution(14946383032088367577)
XLA Ops:
  6.5 0.9 copy.126
  7.8 0.6 reduce-window.6
  8.9 0.7 fusion.78
  10.0 2.6 convolution_convert_fusion.1
  12.6 2.4 reshape.130
  14.9 40.9 %all_to_all.35 = bf16[64,64,128]{2,1,0:T(8,128)(2,1)} all-to-all(bf16[64,64,128]{2,1,0:T(8,128)(2,1)} %reshape.130), channel_id=1, replica_groups=mesh['row'=4,'col'=64] {'col'}, dimensions={0} | all-to-all | bytes 2097152 | tf_op jit(solution)/shard_map/all_to_all | solution.py:51
  56.0 3.1 collective-permute-start
  59.1 0.6 collective-permute-start.1
  59.7 1.0 collective-permute-start.2
  61.0 2.9 convolution_convert_fusion
  63.9 3.8 %reshape.129 = bf16[64,96,128]{2,1,0:T(8,128)(2,1)} reshape(bf16[192,4096]{1,0:T(8,128)(2,1)} %convolution_convert_fusion) | data formatting | bytes 3145728 | tf_op jit(solution)/shard_map/reshape | solution.py:48
  67.8 45.8 %all_to_all.36 = bf16[64,96,128]{2,1,0:T(8,128)(2,1)} all-to-all(bf16[64,96,128]{2,1,0:T(8,128)(2,1)} %reshape.129), channel_id=1, replica_groups=mesh['row'=4,'col'=64] {'col'}, dimensions={0} | all-to-all | bytes 3145728 | tf_op jit(solution)/shard_map/all_to_all | solution.py:51
  113.7 5.6 %fusion.22 = f32[512,384]{1,0:T(8,128)S(1)} fusion(bf16[32,128,384]{2,1,0:T(8,128)(2,1)} %bitcast.140, bf16[512,32,128]{2,1,0:T(8,128)(2,1)} %bitcast.138), kind=kOutput, calls=%fused_computation.19 | convolution fusion | flops 1610612736 | bytes 8126464 | tf_op jit(solution)/shard_map/npak,aku->npu/dot_general | solution.py:57
  119.3 2.4 fusion.31
  121.7 2.0 collective-permute-start.3
  123.7 1.8 collective-permute-start.4
  125.5 1.3 collective-permute-start.5
  126.8 0.7 fusion.54
  127.5 15.7 %collective-permute-done.3 = bf16[512,384]{1,0:T(8,128)(2,1)} collective-permute-done((bf16[512,384]{1,0:T(8,128)(2,1)S(1)}, bf16[512,384]{1,0:T(8,128)(2,1)}, u32[]{:S(2)}, u32[]{:S(2)}) %collective-permute-start.3) | collective-permute-done | bytes 393248 | tf_op jit(solution)/shard_map/ppermute | solution.py:75
  143.2 1.7 fusion.50
  144.9 13.8 %collective-permute-done.4 = bf16[512,384]{1,0:T(8,128)(2,1)S(1)} collective-permute-done((bf16[512,384]{1,0:T(8,128)(2,1)S(1)}, bf16[512,384]{1,0:T(8,128)(2,1)S(1)}, u32[]{:S(2)}, u32[]{:S(2)}) %collective-permute-start.4) | collective-permute-done | bytes 393248 | tf_op jit(solution)/shard_map/ppermute | solution.py:75
  158.8 0.7 fusion.46
  159.5 1.7 add_convert_fusion.1
  161.2 2.3 reshape.132
  163.5 3.4 %copy.193 = bf16[4,64,2,1024]{3,2,0,1:T(2,128)(2,1)} copy(bf16[4,64,2,1024]{3,2,1,0:T(2,128)(2,1)} %reshape.132) | data formatting | bytes 2097152 | tf_op jit(solution)/shard_map/reshape | solution.py:78
  166.9 5.6 %all-to-all-start.1 = ((bf16[64,4,2,1024]{3,2,1,0:T(2,128)(2,1)}), bf16[64,4,2,1024]{3,2,1,0:T(2,128)(2,1)}, u32[]{:S(2)}, u32[]{:S(2)}) async-start(bf16[64,4,2,1024]{3,2,1,0:T(2,128)(2,1)} %bitcast.123), calls=%async_computation.1 | async-start | bytes 2097152 | tf_op jit(solution)/shard_map/all_to_all | solution.py:79
  172.4 20.5 %all-gather.7.cloned.1.call-done = bf16[256,96,128]{2,1,0:T(8,128)(2,1)} async-done(((bf16[64,96,128]{2,1,0:T(8,128)(2,1)}), bf16[256,96,128]{2,1,0:T(8,128)(2,1)}) %all-gather.7.cloned.1.call-update) | async-done | bytes 6291472 | tf_op jit(solution)/shard_map/all_gather | solution.py:53
  192.9 6.7 %fusion.10 = f32[768,384]{1,0:T(8,128)S(1)} fusion(bf16[32,128,384]{2,1,0:T(8,128)(2,1)} %bitcast.141, bf16[768,32,128]{2,1,0:T(8,128)(2,1)} %bitcast.136), kind=kOutput, calls=%fused_computation.15 | convolution fusion | flops 2415919104 | bytes 10616832 | tf_op jit(solution)/shard_map/npak,aku->npu/dot_general | solution.py:57
  199.7 3.6 %fusion.19 = bf16[768,384]{1,0:T(8,128)(2,1)S(1)} fusion(bf16[32,128,384]{2,1,0:T(8,128)(2,1)S(1)} %bitcast.143, bf16[768,32,128]{2,1,0:T(8,128)(2,1)S(1)} %bitcast.137, f32[768,384]{1,0:T(8,128)S(1)} %fusion.10), kind=kOutput, calls=%fused_computation.18 | convolution fusion | flops 2417688576 | bytes 11206656 | tf_op jit(solution)/shard_map/npak,aku->npu/dot_general | solution.py:58
  203.2 2.8 collective-permute-start.7
  206.0 0.9 collective-permute-start.6
  206.9 2.4 collective-permute-start.8
  209.3 1.0 fusion.52
  210.2 10.8 %collective-permute-done.7 = bf16[768,384]{1,0:T(8,128)(2,1)S(1)} collective-permute-done((bf16[768,384]{1,0:T(8,128)(2,1)S(1)}, bf16[768,384]{1,0:T(8,128)(2,1)S(1)}, u32[]{:S(2)}, u32[]{:S(2)}) %collective-permute-start.7) | collective-permute-done | bytes 589856 | tf_op jit(solution)/shard_map/ppermute | solution.py:75
  221.1 1.0 fusion.44
  222.0 10.7 %collective-permute-done.6 = bf16[768,384]{1,0:T(8,128)(2,1)S(1)} collective-permute-done((bf16[768,384]{1,0:T(8,128)(2,1)S(1)}, bf16[768,384]{1,0:T(8,128)(2,1)S(1)}, u32[]{:S(2)}, u32[]{:S(2)}) %collective-permute-start.6) | collective-permute-done | bytes 589856 | tf_op jit(solution)/shard_map/ppermute | solution.py:75
  232.7 1.0 fusion.48
  233.7 2.2 add_convert_fusion
  235.9 5.1 %reshape.134 = bf16[4,64,3,1024]{3,2,1,0:T(4,128)(2,1)} reshape(bf16[768,1024]{1,0:T(8,128)(2,1)} %add_convert_fusion) | data formatting | bytes 3145728 | tf_op jit(solution)/shard_map/reshape | solution.py:78
  241.1 4.8 %copy.151 = bf16[64,4,3,1024]{3,1,2,0:T(4,128)(2,1)} copy(bf16[64,4,3,1024]{3,2,0,1:T(4,128)(2,1)} %bitcast.122) | data formatting | bytes 3145728 | tf_op jit(solution)/shard_map/transpose | solution.py:78
  245.8 6.4 %all-to-all-start.3 = ((bf16[64,4,3,1024]{3,1,2,0:T(4,128)(2,1)}), bf16[64,4,3,1024]{3,1,2,0:T(4,128)(2,1)}, u32[]{:S(2)}, u32[]{:S(2)}) async-start(bf16[64,4,3,1024]{3,1,2,0:T(4,128)(2,1)} %copy.151), calls=%async_computation.3 | async-start | bytes 3145728 | tf_op jit(solution)/shard_map/all_to_all | solution.py:79
  252.6 0.8 copy.140
  253.9 4.7 %fusion.34 = f32[4,128,1024,1]{2,1,3,0:T(8,128)} fusion(bf16[64,4,2,1024]{3,2,1,0:T(2,128)(2,1)} %all-to-all-done.1, f32[4,128,64,2]{1,3,2,0:T(2,128)} %bitcast.127), kind=kOutput, calls=%fused_computation.23 | convolution fusion | flops 805306368 | bytes 3407872 | tf_op jit(solution)/shard_map/rtep,erpf->rtf/dot_general | solution.py:83
  258.5 33.7 %all-to-all-done.3 = bf16[64,4,3,1024]{3,1,2,0:T(4,128)(2,1)} async-done(((bf16[64,4,3,1024]{3,1,2,0:T(4,128)(2,1)}), bf16[64,4,3,1024]{3,1,2,0:T(4,128)(2,1)}, u32[]{:S(2)}, u32[]{:S(2)}) %all-to-all-start.3) | async-done | bytes 1572896 | tf_op jit(solution)/shard_map/all_to_all | solution.py:79
  292.2 3.9 %fusion.8 = bf16[4,128,1024]{2,1,0:T(8,128)(2,1)S(1)} fusion(f32[4,128,1024,1]{2,1,3,0:T(8,128)} %fusion.34, bf16[64,4,3,1024]{3,1,2,0:T(4,128)(2,1)} %all-to-all-done.3, f32[4,128,64,3]{1,0,3,2:T(4,128)S(1)} %bitcast.126), kind=kOutput, calls=%fused_computation.12 | convolution fusion | flops 1209008128 | bytes 5111808 | tf_op jit(solution)/shard_map/rtep,erpf->rtf/dot_general | solution.py:83
  296.1 17.6 %all_to_all.37 = bf16[4,128,1024]{2,1,0:T(8,128)(2,1)} all-to-all(bf16[4,128,1024]{2,1,0:T(8,128)(2,1)S(1)} %fusion.8), channel_id=1, replica_groups=mesh['row'=4,'col'=64] {'row'}, dimensions={0} | all-to-all | bytes 2097152 | tf_op jit(solution)/shard_map/all_to_all | solution.py:88
  313.8 2.3 copy.154
  316.1 2.3 copy.155
  (53 shorter events, 2.4 us)
Async XLA Ops:
  6.5 120.2 %copy-start = (bf16[1,1536,1024]{2,1,0:T(8,128)(2,1)S(1)}, bf16[1,1536,1024]{2,1,0:T(8,128)(2,1)}, u32[]{:S(2)}) copy-start(bf16[1,1536,1024]{2,1,0:T(8,128)(2,1)} %param.11) | copy-start | bytes 9437188
  6.5 107.1 %all-gather.5.cloned.1.call-start = ((), (), s32[]{:S(2)}) async-start(), calls=%async_computation.5 | async-start | bytes 5242880 | tf_op jit(solution)/shard_map/all_gather | solution.py:53
  12.6 43.3 %copy-start.1 = (f32[128,2]{0,1:T(2,128)S(1)}, f32[128,2]{0,1:T(2,128)}, u32[]{:S(2)}) copy-start(f32[128,2]{0,1:T(2,128)} %param.8) | copy-start | bytes 3076
  55.9 137.1 %all-gather.7.cloned.1.call-start = ((), (), s32[]{:S(2)}) async-start(), calls=%async_computation.6 | async-start | bytes 7864320 | tf_op jit(solution)/shard_map/all_gather | solution.py:53
  56.0 11.8 %collective-permute-start = (f32[128,4]{0,1:T(4,128)S(1)}, f32[128,4]{0,1:T(4,128)S(1)}, u32[]{:S(2)}, u32[]{:S(2)}) collective-permute-start(f32[128,4]{0,1:T(4,128)S(1)} %pad_maximum_fusion), channel_id=1, source_target_pairs={{0,192},{64,0},{128,64},{192,128},{1,193},{65,1},{129,65},{193,129... | collective-permute-start | bytes 6152 | tf_op jit(solution)/shard_map/ppermute | solution.py:30
  59.1 8.7 %collective-permute-start.1 = (f32[128,4]{0,1:T(4,128)S(1)}, f32[128,4]{0,1:T(4,128)S(1)}, u32[]{:S(2)}, u32[]{:S(2)}) collective-permute-start(f32[128,4]{0,1:T(4,128)S(1)} %pad_maximum_fusion), channel_id=1, source_target_pairs={{0,128},{64,192},{128,0},{192,64},{1,129},{65,193},{129,1},{193,65... | collective-permute-start | bytes 6152 | tf_op jit(solution)/shard_map/ppermute | solution.py:30
  59.7 8.1 %collective-permute-start.2 = (f32[128,4]{0,1:T(4,128)S(1)}, f32[128,4]{0,1:T(4,128)S(1)}, u32[]{:S(2)}, u32[]{:S(2)}) collective-permute-start(f32[128,4]{0,1:T(4,128)S(1)} %pad_maximum_fusion), channel_id=1, source_target_pairs={{0,64},{64,128},{128,192},{192,0},{1,65},{65,129},{129,193},{193,1... | collective-permute-start | bytes 6152 | tf_op jit(solution)/shard_map/ppermute | solution.py:30
  113.7 5.7 %copy-start.3 = (bf16[256,64,128]{2,1,0:T(8,128)(2,1)S(1)}, bf16[256,64,128]{2,1,0:T(8,128)(2,1)}, u32[]{:S(2)}) copy-start(bf16[256,64,128]{2,1,0:T(8,128)(2,1)} %all-gather.5.cloned.1.call-done) | copy-start | bytes 12582916
  113.7 5.7 %copy-start.4 = (bf16[1,4096,384]{2,1,0:T(8,128)(2,1)S(1)}, bf16[1,4096,384]{2,1,0:T(8,128)(2,1)}, u32[]{:S(2)}) copy-start(bf16[1,4096,384]{2,1,0:T(8,128)(2,1)} %param.10) | copy-start | bytes 9437188
  121.7 21.5 %collective-permute-start.3 = (bf16[512,384]{1,0:T(8,128)(2,1)S(1)}, bf16[512,384]{1,0:T(8,128)(2,1)}, u32[]{:S(2)}, u32[]{:S(2)}) collective-permute-start(bf16[512,384]{1,0:T(8,128)(2,1)S(1)} %fusion.31), channel_id=1, source_target_pairs={{0,64},{64,128},{128,192},{192,0},{1,65},{65,129},{129,193},{193,1... | collective-permute-start | bytes 1179656 | tf_op jit(solution)/shard_map/ppermute | solution.py:75
  123.7 35.0 %collective-permute-start.4 = (bf16[512,384]{1,0:T(8,128)(2,1)S(1)}, bf16[512,384]{1,0:T(8,128)(2,1)S(1)}, u32[]{:S(2)}, u32[]{:S(2)}) collective-permute-start(bf16[512,384]{1,0:T(8,128)(2,1)S(1)} %fusion.31), channel_id=1, source_target_pairs={{0,128},{64,192},{128,0},{192,64},{1,129},{65,193},{129,1},{193,65... | collective-permute-start | bytes 1179656 | tf_op jit(solution)/shard_map/ppermute | solution.py:75
  125.5 34.0 %collective-permute-start.5 = (bf16[512,384]{1,0:T(8,128)(2,1)S(1)}, bf16[512,384]{1,0:T(8,128)(2,1)S(1)}, u32[]{:S(2)}, u32[]{:S(2)}) collective-permute-start(bf16[512,384]{1,0:T(8,128)(2,1)S(1)} %fusion.31), channel_id=1, source_target_pairs={{0,192},{64,0},{128,64},{192,128},{1,193},{65,1},{129,65},{193,129... | collective-permute-start | bytes 1179656 | tf_op jit(solution)/shard_map/ppermute | solution.py:75
  166.9 79.0 %all-to-all-start.1 = ((bf16[64,4,2,1024]{3,2,1,0:T(2,128)(2,1)}), bf16[64,4,2,1024]{3,2,1,0:T(2,128)(2,1)}, u32[]{:S(2)}, u32[]{:S(2)}) async-start(bf16[64,4,2,1024]{3,2,1,0:T(2,128)(2,1)} %bitcast.123), calls=%async_computation.1 | async-start | bytes 2097152 | tf_op jit(solution)/shard_map/all_to_all | solution.py:79
  192.9 6.7 %copy-start.2 = (bf16[256,96,128]{2,1,0:T(8,128)(2,1)S(1)}, bf16[256,96,128]{2,1,0:T(8,128)(2,1)}, u32[]{:S(2)}) copy-start(bf16[256,96,128]{2,1,0:T(8,128)(2,1)} %all-gather.7.cloned.1.call-done) | copy-start | bytes 18874372
  192.9 6.7 %copy-start.5 = (bf16[1,4096,384]{2,1,0:T(8,128)(2,1)S(1)}, bf16[1,4096,384]{2,1,0:T(8,128)(2,1)}, u32[]{:S(2)}) copy-start(bf16[1,4096,384]{2,1,0:T(8,128)(2,1)} %param.10) | copy-start | bytes 9437188
  203.2 17.8 %collective-permute-start.7 = (bf16[768,384]{1,0:T(8,128)(2,1)S(1)}, bf16[768,384]{1,0:T(8,128)(2,1)S(1)}, u32[]{:S(2)}, u32[]{:S(2)}) collective-permute-start(bf16[768,384]{1,0:T(8,128)(2,1)S(1)} %fusion.19), channel_id=1, source_target_pairs={{0,128},{64,192},{128,0},{192,64},{1,129},{65,193},{129,1},{193,65... | collective-permute-start | bytes 1769480 | tf_op jit(solution)/shard_map/ppermute | solution.py:75
  206.0 26.7 %collective-permute-start.6 = (bf16[768,384]{1,0:T(8,128)(2,1)S(1)}, bf16[768,384]{1,0:T(8,128)(2,1)S(1)}, u32[]{:S(2)}, u32[]{:S(2)}) collective-permute-start(bf16[768,384]{1,0:T(8,128)(2,1)S(1)} %fusion.19), channel_id=1, source_target_pairs={{0,64},{64,128},{128,192},{192,0},{1,65},{65,129},{129,193},{193,1... | collective-permute-start | bytes 1769480 | tf_op jit(solution)/shard_map/ppermute | solution.py:75
  206.9 26.9 %collective-permute-start.8 = (bf16[768,384]{1,0:T(8,128)(2,1)S(1)}, bf16[768,384]{1,0:T(8,128)(2,1)S(1)}, u32[]{:S(2)}, u32[]{:S(2)}) collective-permute-start(bf16[768,384]{1,0:T(8,128)(2,1)S(1)} %fusion.19), channel_id=1, source_target_pairs={{0,192},{64,0},{128,64},{192,128},{1,193},{65,1},{129,65},{193,129... | collective-permute-start | bytes 1769480 | tf_op jit(solution)/shard_map/ppermute | solution.py:75
  245.8 46.4 %all-to-all-start.3 = ((bf16[64,4,3,1024]{3,1,2,0:T(4,128)(2,1)}), bf16[64,4,3,1024]{3,1,2,0:T(4,128)(2,1)}, u32[]{:S(2)}, u32[]{:S(2)}) async-start(bf16[64,4,3,1024]{3,1,2,0:T(4,128)(2,1)} %copy.151), calls=%async_computation.3 | async-start | bytes 3145728 | tf_op jit(solution)/shard_map/all_to_all | solution.py:79
Sparse Core Ops, SparseCore 0:
  56.0 47.4 all-gather.4
  113.8 79.1 all-gather.6

commit v6 on v5

--- a/solution.py
+++ b/solution.py
@@ -3,7 +3,7 @@
 from jax import lax
 from jax.sharding import PartitionSpec as P
 
-CHUNKS = ((0, 2), (2, 5))
+CHUNKS = ((0, 3), (3, 5))
 
 
 def local(tokens, expert_ids, gate_weights, w_gate, w_up, w_down):

time: 326 us -> 332 us (1.018)
  starting transfers between devices: 27.7 us -> 33.8 us
  waiting for transfers between devices: 105 us -> 101 us
    all_to_all x2, waiting for transfers between devices: 33.7 us -> 23.5 us  [local(): lax.all_to_all(result, 'col', split_axis=0, concat_axis=0, tiled=True)]
    all_to_all x2, starting transfers between devices: 11.9 us -> 18.7 us  [local(): lax.all_to_all(result, 'col', split_axis=0, concat_axis=0, tiled=True)]
    ppermute x6, waiting for transfers between devices: 51.1 us -> 57.6 us  [local(): moved = lax.ppermute(hidden, 'row', pairs)]
  transfers between devices with their start and end apart: 13 -> 13, of which waited for: 6 -> 8; matrix products, arithmetic and copies ran while one was open for 18% -> 18% of each run, Pallas kernels for 0% -> 0%
where the time goes in v6:
time: 332 us; the launch traced here: 331 us
  blocking collectives  104 us (31%)
  waiting for transfers between devices  101 us (30%)
  matrix products  44.4 us (13%)
  starting transfers between devices  33.8 us (10%)
  local copies, waits for them, and re-layouts  30.3 us (9%)
  between operations  13.7 us (4%)
    all_to_all x2, blocking collectives, local(): lax.all_to_all(outgoing, 'col', split_axis=0, concat_axis=0, tiled=True)  86.6 us
    ppermute x6, waiting for transfers between devices, local(): moved = lax.ppermute(hidden, 'row', pairs)  57.6 us
    all_to_all x2, waiting for transfers between devices, local(): lax.all_to_all(result, 'col', split_axis=0, concat_axis=0, tiled=True)  23.5 us
    all_gather x2, waiting for transfers between devices, local(): rows = lax.all_gather(arrived, 'row', axis=0, tiled=False)  20.2 us
    all_to_all x2, starting transfers between devices, local(): lax.all_to_all(result, 'col', split_axis=0, concat_axis=0, tiled=True)  18.7 us
    all_to_all x1, blocking collectives, local(): lax.all_to_all(combined, 'row', split_axis=0, concat_axis=2, tiled=True)  17.5 us
    dot_general x2, matrix products, local(): jnp.einsum('npak,aku->npu', rows, gate_w, preferred_element_type=jnp.floa...  12.2 us
    reshape x3, local copies, waits for them, and re-layouts, local(): result.reshape(groups, columns, span, quarter).transpose(1, 0, 2, 3)  10.8 us
  transfers between devices with their start and end apart: 13, of which 8 were waited for; matrix products, arithmetic and copies ran while one was open for 18% of the time, Pallas kernels for 0%

profile of v6, /device:TPU:4, one launch (start us, length us, event | category | flops | bytes accessed | tf_op | source)
XLA Modules:
  0.0 330.6 jit_solution(18020959278062507200)
XLA Ops:
  6.5 0.9 copy.126
  8.9 0.7 fusion.78
  10.0 2.9 convolution_convert_fusion
  12.9 3.8 %reshape.130 = bf16[64,96,128]{2,1,0:T(8,128)(2,1)} reshape(bf16[192,4096]{1,0:T(8,128)(2,1)} %convolution_convert_fusion) | data formatting | bytes 3145728 | tf_op jit(solution)/shard_map/reshape | solution.py:48
  16.7 52.3 %all_to_all.35 = bf16[64,96,128]{2,1,0:T(8,128)(2,1)} all-to-all(bf16[64,96,128]{2,1,0:T(8,128)(2,1)} %reshape.130), channel_id=1, replica_groups=mesh['row'=4,'col'=64] {'col'}, dimensions={0} | all-to-all | bytes 3145728 | tf_op jit(solution)/shard_map/all_to_all | solution.py:51
  69.1 3.1 collective-permute-start
  72.8 1.0 collective-permute-start.2
  74.1 2.6 convolution_convert_fusion.1
  76.7 2.4 reshape.129
  79.2 34.3 %all_to_all.36 = bf16[64,64,128]{2,1,0:T(8,128)(2,1)} all-to-all(bf16[64,64,128]{2,1,0:T(8,128)(2,1)} %reshape.129), channel_id=1, replica_groups=mesh['row'=4,'col'=64] {'col'}, dimensions={0} | all-to-all | bytes 2097152 | tf_op jit(solution)/shard_map/all_to_all | solution.py:51
  113.6 20.2 %all-gather.5.cloned.1.call-done = bf16[256,96,128]{2,1,0:T(8,128)(2,1)} async-done(((bf16[64,96,128]{2,1,0:T(8,128)(2,1)}), bf16[256,96,128]{2,1,0:T(8,128)(2,1)}) %all-gather.5.cloned.1.call-update) | async-done | bytes 6291472 | tf_op jit(solution)/shard_map/all_gather | solution.py:53
  133.8 6.7 %fusion.11 = f32[768,384]{1,0:T(8,128)S(1)} fusion(bf16[32,128,384]{2,1,0:T(8,128)(2,1)} %bitcast.140, bf16[768,32,128]{2,1,0:T(8,128)(2,1)} %bitcast.136), kind=kOutput, calls=%fused_computation.16 | convolution fusion | flops 2415919104 | bytes 10616832 | tf_op jit(solution)/shard_map/npak,aku->npu/dot_general | solution.py:57
  140.5 4.4 %fusion.20 = bf16[768,384]{1,0:T(8,128)(2,1)} fusion(bf16[32,128,384]{2,1,0:T(8,128)(2,1)S(1)} %bitcast.142, bf16[768,32,128]{2,1,0:T(8,128)(2,1)S(1)} %bitcast.137, f32[768,384]{1,0:T(8,128)S(1)} %fusion.11), kind=kOutput, calls=%fused_computation.19 | convolution fusion | flops 2417688576 | bytes 11206656 | tf_op jit(solution)/shard_map/npak,aku->npu/dot_general | solution.py:58
  144.9 1.2 collective-permute-start.3
  146.0 1.7 collective-permute-start.4
  147.8 2.1 collective-permute-start.5
  149.9 2.1 fusion.54
  152.0 21.0 %collective-permute-done.3 = bf16[768,384]{1,0:T(8,128)(2,1)} collective-permute-done((bf16[768,384]{1,0:T(8,128)(2,1)}, bf16[768,384]{1,0:T(8,128)(2,1)}, u32[]{:S(2)}, u32[]{:S(2)}) %collective-permute-start.3) | collective-permute-done | bytes 589856 | tf_op jit(solution)/shard_map/ppermute | solution.py:75
  173.0 2.0 fusion.50
  175.1 20.0 %collective-permute-done.4 = bf16[768,384]{1,0:T(8,128)(2,1)S(1)} collective-permute-done((bf16[768,384]{1,0:T(8,128)(2,1)}, bf16[768,384]{1,0:T(8,128)(2,1)S(1)}, u32[]{:S(2)}, u32[]{:S(2)}) %collective-permute-start.4) | collective-permute-done | bytes 589856 | tf_op jit(solution)/shard_map/ppermute | solution.py:75
  195.1 1.0 fusion.46
  196.0 2.2 collective-permute-done.5
  198.2 2.2 add_convert_fusion
  200.4 5.1 %reshape.132 = bf16[4,64,3,1024]{3,2,1,0:T(4,128)(2,1)} reshape(bf16[768,1024]{1,0:T(8,128)(2,1)} %add_convert_fusion) | data formatting | bytes 3145728 | tf_op jit(solution)/shard_map/reshape | solution.py:78
  205.5 4.8 %copy.143 = bf16[64,4,3,1024]{3,1,2,0:T(4,128)(2,1)} copy(bf16[64,4,3,1024]{3,2,0,1:T(4,128)(2,1)} %bitcast.122) | data formatting | bytes 3145728 | tf_op jit(solution)/shard_map/transpose | solution.py:78
  210.3 10.8 %all-to-all-start.1 = ((bf16[64,4,3,1024]{3,1,2,0:T(4,128)(2,1)}), bf16[64,4,3,1024]{3,1,2,0:T(4,128)(2,1)}, u32[]{:S(2)}, u32[]{:S(2)}) async-start(bf16[64,4,3,1024]{3,1,2,0:T(4,128)(2,1)} %copy.143), calls=%async_computation.1 | async-start | bytes 3145728 | tf_op jit(solution)/shard_map/all_to_all | solution.py:79
  221.2 5.5 %fusion.23 = f32[512,384]{1,0:T(8,128)S(1)} fusion(bf16[32,128,384]{2,1,0:T(8,128)(2,1)} %bitcast.141, bf16[512,32,128]{2,1,0:T(8,128)(2,1)} %bitcast.138), kind=kOutput, calls=%fused_computation.20 | convolution fusion | flops 1610612736 | bytes 8126464 | tf_op jit(solution)/shard_map/npak,aku->npu/dot_general | solution.py:57
  226.8 2.5 fusion.32
  229.3 2.0 collective-permute-start.7
  231.3 0.7 fusion.52
  232.0 3.3 %collective-permute-start.8 = (bf16[512,384]{1,0:T(8,128)(2,1)S(1)}, bf16[512,384]{1,0:T(8,128)(2,1)S(1)}, u32[]{:S(2)}, u32[]{:S(2)}) collective-permute-start(bf16[512,384]{1,0:T(8,128)(2,1)S(1)} %fusion.32), channel_id=1, source_target_pairs={{0,192},{64,0},{128,64},{192,128},{1,193},{65,1},{129,65},{193,129... | collective-permute-start | bytes 1179656 | tf_op jit(solution)/shard_map/ppermute | solution.py:75
  235.3 7.5 %collective-permute-done.7 = bf16[512,384]{1,0:T(8,128)(2,1)S(1)} collective-permute-done((bf16[512,384]{1,0:T(8,128)(2,1)S(1)}, bf16[512,384]{1,0:T(8,128)(2,1)S(1)}, u32[]{:S(2)}, u32[]{:S(2)}) %collective-permute-start.7) | collective-permute-done | bytes 393248 | tf_op jit(solution)/shard_map/ppermute | solution.py:75
  242.9 0.7 fusion.44
  243.6 6.9 %collective-permute-done.6 = bf16[512,384]{1,0:T(8,128)(2,1)S(1)} collective-permute-done((bf16[512,384]{1,0:T(8,128)(2,1)S(1)}, bf16[512,384]{1,0:T(8,128)(2,1)S(1)}, u32[]{:S(2)}, u32[]{:S(2)}) %collective-permute-start.6) | collective-permute-done | bytes 393248 | tf_op jit(solution)/shard_map/ppermute | solution.py:75
  250.5 0.7 fusion.48
  251.2 1.7 add_convert_fusion.1
  252.9 2.3 reshape.134
  255.2 3.4 %copy.193 = bf16[4,64,2,1024]{3,2,0,1:T(2,128)(2,1)} copy(bf16[4,64,2,1024]{3,2,1,0:T(2,128)(2,1)} %reshape.134) | data formatting | bytes 2097152 | tf_op jit(solution)/shard_map/reshape | solution.py:78
  258.5 2.6 all-to-all-done.1
  261.1 7.9 %all-to-all-start.3 = ((bf16[64,4,2,1024]{3,2,1,0:T(2,128)(2,1)}), bf16[64,4,2,1024]{3,2,1,0:T(2,128)(2,1)}, u32[]{:S(2)}, u32[]{:S(2)}) async-start(bf16[64,4,2,1024]{3,2,1,0:T(2,128)(2,1)} %bitcast.123), calls=%async_computation.3 | async-start | bytes 2097152 | tf_op jit(solution)/shard_map/all_to_all | solution.py:79
  269.5 1.0 select_reduce_fusion.1
  270.5 1.8 copy.148
  272.3 4.5 %fusion.9 = f32[4,128,1024,1]{2,1,3,0:T(8,128)} fusion(bf16[64,4,3,1024]{3,1,2,0:T(4,128)(2,1)} %all-to-all-done.1, f32[4,128,64,3]{1,0,3,2:T(4,128)S(1)} %bitcast.126), kind=kOutput, calls=%fused_computation.14 | convolution fusion | flops 1207959552 | bytes 4063232 | tf_op jit(solution)/shard_map/rtep,erpf->rtf/dot_general | solution.py:83
  276.9 20.9 %all-to-all-done.3 = bf16[64,4,2,1024]{3,2,1,0:T(2,128)(2,1)} async-done(((bf16[64,4,2,1024]{3,2,1,0:T(2,128)(2,1)}), bf16[64,4,2,1024]{3,2,1,0:T(2,128)(2,1)}, u32[]{:S(2)}, u32[]{:S(2)}) %all-to-all-start.3) | async-done | bytes 1048608 | tf_op jit(solution)/shard_map/all_to_all | solution.py:79
  297.8 4.0 %fusion.8 = bf16[4,128,1024]{2,1,0:T(8,128)(2,1)S(1)} fusion(f32[4,128,1024,1]{2,1,3,0:T(8,128)} %fusion.9, bf16[64,4,2,1024]{3,2,1,0:T(2,128)(2,1)} %all-to-all-done.3, f32[4,128,64,2]{1,3,2,0:T(2,128)} %bitcast.127), kind=kOutput, calls=%fused_computation.12 | convolution fusion | flops 806354944 | bytes 4456448 | tf_op jit(solution)/shard_map/rtep,erpf->rtf/dot_general | solution.py:83
  301.8 17.5 %all_to_all.37 = bf16[4,128,1024]{2,1,0:T(8,128)(2,1)} all-to-all(bf16[4,128,1024]{2,1,0:T(8,128)(2,1)S(1)} %fusion.8), channel_id=1, replica_groups=mesh['row'=4,'col'=64] {'row'}, dimensions={0} | all-to-all | bytes 2097152 | tf_op jit(solution)/shard_map/all_to_all | solution.py:88
  319.2 2.3 copy.154
  321.5 2.3 copy.155
  (53 shorter events, 3.3 us)
Async XLA Ops:
  6.5 143.4 %copy-start = (bf16[1,1536,1024]{2,1,0:T(8,128)(2,1)S(1)}, bf16[1,1536,1024]{2,1,0:T(8,128)(2,1)}, u32[]{:S(2)}) copy-start(bf16[1,1536,1024]{2,1,0:T(8,128)(2,1)} %param.11) | copy-start | bytes 9437188
  6.5 127.2 %all-gather.5.cloned.1.call-start = ((), (), s32[]{:S(2)}) async-start(), calls=%async_computation.5 | async-start | bytes 7864320 | tf_op jit(solution)/shard_map/all_gather | solution.py:53
  16.7 52.3 %copy-start.1 = (f32[128,2]{0,1:T(2,128)S(1)}, f32[128,2]{0,1:T(2,128)}, u32[]{:S(2)}) copy-start(f32[128,2]{0,1:T(2,128)} %param.8) | copy-start | bytes 3076
  69.0 152.2 %all-gather.7.cloned.1.call-start = ((), (), s32[]{:S(2)}) async-start(), calls=%async_computation.6 | async-start | bytes 5242880 | tf_op jit(solution)/shard_map/all_gather | solution.py:53
  69.1 10.1 %collective-permute-start = (f32[128,4]{0,1:T(4,128)S(1)}, f32[128,4]{0,1:T(4,128)S(1)}, u32[]{:S(2)}, u32[]{:S(2)}) collective-permute-start(f32[128,4]{0,1:T(4,128)S(1)} %pad_maximum_fusion), channel_id=1, source_target_pairs={{0,192},{64,0},{128,64},{192,128},{1,193},{65,1},{129,65},{193,129... | collective-permute-start | bytes 6152 | tf_op jit(solution)/shard_map/ppermute | solution.py:30
  72.2 7.0 %collective-permute-start.1 = (f32[128,4]{0,1:T(4,128)S(1)}, f32[128,4]{0,1:T(4,128)S(1)}, u32[]{:S(2)}, u32[]{:S(2)}) collective-permute-start(f32[128,4]{0,1:T(4,128)S(1)} %pad_maximum_fusion), channel_id=1, source_target_pairs={{0,128},{64,192},{128,0},{192,64},{1,129},{65,193},{129,1},{193,65... | collective-permute-start | bytes 6152 | tf_op jit(solution)/shard_map/ppermute | solution.py:30
  72.8 6.3 %collective-permute-start.2 = (f32[128,4]{0,1:T(4,128)S(1)}, f32[128,4]{0,1:T(4,128)S(1)}, u32[]{:S(2)}, u32[]{:S(2)}) collective-permute-start(f32[128,4]{0,1:T(4,128)S(1)} %pad_maximum_fusion), channel_id=1, source_target_pairs={{0,64},{64,128},{128,192},{192,0},{1,65},{65,129},{129,193},{193,1... | collective-permute-start | bytes 6152 | tf_op jit(solution)/shard_map/ppermute | solution.py:30
  133.8 6.7 %copy-start.2 = (bf16[256,96,128]{2,1,0:T(8,128)(2,1)S(1)}, bf16[256,96,128]{2,1,0:T(8,128)(2,1)}, u32[]{:S(2)}) copy-start(bf16[256,96,128]{2,1,0:T(8,128)(2,1)} %all-gather.5.cloned.1.call-done) | copy-start | bytes 18874372
  133.8 6.7 %copy-start.4 = (bf16[1,4096,384]{2,1,0:T(8,128)(2,1)S(1)}, bf16[1,4096,384]{2,1,0:T(8,128)(2,1)}, u32[]{:S(2)}) copy-start(bf16[1,4096,384]{2,1,0:T(8,128)(2,1)} %param.10) | copy-start | bytes 9437188
  144.9 28.1 %collective-permute-start.3 = (bf16[768,384]{1,0:T(8,128)(2,1)}, bf16[768,384]{1,0:T(8,128)(2,1)}, u32[]{:S(2)}, u32[]{:S(2)}) collective-permute-start(bf16[768,384]{1,0:T(8,128)(2,1)} %fusion.20), channel_id=1, source_target_pairs={{0,64},{64,128},{128,192},{192,0},{1,65},{65,129},{129,193},{193,1... | collective-permute-start | bytes 1769480 | tf_op jit(solution)/shard_map/ppermute | solution.py:75
  146.0 49.0 %collective-permute-start.4 = (bf16[768,384]{1,0:T(8,128)(2,1)}, bf16[768,384]{1,0:T(8,128)(2,1)S(1)}, u32[]{:S(2)}, u32[]{:S(2)}) collective-permute-start(bf16[768,384]{1,0:T(8,128)(2,1)} %fusion.20), channel_id=1, source_target_pairs={{0,128},{64,192},{128,0},{192,64},{1,129},{65,193},{129,1},{193,65... | collective-permute-start | bytes 1769480 | tf_op jit(solution)/shard_map/ppermute | solution.py:75
  147.8 50.5 %collective-permute-start.5 = (bf16[768,384]{1,0:T(8,128)(2,1)}, bf16[768,384]{1,0:T(8,128)(2,1)S(1)}, u32[]{:S(2)}, u32[]{:S(2)}) collective-permute-start(bf16[768,384]{1,0:T(8,128)(2,1)} %fusion.20), channel_id=1, source_target_pairs={{0,192},{64,0},{128,64},{192,128},{1,193},{65,1},{129,65},{193,129... | collective-permute-start | bytes 1769480 | tf_op jit(solution)/shard_map/ppermute | solution.py:75
  210.3 50.8 %all-to-all-start.1 = ((bf16[64,4,3,1024]{3,1,2,0:T(4,128)(2,1)}), bf16[64,4,3,1024]{3,1,2,0:T(4,128)(2,1)}, u32[]{:S(2)}, u32[]{:S(2)}) async-start(bf16[64,4,3,1024]{3,1,2,0:T(4,128)(2,1)} %copy.143), calls=%async_computation.1 | async-start | bytes 3145728 | tf_op jit(solution)/shard_map/all_to_all | solution.py:79
  221.2 5.6 %copy-start.3 = (bf16[256,64,128]{2,1,0:T(8,128)(2,1)S(1)}, bf16[256,64,128]{2,1,0:T(8,128)(2,1)}, u32[]{:S(2)}) copy-start(bf16[256,64,128]{2,1,0:T(8,128)(2,1)} %all-gather.7.cloned.1.call-done) | copy-start | bytes 12582916
  221.2 5.6 %copy-start.5 = (bf16[1,4096,384]{2,1,0:T(8,128)(2,1)S(1)}, bf16[1,4096,384]{2,1,0:T(8,128)(2,1)}, u32[]{:S(2)}) copy-start(bf16[1,4096,384]{2,1,0:T(8,128)(2,1)} %param.10) | copy-start | bytes 9437188
  229.3 13.6 %collective-permute-start.7 = (bf16[512,384]{1,0:T(8,128)(2,1)S(1)}, bf16[512,384]{1,0:T(8,128)(2,1)S(1)}, u32[]{:S(2)}, u32[]{:S(2)}) collective-permute-start(bf16[512,384]{1,0:T(8,128)(2,1)S(1)} %fusion.32), channel_id=1, source_target_pairs={{0,128},{64,192},{128,0},{192,64},{1,129},{65,193},{129,1},{193,65... | collective-permute-start | bytes 1179656 | tf_op jit(solution)/shard_map/ppermute | solution.py:75
  231.3 19.1 %collective-permute-start.6 = (bf16[512,384]{1,0:T(8,128)(2,1)S(1)}, bf16[512,384]{1,0:T(8,128)(2,1)S(1)}, u32[]{:S(2)}, u32[]{:S(2)}) collective-permute-start(bf16[512,384]{1,0:T(8,128)(2,1)S(1)} %fusion.32), channel_id=1, source_target_pairs={{0,64},{64,128},{128,192},{192,0},{1,65},{65,129},{129,193},{193,1... | collective-permute-start | bytes 1179656 | tf_op jit(solution)/shard_map/ppermute | solution.py:75
  232.0 19.1 %collective-permute-start.8 = (bf16[512,384]{1,0:T(8,128)(2,1)S(1)}, bf16[512,384]{1,0:T(8,128)(2,1)S(1)}, u32[]{:S(2)}, u32[]{:S(2)}) collective-permute-start(bf16[512,384]{1,0:T(8,128)(2,1)S(1)} %fusion.32), channel_id=1, source_target_pairs={{0,192},{64,0},{128,64},{192,128},{1,193},{65,1},{129,65},{193,129... | collective-permute-start | bytes 1179656 | tf_op jit(solution)/shard_map/ppermute | solution.py:75
  261.1 36.6 %all-to-all-start.3 = ((bf16[64,4,2,1024]{3,2,1,0:T(2,128)(2,1)}), bf16[64,4,2,1024]{3,2,1,0:T(2,128)(2,1)}, u32[]{:S(2)}, u32[]{:S(2)}) async-start(bf16[64,4,2,1024]{3,2,1,0:T(2,128)(2,1)} %bitcast.123), calls=%async_computation.3 | async-start | bytes 2097152 | tf_op jit(solution)/shard_map/all_to_all | solution.py:79
Sparse Core Ops, SparseCore 0:
  69.1 64.6 all-gather.4
  135.6 73.1 all-gather.6

commit v7 on v5

--- a/solution.py
+++ b/solution.py
@@ -84,8 +84,11 @@
             "rtep,erpf->rtf", weights, back.astype(jnp.float32),
             precision=lax.Precision.HIGHEST, preferred_element_type=jnp.float32,
         )
+        if index + 1 < len(stages):
+            combined, later = lax.optimization_barrier((combined, stages[index + 1][2]))
+            stages[index + 1] = stages[index + 1][:2] + (later,)
     combined = combined.astype(jnp.bfloat16)
-    home = lax.all_to_all(combined, "row", split_axis=0, concat_axis=2, tiled=True)
+    home = lax.all_to_all(combined.transpose(1, 0, 2), "row", split_axis=1, concat_axis=1, tiled=True)
     return home.reshape(token_count, width)
 
 

time: 326 us -> 337 us (1.034)
  waiting for transfers between devices: 105 us -> 115 us
    all_to_all x2, waiting for transfers between devices: 33.7 us -> 67 us  [local(): lax.all_to_all(result, 'col', split_axis=0, concat_axis=0, tiled=True)]
    all_gather x2, waiting for transfers between devices: 20.5 us -> 0.02 us  [local(): rows = lax.all_gather(arrived, 'row', axis=0, tiled=False)]
  transfers between devices with their start and end apart: 13 -> 13, of which waited for: 6 -> 7; matrix products, arithmetic and copies ran while one was open for 18% -> 10% of each run, Pallas kernels for 0% -> 0%
where the time goes in v7:
time: 337 us; the launch traced here: 336 us
  waiting for transfers between devices  115 us (34%)
  blocking collectives  104 us (31%)
  matrix products  42.4 us (13%)
  local copies, waits for them, and re-layouts  29.3 us (9%)
  starting transfers between devices  28.7 us (9%)
  between operations  13.7 us (4%)
    all_to_all x2, blocking collectives, local(): lax.all_to_all(outgoing, 'col', split_axis=0, concat_axis=0, tiled=True)  86.7 us
    all_to_all x2, waiting for transfers between devices, local(): lax.all_to_all(result, 'col', split_axis=0, concat_axis=0, tiled=True)  67 us
    ppermute x6, waiting for transfers between devices, local(): moved = lax.ppermute(hidden, 'row', pairs)  47.8 us
    all_to_all x1, blocking collectives, local(): lax.all_to_all(combined.transpose(1, 0, 2), 'row', split_axis=1, concat_a...  17.7 us
    dot_general x2, matrix products, local(): jnp.einsum('npak,aku->npu', rows, gate_w, preferred_element_type=jnp.floa...  12.4 us
    all_to_all x2, starting transfers between devices, local(): lax.all_to_all(result, 'col', split_axis=0, concat_axis=0, tiled=True)  12.2 us
    ppermute x6, starting transfers between devices, local(): moved = lax.ppermute(hidden, 'row', pairs)  11.8 us
    reshape x3, local copies, waits for them, and re-layouts, local(): result.reshape(groups, columns, span, quarter).transpose(1, 0, 2, 3)  10.8 us
  transfers between devices with their start and end apart: 13, of which 7 were waited for; matrix products, arithmetic and copies ran while one was open for 10% of the time, Pallas kernels for 0%

profile of v7, /device:TPU:4, one launch (start us, length us, event | category | flops | bytes accessed | tf_op | source)
XLA Modules:
  0.0 335.7 jit_solution(14068986980309047235)
XLA Ops:
  6.5 0.9 copy.126
  7.8 0.6 reduce-window.6
  8.9 0.7 fusion.80
  10.0 2.6 convolution_convert_fusion.1
  12.6 2.4 reshape.129
  14.9 40.9 %all_to_all.25 = bf16[64,64,128]{2,1,0:T(8,128)(2,1)} all-to-all(bf16[64,64,128]{2,1,0:T(8,128)(2,1)} %reshape.129), channel_id=1, replica_groups=mesh['row'=4,'col'=64] {'col'}, dimensions={0} | all-to-all | bytes 2097152 | tf_op jit(solution)/shard_map/all_to_all | solution.py:51
  56.0 3.1 collective-permute-start
  59.1 0.6 collective-permute-start.1
  59.7 1.0 collective-permute-start.2
  61.0 2.9 convolution_convert_fusion
  63.9 3.8 %reshape.128 = bf16[64,96,128]{2,1,0:T(8,128)(2,1)} reshape(bf16[192,4096]{1,0:T(8,128)(2,1)} %convolution_convert_fusion) | data formatting | bytes 3145728 | tf_op jit(solution)/shard_map/reshape | solution.py:48
  67.8 45.8 %all_to_all.26 = bf16[64,96,128]{2,1,0:T(8,128)(2,1)} all-to-all(bf16[64,96,128]{2,1,0:T(8,128)(2,1)} %reshape.128), channel_id=1, replica_groups=mesh['row'=4,'col'=64] {'col'}, dimensions={0} | all-to-all | bytes 3145728 | tf_op jit(solution)/shard_map/all_to_all | solution.py:51
  113.7 5.6 %fusion.25 = f32[512,384]{1,0:T(8,128)S(1)} fusion(bf16[32,128,384]{2,1,0:T(8,128)(2,1)} %bitcast.140, bf16[512,32,128]{2,1,0:T(8,128)(2,1)} %bitcast.138), kind=kOutput, calls=%fused_computation.21 | convolution fusion | flops 1610612736 | bytes 8126464 | tf_op jit(solution)/shard_map/npak,aku->npu/dot_general | solution.py:57
  119.3 2.4 fusion.34
  121.7 2.0 collective-permute-start.4
  123.7 1.2 collective-permute-start.3
  124.9 2.0 collective-permute-start.5
  127.0 0.7 fusion.56
  127.7 16.2 %collective-permute-done.4 = bf16[512,384]{1,0:T(8,128)(2,1)} collective-permute-done((bf16[512,384]{1,0:T(8,128)(2,1)S(1)}, bf16[512,384]{1,0:T(8,128)(2,1)}, u32[]{:S(2)}, u32[]{:S(2)}) %collective-permute-start.4) | collective-permute-done | bytes 393248 | tf_op jit(solution)/shard_map/ppermute | solution.py:75
  143.9 1.7 fusion.48
  145.6 11.7 %collective-permute-done.3 = bf16[512,384]{1,0:T(8,128)(2,1)S(1)} collective-permute-done((bf16[512,384]{1,0:T(8,128)(2,1)S(1)}, bf16[512,384]{1,0:T(8,128)(2,1)S(1)}, u32[]{:S(2)}, u32[]{:S(2)}) %collective-permute-start.3) | collective-permute-done | bytes 393248 | tf_op jit(solution)/shard_map/ppermute | solution.py:75
  157.3 0.7 fusion.52
  158.2 1.7 add_convert_fusion.1
  159.9 2.3 reshape.131
  162.2 3.4 copy.195
  165.5 5.6 %all-to-all-start.1 = ((bf16[64,4,2,1024]{3,2,1,0:T(2,128)(2,1)}), bf16[64,4,2,1024]{3,2,1,0:T(2,128)(2,1)}, u32[]{:S(2)}, u32[]{:S(2)}) async-start(bf16[64,4,2,1024]{3,2,1,0:T(2,128)(2,1)} %bitcast.124), calls=%async_computation.1 | async-start | bytes 2097152 | tf_op jit(solution)/shard_map/all_to_all | solution.py:79
  171.1 0.3 select_reduce_fusion.1
  171.5 0.8 copy.140
  172.3 27.5 %all-to-all-done.1 = bf16[64,4,2,1024]{3,2,1,0:T(2,128)(2,1)} async-done(((bf16[64,4,2,1024]{3,2,1,0:T(2,128)(2,1)}), bf16[64,4,2,1024]{3,2,1,0:T(2,128)(2,1)}, u32[]{:S(2)}, u32[]{:S(2)}) %all-to-all-start.1) | async-done | bytes 1048608 | tf_op jit(solution)/shard_map/all_to_all | solution.py:79
  199.8 4.6 %convolution_bitcast_fusion = f32[4,128,1024]{2,1,0:T(8,128)} fusion(bf16[64,4,2,1024]{3,2,1,0:T(2,128)(2,1)} %all-to-all-done.1, f32[4,128,64,2]{1,3,2,0:T(2,128)} %bitcast.127), kind=kOutput, calls=%fused_computation.14 | convolution fusion | flops 805306368 | bytes 3407872 | tf_op jit(solution)/shard_map/rtep,erpf->rtf/dot_general | solution.py:83
  204.5 6.7 %fusion.10 = f32[768,384]{1,0:T(8,128)S(1)} fusion(bf16[32,128,384]{2,1,0:T(8,128)(2,1)} %bitcast.141, bf16[768,32,128]{2,1,0:T(8,128)(2,1)} %bitcast.136), kind=kOutput, calls=%fused_computation.16 | convolution fusion | flops 2415919104 | bytes 10616832 | tf_op jit(solution)/shard_map/npak,aku->npu/dot_general | solution.py:57
  211.2 3.6 %fusion.22 = bf16[768,384]{1,0:T(8,128)(2,1)S(1)} fusion(bf16[32,128,384]{2,1,0:T(8,128)(2,1)S(1)} %bitcast.143, bf16[768,32,128]{2,1,0:T(8,128)(2,1)S(1)} %bitcast.137, f32[768,384]{1,0:T(8,128)S(1)} %fusion.10), kind=kOutput, calls=%fused_computation.20 | convolution fusion | flops 2417688576 | bytes 11206656 | tf_op jit(solution)/shard_map/npak,aku->npu/dot_general | solution.py:58
  214.8 3.3 collective-permute-start.7
  218.1 3.2 collective-permute-start.8
  221.3 1.0 fusion.54
  222.3 10.4 %collective-permute-done.7 = bf16[768,384]{1,0:T(8,128)(2,1)S(1)} collective-permute-done((bf16[768,384]{1,0:T(8,128)(2,1)S(1)}, bf16[768,384]{1,0:T(8,128)(2,1)S(1)}, u32[]{:S(2)}, u32[]{:S(2)}) %collective-permute-start.7) | collective-permute-done | bytes 589856 | tf_op jit(solution)/shard_map/ppermute | solution.py:75
  232.7 1.0 fusion.46
  233.7 9.3 %collective-permute-done.6 = bf16[768,384]{1,0:T(8,128)(2,1)S(1)} collective-permute-done((bf16[768,384]{1,0:T(8,128)(2,1)S(1)}, bf16[768,384]{1,0:T(8,128)(2,1)S(1)}, u32[]{:S(2)}, u32[]{:S(2)}) %collective-permute-start.6) | collective-permute-done | bytes 589856 | tf_op jit(solution)/shard_map/ppermute | solution.py:75
  243.0 1.0 fusion.50
  244.0 2.2 add_convert_fusion
  246.2 5.1 %reshape.133 = bf16[4,64,3,1024]{3,2,1,0:T(4,128)(2,1)} reshape(bf16[768,1024]{1,0:T(8,128)(2,1)} %add_convert_fusion) | data formatting | bytes 3145728 | tf_op jit(solution)/shard_map/reshape | solution.py:78
  251.3 4.8 %copy.151 = bf16[64,4,3,1024]{3,1,2,0:T(4,128)(2,1)} copy(bf16[64,4,3,1024]{3,2,0,1:T(4,128)(2,1)} %bitcast.123) | data formatting | bytes 3145728 | tf_op jit(solution)/shard_map/transpose | solution.py:78
  256.1 6.6 %all-to-all-start.3 = ((bf16[64,4,3,1024]{3,1,2,0:T(4,128)(2,1)}), bf16[64,4,3,1024]{3,1,2,0:T(4,128)(2,1)}, u32[]{:S(2)}, u32[]{:S(2)}) async-start(bf16[64,4,3,1024]{3,1,2,0:T(4,128)(2,1)} %copy.151), calls=%async_computation.3 | async-start | bytes 3145728 | tf_op jit(solution)/shard_map/all_to_all | solution.py:79
  263.2 39.6 %all-to-all-done.3 = bf16[64,4,3,1024]{3,1,2,0:T(4,128)(2,1)} async-done(((bf16[64,4,3,1024]{3,1,2,0:T(4,128)(2,1)}), bf16[64,4,3,1024]{3,1,2,0:T(4,128)(2,1)}, u32[]{:S(2)}, u32[]{:S(2)}) %all-to-all-start.3) | async-done | bytes 1572896 | tf_op jit(solution)/shard_map/all_to_all | solution.py:79
  302.7 3.9 %fusion.19 = bf16[128,4,1024]{2,0,1:T(8,128)(2,1)S(1)} fusion(f32[4,128,1024]{2,1,0:T(8,128)} %convolution_bitcast_fusion, bf16[64,4,3,1024]{3,1,2,0:T(4,128)(2,1)} %all-to-all-done.3, f32[4,128,64,3]{1,0,3,2:T(4,128)S(1)} %bitcast.126), kind=kOutput, calls=%fused_computation.19 | convolution fusion | flops 1209008128 | bytes 5111808 | tf_op jit(solution)/shard_map/rtep,erpf->rtf/dot_general | solution.py:83
  306.6 17.7 %all_to_all.27 = bf16[128,4,1024]{2,0,1:T(8,128)(2,1)} all-to-all(bf16[128,4,1024]{2,0,1:T(8,128)(2,1)S(1)} %fusion.19), channel_id=1, replica_groups=mesh['row'=4,'col'=64] {'row'}, dimensions={1} | all-to-all | bytes 2097152 | tf_op jit(solution)/shard_map/all_to_all | solution.py:91
  324.3 2.3 copy.154
  326.6 2.3 copy.155
  (53 shorter events, 2.2 us)
Async XLA Ops:
  6.5 120.4 %copy-start = (bf16[1,1536,1024]{2,1,0:T(8,128)(2,1)S(1)}, bf16[1,1536,1024]{2,1,0:T(8,128)(2,1)}, u32[]{:S(2)}) copy-start(bf16[1,1536,1024]{2,1,0:T(8,128)(2,1)} %param.11) | copy-start | bytes 9437188
  6.5 107.1 %all-gather.5.cloned.1.call-start = ((), (), s32[]{:S(2)}) async-start(), calls=%async_computation.5 | async-start | bytes 5242880 | tf_op jit(solution)/shard_map/all_gather | solution.py:53
  12.6 43.3 %copy-start.1 = (f32[128,2]{0,1:T(2,128)S(1)}, f32[128,2]{0,1:T(2,128)}, u32[]{:S(2)}) copy-start(f32[128,2]{0,1:T(2,128)} %param.8) | copy-start | bytes 3076
  55.9 148.6 %all-gather.7.cloned.1.call-start = ((), (), s32[]{:S(2)}) async-start(), calls=%async_computation.6 | async-start | bytes 7864320 | tf_op jit(solution)/shard_map/all_gather | solution.py:53
  56.0 11.8 %collective-permute-start = (f32[128,4]{0,1:T(4,128)S(1)}, f32[128,4]{0,1:T(4,128)S(1)}, u32[]{:S(2)}, u32[]{:S(2)}) collective-permute-start(f32[128,4]{0,1:T(4,128)S(1)} %pad_maximum_fusion), channel_id=1, source_target_pairs={{0,192},{64,0},{128,64},{192,128},{1,193},{65,1},{129,65},{193,129... | collective-permute-start | bytes 6152 | tf_op jit(solution)/shard_map/ppermute | solution.py:30
  59.1 8.7 %collective-permute-start.1 = (f32[128,4]{0,1:T(4,128)S(1)}, f32[128,4]{0,1:T(4,128)S(1)}, u32[]{:S(2)}, u32[]{:S(2)}) collective-permute-start(f32[128,4]{0,1:T(4,128)S(1)} %pad_maximum_fusion), channel_id=1, source_target_pairs={{0,128},{64,192},{128,0},{192,64},{1,129},{65,193},{129,1},{193,65... | collective-permute-start | bytes 6152 | tf_op jit(solution)/shard_map/ppermute | solution.py:30
  59.7 8.1 %collective-permute-start.2 = (f32[128,4]{0,1:T(4,128)S(1)}, f32[128,4]{0,1:T(4,128)S(1)}, u32[]{:S(2)}, u32[]{:S(2)}) collective-permute-start(f32[128,4]{0,1:T(4,128)S(1)} %pad_maximum_fusion), channel_id=1, source_target_pairs={{0,64},{64,128},{128,192},{192,0},{1,65},{65,129},{129,193},{193,1... | collective-permute-start | bytes 6152 | tf_op jit(solution)/shard_map/ppermute | solution.py:30
  113.7 5.7 %copy-start.3 = (bf16[256,64,128]{2,1,0:T(8,128)(2,1)S(1)}, bf16[256,64,128]{2,1,0:T(8,128)(2,1)}, u32[]{:S(2)}) copy-start(bf16[256,64,128]{2,1,0:T(8,128)(2,1)} %all-gather.5.cloned.1.call-done) | copy-start | bytes 12582916
  113.7 5.7 %copy-start.4 = (bf16[1,4096,384]{2,1,0:T(8,128)(2,1)S(1)}, bf16[1,4096,384]{2,1,0:T(8,128)(2,1)}, u32[]{:S(2)}) copy-start(bf16[1,4096,384]{2,1,0:T(8,128)(2,1)} %param.10) | copy-start | bytes 9437188
  121.7 22.2 %collective-permute-start.4 = (bf16[512,384]{1,0:T(8,128)(2,1)S(1)}, bf16[512,384]{1,0:T(8,128)(2,1)}, u32[]{:S(2)}, u32[]{:S(2)}) collective-permute-start(bf16[512,384]{1,0:T(8,128)(2,1)S(1)} %fusion.34), channel_id=1, source_target_pairs={{0,128},{64,192},{128,0},{192,64},{1,129},{65,193},{129,1},{193,65... | collective-permute-start | bytes 1179656 | tf_op jit(solution)/shard_map/ppermute | solution.py:75
  123.7 33.6 %collective-permute-start.3 = (bf16[512,384]{1,0:T(8,128)(2,1)S(1)}, bf16[512,384]{1,0:T(8,128)(2,1)S(1)}, u32[]{:S(2)}, u32[]{:S(2)}) collective-permute-start(bf16[512,384]{1,0:T(8,128)(2,1)S(1)} %fusion.34), channel_id=1, source_target_pairs={{0,64},{64,128},{128,192},{192,0},{1,65},{65,129},{129,193},{193,1... | collective-permute-start | bytes 1179656 | tf_op jit(solution)/shard_map/ppermute | solution.py:75
  124.9 33.2 %collective-permute-start.5 = (bf16[512,384]{1,0:T(8,128)(2,1)S(1)}, bf16[512,384]{1,0:T(8,128)(2,1)S(1)}, u32[]{:S(2)}, u32[]{:S(2)}) collective-permute-start(bf16[512,384]{1,0:T(8,128)(2,1)S(1)} %fusion.34), channel_id=1, source_target_pairs={{0,192},{64,0},{128,64},{192,128},{1,193},{65,1},{129,65},{193,129... | collective-permute-start | bytes 1179656 | tf_op jit(solution)/shard_map/ppermute | solution.py:75
  165.5 34.3 %all-to-all-start.1 = ((bf16[64,4,2,1024]{3,2,1,0:T(2,128)(2,1)}), bf16[64,4,2,1024]{3,2,1,0:T(2,128)(2,1)}, u32[]{:S(2)}, u32[]{:S(2)}) async-start(bf16[64,4,2,1024]{3,2,1,0:T(2,128)(2,1)} %bitcast.124), calls=%async_computation.1 | async-start | bytes 2097152 | tf_op jit(solution)/shard_map/all_to_all | solution.py:79
  204.4 6.8 %copy-start.2 = (bf16[256,96,128]{2,1,0:T(8,128)(2,1)S(1)}, bf16[256,96,128]{2,1,0:T(8,128)(2,1)}, u32[]{:S(2)}) copy-start(bf16[256,96,128]{2,1,0:T(8,128)(2,1)} %all-gather.7.cloned.1.call-done) | copy-start | bytes 18874372
  204.5 6.8 %copy-start.5 = (bf16[1,4096,384]{2,1,0:T(8,128)(2,1)S(1)}, bf16[1,4096,384]{2,1,0:T(8,128)(2,1)}, u32[]{:S(2)}) copy-start(bf16[1,4096,384]{2,1,0:T(8,128)(2,1)} %param.10) | copy-start | bytes 9437188
  214.8 17.9 %collective-permute-start.7 = (bf16[768,384]{1,0:T(8,128)(2,1)S(1)}, bf16[768,384]{1,0:T(8,128)(2,1)S(1)}, u32[]{:S(2)}, u32[]{:S(2)}) collective-permute-start(bf16[768,384]{1,0:T(8,128)(2,1)S(1)} %fusion.22), channel_id=1, source_target_pairs={{0,128},{64,192},{128,0},{192,64},{1,129},{65,193},{129,1},{193,65... | collective-permute-start | bytes 1769480 | tf_op jit(solution)/shard_map/ppermute | solution.py:75
  218.1 24.9 %collective-permute-start.6 = (bf16[768,384]{1,0:T(8,128)(2,1)S(1)}, bf16[768,384]{1,0:T(8,128)(2,1)S(1)}, u32[]{:S(2)}, u32[]{:S(2)}) collective-permute-start(bf16[768,384]{1,0:T(8,128)(2,1)S(1)} %fusion.22), channel_id=1, source_target_pairs={{0,64},{64,128},{128,192},{192,0},{1,65},{65,129},{129,193},{193,1... | collective-permute-start | bytes 1769480 | tf_op jit(solution)/shard_map/ppermute | solution.py:75
  218.1 25.9 %collective-permute-start.8 = (bf16[768,384]{1,0:T(8,128)(2,1)S(1)}, bf16[768,384]{1,0:T(8,128)(2,1)S(1)}, u32[]{:S(2)}, u32[]{:S(2)}) collective-permute-start(bf16[768,384]{1,0:T(8,128)(2,1)S(1)} %fusion.22), channel_id=1, source_target_pairs={{0,192},{64,0},{128,64},{192,128},{1,193},{65,1},{129,65},{193,129... | collective-permute-start | bytes 1769480 | tf_op jit(solution)/shard_map/ppermute | solution.py:75
  256.1 46.6 %all-to-all-start.3 = ((bf16[64,4,3,1024]{3,1,2,0:T(4,128)(2,1)}), bf16[64,4,3,1024]{3,1,2,0:T(4,128)(2,1)}, u32[]{:S(2)}, u32[]{:S(2)}) async-start(bf16[64,4,3,1024]{3,1,2,0:T(4,128)(2,1)} %copy.151), calls=%async_computation.3 | async-start | bytes 3145728 | tf_op jit(solution)/shard_map/all_to_all | solution.py:79
Sparse Core Ops, SparseCore 0:
  56.0 47.4 all-gather.4
  113.8 78.8 all-gather.6

commit v8 on v5

--- a/solution.py
+++ b/solution.py
@@ -1,7 +1,7 @@
 import jax
 import jax.numpy as jnp
 from jax import lax
-from jax.sharding import PartitionSpec as P
+from jax.sharding import Mesh, PartitionSpec as P
 
 CHUNKS = ((0, 2), (2, 5))
 
@@ -11,7 +11,9 @@
     width = tokens.shape[1]
     unit_count = w_gate.shape[2]
     quarter = w_down.shape[2]
-    columns = lax.axis_size("col")
+    high = lax.axis_size("hi")
+    low = lax.axis_size("lo")
+    columns = high * low
     groups = lax.axis_size("row")
     experts = w_gate.shape[0] * columns
     capacity = max(2, token_count * top_count * 5 // (4 * experts))
@@ -48,7 +50,10 @@
         outgoing = outgoing.reshape(columns, span * width // 128, 128)
         if previous is not None:
             outgoing, _, meta = lax.optimization_barrier((outgoing, previous, meta))
-        arrived = lax.all_to_all(outgoing, "col", split_axis=0, concat_axis=0, tiled=True)
+        staged = outgoing.reshape(high, low, span * width // 128, 128)
+        staged = lax.all_to_all(staged, "lo", split_axis=1, concat_axis=1, tiled=True)
+        staged = lax.all_to_all(staged, "hi", split_axis=0, concat_axis=0, tiled=True)
+        arrived = staged.reshape(columns, span * width // 128, 128)
         previous = arrived
         rows = lax.all_gather(arrived, "row", axis=0, tiled=False)
         rows = rows.reshape(groups * columns, span, width // 128, 128)
@@ -76,7 +81,7 @@
             total = total + jnp.dot(moved, down_blocks[step], preferred_element_type=jnp.float32)
         result = total.astype(jnp.bfloat16)
         result = result.reshape(groups, columns, span, quarter).transpose(1, 0, 2, 3)
-        back = lax.all_to_all(result, "col", split_axis=0, concat_axis=0, tiled=True)
+        back = lax.all_to_all(result, ("hi", "lo"), split_axis=0, concat_axis=0, tiled=True)
         match = (all_slots[:, :, :, None] == wanted.astype(jnp.float32)[None, None, None, :])
         weights = jnp.sum(jnp.where(match, all_shares[:, :, :, None], 0.0), axis=2)
         weights = weights.reshape(groups, token_count, experts, span)
@@ -90,14 +95,14 @@
 
 
 def solution(mesh):
-    placed = (
-        P(("row", "col"), None),
-        P(("row", "col"), None),
-        P(("row", "col"), None),
-        P("col", None, "row"),
-        P("col", None, "row"),
-        P("col", None, "row"),
+    high = mesh.devices.shape[1] // 8 if mesh.devices.shape[1] % 8 == 0 else 1
+    split = Mesh(
+        mesh.devices.reshape(mesh.devices.shape[0], high, mesh.devices.shape[1] // high),
+        ("row", "hi", "lo"),
     )
+    tokens_spec = P(("row", "hi", "lo"), None)
+    weights_spec = P(("hi", "lo"), None, "row")
+    placed = (tokens_spec, tokens_spec, tokens_spec, weights_spec, weights_spec, weights_spec)
     return jax.shard_map(
-        local, mesh=mesh, in_specs=placed, out_specs=P(("row", "col"), None), check_vma=False
+        local, mesh=split, in_specs=placed, out_specs=tokens_spec, check_vma=False
     )

time: 326 us -> 365 us (1.12)
  blocking collectives: 104 us -> 139 us
    all_to_all x2 -> x4, blocking collectives: 86.7 us -> 122 us  [the longest x2 80.7 us: local(): lax.all_to_all(staged, 'hi', split_axis=0, concat_axis=0, tiled=True)]
    another operation x1 -> x3, local copies, waits for them, and re-layouts: 0.01 us -> 3.66 us  [the longest x2 3.65 us: local(): staged = outgoing.reshape(high, low, span * width // 128, 128)]
  transfers between devices with their start and end apart: 13 -> 13, of which waited for: 6 -> 6; matrix products, arithmetic and copies ran while one was open for 18% -> 16% of each run, Pallas kernels for 0% -> 0%
where the time goes in v8:
time: 365 us; the launch traced here: 364 us
  blocking collectives  139 us (38%)
  waiting for transfers between devices  105 us (29%)
  matrix products  42.4 us (12%)
  local copies, waits for them, and re-layouts  32.4 us (9%)
  starting transfers between devices  28.1 us (8%)
  between operations  13.7 us (4%)
    all_to_all x2, blocking collectives, local(): lax.all_to_all(staged, 'hi', split_axis=0, concat_axis=0, tiled=True)  80.7 us
    ppermute x6, waiting for transfers between devices, local(): moved = lax.ppermute(hidden, 'row', pairs)  52.9 us
    all_to_all x2, blocking collectives, local(): lax.all_to_all(staged, 'lo', split_axis=1, concat_axis=1, tiled=True)  41.4 us
    all_to_all x2, waiting for transfers between devices, local(): lax.all_to_all(result, ('hi', 'lo'), split_axis=0, concat_axis=0, tiled=T...  33.8 us
    all_gather x2, waiting for transfers between devices, local(): rows = lax.all_gather(arrived, 'row', axis=0, tiled=False)  18.7 us
    all_to_all x1, blocking collectives, local(): lax.all_to_all(combined, 'row', split_axis=0, concat_axis=2, tiled=True)  17.3 us
    all_to_all x2, starting transfers between devices, local(): lax.all_to_all(result, ('hi', 'lo'), split_axis=0, concat_axis=0, tiled=T...  13.5 us
    dot_general x2, matrix products, local(): jnp.einsum('npak,aku->npu', rows, gate_w, preferred_element_type=jnp.floa...  12.3 us
  transfers between devices with their start and end apart: 13, of which 6 were waited for; matrix products, arithmetic and copies ran while one was open for 16% of the time, Pallas kernels for 0%

profile of v8, /device:TPU:4, one launch (start us, length us, event | category | flops | bytes accessed | tf_op | source)
XLA Modules:
  0.0 363.7 jit_solution(12109151928093625833)
XLA Ops:
  6.5 0.9 copy.169
  8.9 0.7 fusion.78
  10.0 2.6 convolution_convert_fusion.1
  12.6 2.3 reshape_reshape.3
  14.9 1.3 copy.184
  16.3 17.6 %all_to_all.45 = bf16[8,8,64,128]{3,2,0,1:T(8,128)(2,1)S(1)} all-to-all(bf16[8,8,64,128]{3,2,0,1:T(8,128)(2,1)S(1)} %copy.184), channel_id=1, replica_groups=mesh['row'=4,'hi'=8,'lo'=8] {'lo'}, dimensions={1} | all-to-all | bytes 2097152 | tf_op jit(solution)/shard_map/all_to_all | solution.py:54
  33.9 37.1 %all_to_all.46 = bf16[8,8,64,128]{3,2,1,0:T(8,128)(2,1)} all-to-all(bf16[8,8,64,128]{3,2,1,0:T(8,128)(2,1)S(1)} %copy.185), channel_id=1, replica_groups=mesh['row'=4,'hi'=8,'lo'=8] {'hi'}, dimensions={0} | all-to-all | bytes 2097152 | tf_op jit(solution)/shard_map/all_to_all | solution.py:55
  71.2 3.1 collective-permute-start
  74.9 1.0 collective-permute-start.2
  76.2 2.9 convolution_convert_fusion
  79.2 3.8 %reshape.130 = bf16[64,96,128]{2,1,0:T(8,128)(2,1)} reshape(bf16[192,4096]{1,0:T(8,128)(2,1)} %convolution_convert_fusion) | data formatting | bytes 3145728 | tf_op jit(solution)/shard_map/reshape | solution.py:50
  83.1 1.5 copy.194
  84.6 23.8 %all_to_all.47 = bf16[8,8,96,128]{3,2,0,1:T(8,128)(2,1)S(1)} all-to-all(bf16[8,8,96,128]{3,2,0,1:T(8,128)(2,1)S(1)} %copy.194), channel_id=1, replica_groups=mesh['row'=4,'hi'=8,'lo'=8] {'lo'}, dimensions={1} | all-to-all | bytes 3145728 | tf_op jit(solution)/shard_map/all_to_all | solution.py:54
  108.6 43.6 %all_to_all.48 = bf16[8,8,96,128]{3,2,1,0:T(8,128)(2,1)} all-to-all(bf16[8,8,96,128]{3,2,1,0:T(8,128)(2,1)S(1)} %copy.195), channel_id=1, replica_groups=mesh['row'=4,'hi'=8,'lo'=8] {'hi'}, dimensions={0} | all-to-all | bytes 3145728 | tf_op jit(solution)/shard_map/all_to_all | solution.py:55
  152.2 5.6 %fusion.22 = f32[512,384]{1,0:T(8,128)S(1)} fusion(bf16[32,128,384]{2,1,0:T(8,128)(2,1)} %bitcast.146, bf16[512,32,128]{2,1,0:T(8,128)(2,1)} %bitcast.144), kind=kOutput, calls=%fused_computation.19 | convolution fusion | flops 1610612736 | bytes 8126464 | tf_op jit(solution)/shard_map/npak,aku->npu/dot_general | solution.py:62
  157.9 2.4 fusion.31
  160.2 1.9 collective-permute-start.3
  162.1 1.9 collective-permute-start.4
  164.0 1.0 collective-permute-start.5
  165.7 16.0 %collective-permute-done.3 = bf16[512,384]{1,0:T(8,128)(2,1)} collective-permute-done((bf16[512,384]{1,0:T(8,128)(2,1)S(1)}, bf16[512,384]{1,0:T(8,128)(2,1)}, u32[]{:S(2)}, u32[]{:S(2)}) %collective-permute-start.3) | collective-permute-done | bytes 393248 | tf_op jit(solution)/shard_map/ppermute | solution.py:80
  181.7 1.7 fusion.50
  183.4 14.4 %collective-permute-done.4 = bf16[512,384]{1,0:T(8,128)(2,1)S(1)} collective-permute-done((bf16[512,384]{1,0:T(8,128)(2,1)S(1)}, bf16[512,384]{1,0:T(8,128)(2,1)S(1)}, u32[]{:S(2)}, u32[]{:S(2)}) %collective-permute-start.4) | collective-permute-done | bytes 393248 | tf_op jit(solution)/shard_map/ppermute | solution.py:80
  198.5 1.7 add_convert_fusion.1
  200.2 2.3 reshape.132
  202.5 3.4 copy.240
  205.9 7.5 %all-to-all-start.2 = ((bf16[64,4,2,1024]{3,2,1,0:T(2,128)(2,1)}), bf16[64,4,2,1024]{3,2,1,0:T(2,128)(2,1)}, u32[]{:S(2)}, u32[]{:S(2)}) async-start(bf16[64,4,2,1024]{3,2,1,0:T(2,128)(2,1)} %bitcast.129), calls=%async_computation.2 | async-start | bytes 2097152 | tf_op jit(solution)/shard_map/all_to_all | solution.py:84
  213.3 18.7 %all-gather.5.cloned.1.call-done = bf16[4,64,96,128]{3,2,1,0:T(8,128)(2,1)} async-done(((bf16[1,64,96,128]{3,2,1,0:T(8,128)(2,1)}), bf16[4,64,96,128]{3,2,1,0:T(8,128)(2,1)}) %all-gather.5.cloned.1.call-update) | async-done | bytes 6291472 | tf_op jit(solution)/shard_map/all_gather | solution.py:58
  232.0 6.7 %fusion.10 = f32[768,384]{1,0:T(8,128)S(1)} fusion(bf16[32,128,384]{2,1,0:T(8,128)(2,1)} %bitcast.147, bf16[768,32,128]{2,1,0:T(8,128)(2,1)} %bitcast.142), kind=kOutput, calls=%fused_computation.15 | convolution fusion | flops 2415919104 | bytes 10616832 | tf_op jit(solution)/shard_map/npak,aku->npu/dot_general | solution.py:62
  238.7 3.6 fusion.19
  242.3 1.8 collective-permute-start.7
  244.1 1.6 collective-permute-start.6
  245.8 1.6 collective-permute-start.8
  247.4 1.0 fusion.52
  248.3 11.8 %collective-permute-done.7 = bf16[768,384]{1,0:T(8,128)(2,1)S(1)} collective-permute-done((bf16[768,384]{1,0:T(8,128)(2,1)S(1)}, bf16[768,384]{1,0:T(8,128)(2,1)S(1)}, u32[]{:S(2)}, u32[]{:S(2)}) %collective-permute-start.7) | collective-permute-done | bytes 589856 | tf_op jit(solution)/shard_map/ppermute | solution.py:80
  260.1 1.0 fusion.44
  261.1 10.7 %collective-permute-done.6 = bf16[768,384]{1,0:T(8,128)(2,1)S(1)} collective-permute-done((bf16[768,384]{1,0:T(8,128)(2,1)S(1)}, bf16[768,384]{1,0:T(8,128)(2,1)S(1)}, u32[]{:S(2)}, u32[]{:S(2)}) %collective-permute-start.6) | collective-permute-done | bytes 589856 | tf_op jit(solution)/shard_map/ppermute | solution.py:80
  271.8 1.0 fusion.48
  272.8 2.2 add_convert_fusion
  275.0 5.1 %reshape.135 = bf16[4,64,3,1024]{3,2,1,0:T(4,128)(2,1)} reshape(bf16[768,1024]{1,0:T(8,128)(2,1)} %add_convert_fusion) | data formatting | bytes 3145728 | tf_op jit(solution)/shard_map/reshape | solution.py:83
  280.1 4.8 %copy.198 = bf16[64,4,3,1024]{3,1,2,0:T(4,128)(2,1)} copy(bf16[64,4,3,1024]{3,2,0,1:T(4,128)(2,1)} %bitcast.125) | data formatting | bytes 3145728 | tf_op jit(solution)/shard_map/transpose | solution.py:83
  284.9 6.1 %all-to-all-start.5 = ((bf16[64,4,3,1024]{3,1,2,0:T(4,128)(2,1)}), bf16[64,4,3,1024]{3,1,2,0:T(4,128)(2,1)}, u32[]{:S(2)}, u32[]{:S(2)}) async-start(bf16[64,4,3,1024]{3,1,2,0:T(4,128)(2,1)} %copy.198), calls=%async_computation.5 | async-start | bytes 3145728 | tf_op jit(solution)/shard_map/all_to_all | solution.py:84
  291.3 0.8 copy.183
  292.6 4.7 %fusion.34 = f32[4,128,1024,1]{2,1,3,0:T(8,128)} fusion(bf16[64,4,2,1024]{3,2,1,0:T(2,128)(2,1)} %all-to-all-done.2, f32[4,128,64,2]{1,3,2,0:T(2,128)} %bitcast.133), kind=kOutput, calls=%fused_computation.23 | convolution fusion | flops 805306368 | bytes 3407872 | tf_op jit(solution)/shard_map/rtep,erpf->rtf/dot_general | solution.py:88
  297.2 33.8 %all-to-all-done.5 = bf16[64,4,3,1024]{3,1,2,0:T(4,128)(2,1)} async-done(((bf16[64,4,3,1024]{3,1,2,0:T(4,128)(2,1)}), bf16[64,4,3,1024]{3,1,2,0:T(4,128)(2,1)}, u32[]{:S(2)}, u32[]{:S(2)}) %all-to-all-start.5) | async-done | bytes 1572896 | tf_op jit(solution)/shard_map/all_to_all | solution.py:84
  331.0 3.9 %fusion.8 = bf16[4,128,1024]{2,1,0:T(8,128)(2,1)S(1)} fusion(f32[4,128,1024,1]{2,1,3,0:T(8,128)} %fusion.34, bf16[64,4,3,1024]{3,1,2,0:T(4,128)(2,1)} %all-to-all-done.5, f32[4,128,64,3]{1,0,3,2:T(4,128)S(1)} %bitcast.132), kind=kOutput, calls=%fused_computation.12 | convolution fusion | flops 1209008128 | bytes 5111808 | tf_op jit(solution)/shard_map/rtep,erpf->rtf/dot_general | solution.py:88
  334.9 17.3 %all_to_all.49 = bf16[4,128,1024]{2,1,0:T(8,128)(2,1)} all-to-all(bf16[4,128,1024]{2,1,0:T(8,128)(2,1)S(1)} %fusion.8), channel_id=1, replica_groups=mesh['row'=4,'hi'=8,'lo'=8] {'row'}, dimensions={0} | all-to-all | bytes 2097152 | tf_op jit(solution)/shard_map/all_to_all | solution.py:93
  352.3 2.3 copy.201
  354.6 2.3 copy.202
  (59 shorter events, 5.3 us)
Async XLA Ops:
  6.5 158.4 %copy-start = (bf16[1,1536,1024]{2,1,0:T(8,128)(2,1)S(1)}, bf16[1,1536,1024]{2,1,0:T(8,128)(2,1)}, u32[]{:S(2)}) copy-start(bf16[1,1536,1024]{2,1,0:T(8,128)(2,1)} %param.11) | copy-start | bytes 9437188
  6.5 145.6 %all-gather.3.cloned.1.call-start = ((), (), s32[]{:S(2)}) async-start(), calls=%async_computation.7 | async-start | bytes 5242880 | tf_op jit(solution)/shard_map/all_gather | solution.py:58
  33.8 37.3 %copy-start.1 = (f32[128,2]{0,1:T(2,128)S(1)}, f32[128,2]{0,1:T(2,128)}, u32[]{:S(2)}) copy-start(f32[128,2]{0,1:T(2,128)} %param.8) | copy-start | bytes 3076
  71.1 160.9 %all-gather.5.cloned.1.call-start = ((), (), s32[]{:S(2)}) async-start(), calls=%async_computation.8 | async-start | bytes 7864320 | tf_op jit(solution)/shard_map/all_gather | solution.py:58
  71.2 11.8 %collective-permute-start = (f32[128,4]{0,1:T(4,128)S(1)}, f32[128,4]{0,1:T(4,128)S(1)}, u32[]{:S(2)}, u32[]{:S(2)}) collective-permute-start(f32[128,4]{0,1:T(4,128)S(1)} %pad_maximum_fusion), channel_id=1, source_target_pairs={{0,192},{64,0},{128,64},{192,128},{1,193},{65,1},{129,65},{193,129... | collective-permute-start | bytes 6152 | tf_op jit(solution)/shard_map/ppermute | solution.py:32
  74.3 8.7 %collective-permute-start.1 = (f32[128,4]{0,1:T(4,128)S(1)}, f32[128,4]{0,1:T(4,128)S(1)}, u32[]{:S(2)}, u32[]{:S(2)}) collective-permute-start(f32[128,4]{0,1:T(4,128)S(1)} %pad_maximum_fusion), channel_id=1, source_target_pairs={{0,128},{64,192},{128,0},{192,64},{1,129},{65,193},{129,1},{193,65... | collective-permute-start | bytes 6152 | tf_op jit(solution)/shard_map/ppermute | solution.py:32
  74.9 8.1 %collective-permute-start.2 = (f32[128,4]{0,1:T(4,128)S(1)}, f32[128,4]{0,1:T(4,128)S(1)}, u32[]{:S(2)}, u32[]{:S(2)}) collective-permute-start(f32[128,4]{0,1:T(4,128)S(1)} %pad_maximum_fusion), channel_id=1, source_target_pairs={{0,64},{64,128},{128,192},{192,0},{1,65},{65,129},{129,193},{193,1... | collective-permute-start | bytes 6152 | tf_op jit(solution)/shard_map/ppermute | solution.py:32
  152.2 5.7 %copy-start.3 = (bf16[4,64,64,128]{3,2,1,0:T(8,128)(2,1)S(1)}, bf16[4,64,64,128]{3,2,1,0:T(8,128)(2,1)}, u32[]{:S(2)}) copy-start(bf16[4,64,64,128]{3,2,1,0:T(8,128)(2,1)} %all-gather.3.cloned.1.call-done) | copy-start | bytes 12582916
  152.2 5.7 %copy-start.4 = (bf16[1,4096,384]{2,1,0:T(8,128)(2,1)S(1)}, bf16[1,4096,384]{2,1,0:T(8,128)(2,1)}, u32[]{:S(2)}) copy-start(bf16[1,4096,384]{2,1,0:T(8,128)(2,1)} %param.10) | copy-start | bytes 9437188
  160.2 21.5 %collective-permute-start.3 = (bf16[512,384]{1,0:T(8,128)(2,1)S(1)}, bf16[512,384]{1,0:T(8,128)(2,1)}, u32[]{:S(2)}, u32[]{:S(2)}) collective-permute-start(bf16[512,384]{1,0:T(8,128)(2,1)S(1)} %fusion.31), channel_id=1, source_target_pairs={{0,64},{64,128},{128,192},{192,0},{1,65},{65,129},{129,193},{193,1... | collective-permute-start | bytes 1179656 | tf_op jit(solution)/shard_map/ppermute | solution.py:80
  162.1 35.7 %collective-permute-start.4 = (bf16[512,384]{1,0:T(8,128)(2,1)S(1)}, bf16[512,384]{1,0:T(8,128)(2,1)S(1)}, u32[]{:S(2)}, u32[]{:S(2)}) collective-permute-start(bf16[512,384]{1,0:T(8,128)(2,1)S(1)} %fusion.31), channel_id=1, source_target_pairs={{0,128},{64,192},{128,0},{192,64},{1,129},{65,193},{129,1},{193,65... | collective-permute-start | bytes 1179656 | tf_op jit(solution)/shard_map/ppermute | solution.py:80
  164.0 34.5 %collective-permute-start.5 = (bf16[512,384]{1,0:T(8,128)(2,1)S(1)}, bf16[512,384]{1,0:T(8,128)(2,1)S(1)}, u32[]{:S(2)}, u32[]{:S(2)}) collective-permute-start(bf16[512,384]{1,0:T(8,128)(2,1)S(1)} %fusion.31), channel_id=1, source_target_pairs={{0,192},{64,0},{128,64},{192,128},{1,193},{65,1},{129,65},{193,129... | collective-permute-start | bytes 1179656 | tf_op jit(solution)/shard_map/ppermute | solution.py:80
  205.9 79.0 %all-to-all-start.2 = ((bf16[64,4,2,1024]{3,2,1,0:T(2,128)(2,1)}), bf16[64,4,2,1024]{3,2,1,0:T(2,128)(2,1)}, u32[]{:S(2)}, u32[]{:S(2)}) async-start(bf16[64,4,2,1024]{3,2,1,0:T(2,128)(2,1)} %bitcast.129), calls=%async_computation.2 | async-start | bytes 2097152 | tf_op jit(solution)/shard_map/all_to_all | solution.py:84
  232.0 6.7 %copy-start.2 = (bf16[4,64,96,128]{3,2,1,0:T(8,128)(2,1)S(1)}, bf16[4,64,96,128]{3,2,1,0:T(8,128)(2,1)}, u32[]{:S(2)}) copy-start(bf16[4,64,96,128]{3,2,1,0:T(8,128)(2,1)} %all-gather.5.cloned.1.call-done) | copy-start | bytes 18874372
  232.0 6.7 %copy-start.5 = (bf16[1,4096,384]{2,1,0:T(8,128)(2,1)S(1)}, bf16[1,4096,384]{2,1,0:T(8,128)(2,1)}, u32[]{:S(2)}) copy-start(bf16[1,4096,384]{2,1,0:T(8,128)(2,1)} %param.10) | copy-start | bytes 9437188
  242.3 17.8 %collective-permute-start.7 = (bf16[768,384]{1,0:T(8,128)(2,1)S(1)}, bf16[768,384]{1,0:T(8,128)(2,1)S(1)}, u32[]{:S(2)}, u32[]{:S(2)}) collective-permute-start(bf16[768,384]{1,0:T(8,128)(2,1)S(1)} %fusion.19), channel_id=1, source_target_pairs={{0,128},{64,192},{128,0},{192,64},{1,129},{65,193},{129,1},{193,65... | collective-permute-start | bytes 1769480 | tf_op jit(solution)/shard_map/ppermute | solution.py:80
  244.1 27.7 %collective-permute-start.6 = (bf16[768,384]{1,0:T(8,128)(2,1)S(1)}, bf16[768,384]{1,0:T(8,128)(2,1)S(1)}, u32[]{:S(2)}, u32[]{:S(2)}) collective-permute-start(bf16[768,384]{1,0:T(8,128)(2,1)S(1)} %fusion.19), channel_id=1, source_target_pairs={{0,64},{64,128},{128,192},{192,0},{1,65},{65,129},{129,193},{193,1... | collective-permute-start | bytes 1769480 | tf_op jit(solution)/shard_map/ppermute | solution.py:80
  245.8 27.0 %collective-permute-start.8 = (bf16[768,384]{1,0:T(8,128)(2,1)S(1)}, bf16[768,384]{1,0:T(8,128)(2,1)S(1)}, u32[]{:S(2)}, u32[]{:S(2)}) collective-permute-start(bf16[768,384]{1,0:T(8,128)(2,1)S(1)} %fusion.19), channel_id=1, source_target_pairs={{0,192},{64,0},{128,64},{192,128},{1,193},{65,1},{129,65},{193,129... | collective-permute-start | bytes 1769480 | tf_op jit(solution)/shard_map/ppermute | solution.py:80
  284.9 46.2 %all-to-all-start.5 = ((bf16[64,4,3,1024]{3,1,2,0:T(4,128)(2,1)}), bf16[64,4,3,1024]{3,1,2,0:T(4,128)(2,1)}, u32[]{:S(2)}, u32[]{:S(2)}) async-start(bf16[64,4,3,1024]{3,1,2,0:T(4,128)(2,1)} %copy.198), calls=%async_computation.5 | async-start | bytes 3145728 | tf_op jit(solution)/shard_map/all_to_all | solution.py:84
Sparse Core Ops, SparseCore 0:
  71.2 47.4 all-gather.2
  152.3 79.6 all-gather.4

commit v9 on v5

--- a/solution.py
+++ b/solution.py
@@ -69,6 +69,7 @@
     ]
     combined = jnp.zeros((groups, token_count, quarter), jnp.float32)
     for index, (span, wanted, hidden) in enumerate(stages):
+        earlier_done = index > 0
         total = jnp.dot(hidden, down_blocks[0], preferred_element_type=jnp.float32)
         for step in range(1, groups):
             pairs = [(i, (i + step) % groups) for i in range(groups)]
@@ -76,6 +77,8 @@
             total = total + jnp.dot(moved, down_blocks[step], preferred_element_type=jnp.float32)
         result = total.astype(jnp.bfloat16)
         result = result.reshape(groups, columns, span, quarter).transpose(1, 0, 2, 3)
+        if earlier_done:
+            result, combined = lax.optimization_barrier((result, combined))
         back = lax.all_to_all(result, "col", split_axis=0, concat_axis=0, tiled=True)
         match = (all_slots[:, :, :, None] == wanted.astype(jnp.float32)[None, None, None, :])
         weights = jnp.sum(jnp.where(match, all_shares[:, :, :, None], 0.0), axis=2)

time: 326 us -> 327 us (level)
    ppermute x6, waiting for transfers between devices: 51.1 us -> 41.5 us  [local(): moved = lax.ppermute(hidden, 'row', pairs)]
    all_to_all x2, waiting for transfers between devices: 33.7 us -> 39.6 us  [local(): lax.all_to_all(result, 'col', split_axis=0, concat_axis=0, tiled=True)]
    optimization_barrier x0 -> x1, local copies, waits for them, and re-layouts: none -> 4.8 us  [local(): result, combined = lax.optimization_barrier((result, combined))]
    transpose x1 -> x0, local copies, waits for them, and re-layouts: 4.76 us -> none  [local(): result.reshape(groups, columns, span, quarter).transpose(1, 0, 2, 3)]
  transfers between devices with their start and end apart: 13 -> 13, of which waited for: 6 -> 7; matrix products, arithmetic and copies ran while one was open for 18% -> 15% of each run, Pallas kernels for 0% -> 0%
where the time goes in v9:
time: 327 us; the launch traced here: 326 us
  blocking collectives  105 us (32%)
  waiting for transfers between devices  103 us (31%)
  matrix products  45.3 us (14%)
  local copies, waits for them, and re-layouts  29.3 us (9%)
  starting transfers between devices  27.6 us (8%)
  between operations  13.7 us (4%)
    all_to_all x2, blocking collectives, local(): lax.all_to_all(outgoing, 'col', split_axis=0, concat_axis=0, tiled=True)  86.7 us
    ppermute x6, waiting for transfers between devices, local(): moved = lax.ppermute(hidden, 'row', pairs)  41.5 us
    all_to_all x2, waiting for transfers between devices, local(): lax.all_to_all(result, 'col', split_axis=0, concat_axis=0, tiled=True)  39.6 us
    all_gather x2, waiting for transfers between devices, local(): rows = lax.all_gather(arrived, 'row', axis=0, tiled=False)  21.6 us
    all_to_all x1, blocking collectives, local(): lax.all_to_all(combined, 'row', split_axis=0, concat_axis=2, tiled=True)  18 us
    dot_general x2, matrix products, local(): jnp.einsum('npak,aku->npu', rows, gate_w, preferred_element_type=jnp.floa...  12.3 us
    all_to_all x2, starting transfers between devices, local(): lax.all_to_all(result, 'col', split_axis=0, concat_axis=0, tiled=True)  11.9 us
    ppermute x6, starting transfers between devices, local(): moved = lax.ppermute(hidden, 'row', pairs)  11 us
  transfers between devices with their start and end apart: 13, of which 7 were waited for; matrix products, arithmetic and copies ran while one was open for 15% of the time, Pallas kernels for 0%

profile of v9, /device:TPU:4, one launch (start us, length us, event | category | flops | bytes accessed | tf_op | source)
XLA Modules:
  0.0 326.2 jit_solution(17489950806816091429)
XLA Ops:
  6.5 0.9 copy.126
  7.8 0.6 reduce-window.6
  8.9 0.7 fusion.77
  10.0 2.6 convolution_convert_fusion.1
  12.6 2.3 reshape.130
  14.9 40.9 %all_to_all.35 = bf16[64,64,128]{2,1,0:T(8,128)(2,1)} all-to-all(bf16[64,64,128]{2,1,0:T(8,128)(2,1)} %reshape.130), channel_id=1, replica_groups=mesh['row'=4,'col'=64] {'col'}, dimensions={0} | all-to-all | bytes 2097152 | tf_op jit(solution)/shard_map/all_to_all | solution.py:51
  56.0 3.1 collective-permute-start
  59.0 0.6 collective-permute-start.1
  59.7 1.0 collective-permute-start.2
  61.0 2.9 convolution_convert_fusion
  63.9 3.8 %reshape.129 = bf16[64,96,128]{2,1,0:T(8,128)(2,1)} reshape(bf16[192,4096]{1,0:T(8,128)(2,1)} %convolution_convert_fusion) | data formatting | bytes 3145728 | tf_op jit(solution)/shard_map/reshape | solution.py:48
  67.8 45.8 %all_to_all.36 = bf16[64,96,128]{2,1,0:T(8,128)(2,1)} all-to-all(bf16[64,96,128]{2,1,0:T(8,128)(2,1)} %reshape.129), channel_id=1, replica_groups=mesh['row'=4,'col'=64] {'col'}, dimensions={0} | all-to-all | bytes 3145728 | tf_op jit(solution)/shard_map/all_to_all | solution.py:51
  113.7 5.6 %fusion.22 = f32[512,384]{1,0:T(8,128)S(1)} fusion(bf16[32,128,384]{2,1,0:T(8,128)(2,1)} %bitcast.140, bf16[512,32,128]{2,1,0:T(8,128)(2,1)} %bitcast.138), kind=kOutput, calls=%fused_computation.20 | convolution fusion | flops 1610612736 | bytes 8126464 | tf_op jit(solution)/shard_map/npak,aku->npu/dot_general | solution.py:57
  119.3 2.4 fusion.31
  121.7 2.0 collective-permute-start.7
  124.2 1.2 collective-permute-start.6
  125.4 2.0 collective-permute-start.8
  127.5 0.7 fusion.51
  128.2 15.7 %collective-permute-done.7 = bf16[512,384]{1,0:T(8,128)(2,1)} collective-permute-done((bf16[512,384]{1,0:T(8,128)(2,1)S(1)}, bf16[512,384]{1,0:T(8,128)(2,1)}, u32[]{:S(2)}, u32[]{:S(2)}) %collective-permute-start.7) | collective-permute-done | bytes 393248 | tf_op jit(solution)/shard_map/ppermute | solution.py:76
  143.8 1.7 fusion.43
  145.5 11.7 %collective-permute-done.6 = bf16[512,384]{1,0:T(8,128)(2,1)S(1)} collective-permute-done((bf16[512,384]{1,0:T(8,128)(2,1)S(1)}, bf16[512,384]{1,0:T(8,128)(2,1)S(1)}, u32[]{:S(2)}, u32[]{:S(2)}) %collective-permute-start.6) | collective-permute-done | bytes 393248 | tf_op jit(solution)/shard_map/ppermute | solution.py:76
  157.3 0.7 fusion.47
  158.1 1.7 add_convert_fusion.1
  159.8 2.3 reshape.133
  162.1 3.4 %copy.193 = bf16[4,64,2,1024]{3,2,0,1:T(2,128)(2,1)} copy(bf16[4,64,2,1024]{3,2,1,0:T(2,128)(2,1)} %reshape.133) | data formatting | bytes 2097152 | tf_op jit(solution)/shard_map/reshape | solution.py:79
  165.5 5.6 %all-to-all-start.2 = ((bf16[64,4,2,1024]{3,2,1,0:T(2,128)(2,1)}), bf16[64,4,2,1024]{3,2,1,0:T(2,128)(2,1)}, u32[]{:S(2)}, u32[]{:S(2)}) async-start(bf16[64,4,2,1024]{3,2,1,0:T(2,128)(2,1)} %bitcast.123), calls=%async_computation.2 | async-start | bytes 2097152 | tf_op jit(solution)/shard_map/all_to_all | solution.py:82
  171.1 21.6 %all-gather.5.cloned.1.call-done = bf16[256,96,128]{2,1,0:T(8,128)(2,1)} async-done(((bf16[64,96,128]{2,1,0:T(8,128)(2,1)}), bf16[256,96,128]{2,1,0:T(8,128)(2,1)}) %all-gather.5.cloned.1.call-update) | async-done | bytes 6291472 | tf_op jit(solution)/shard_map/all_gather | solution.py:53
  192.7 6.7 %fusion.10 = f32[768,384]{1,0:T(8,128)S(1)} fusion(bf16[32,128,384]{2,1,0:T(8,128)(2,1)} %bitcast.141, bf16[768,32,128]{2,1,0:T(8,128)(2,1)} %bitcast.136), kind=kOutput, calls=%fused_computation.16 | convolution fusion | flops 2415919104 | bytes 10616832 | tf_op jit(solution)/shard_map/npak,aku->npu/dot_general | solution.py:57
  199.4 4.4 %fusion.19 = bf16[768,384]{1,0:T(8,128)(2,1)} fusion(bf16[32,128,384]{2,1,0:T(8,128)(2,1)S(1)} %bitcast.143, bf16[768,32,128]{2,1,0:T(8,128)(2,1)S(1)} %bitcast.137, f32[768,384]{1,0:T(8,128)S(1)} %fusion.10), kind=kOutput, calls=%fused_computation.19 | convolution fusion | flops 2417688576 | bytes 11206656 | tf_op jit(solution)/shard_map/npak,aku->npu/dot_general | solution.py:58
  203.8 2.5 collective-permute-start.4
  206.7 0.8 copy.142
  207.5 4.6 %convolution_bitcast_fusion = f32[4,128,1024]{2,1,0:T(8,128)} fusion(bf16[64,4,2,1024]{3,2,1,0:T(2,128)(2,1)} %all-to-all-done.2, f32[4,128,64,2]{1,3,2,0:T(2,128)} %bitcast.127), kind=kOutput, calls=%fused_computation.14 | convolution fusion | flops 805306368 | bytes 3407872 | tf_op jit(solution)/shard_map/rtep,erpf->rtf/dot_general | solution.py:86
  212.1 0.6 collective-permute-start.3
  212.8 2.6 collective-permute-start.5
  215.4 2.1 fusion.53
  217.5 4.4 %collective-permute-done.4 = bf16[768,384]{1,0:T(8,128)(2,1)} collective-permute-done((bf16[768,384]{1,0:T(8,128)(2,1)}, bf16[768,384]{1,0:T(8,128)(2,1)}, u32[]{:S(2)}, u32[]{:S(2)}) %collective-permute-start.4) | collective-permute-done | bytes 589856 | tf_op jit(solution)/shard_map/ppermute | solution.py:76
  221.8 2.0 fusion.45
  223.9 9.6 %collective-permute-done.3 = bf16[768,384]{1,0:T(8,128)(2,1)S(1)} collective-permute-done((bf16[768,384]{1,0:T(8,128)(2,1)}, bf16[768,384]{1,0:T(8,128)(2,1)S(1)}, u32[]{:S(2)}, u32[]{:S(2)}) %collective-permute-start.3) | collective-permute-done | bytes 589856 | tf_op jit(solution)/shard_map/ppermute | solution.py:76
  233.5 1.0 fusion.49
  234.4 2.2 add_convert_fusion
  236.7 5.1 %reshape.131 = bf16[4,64,3,1024]{3,2,1,0:T(4,128)(2,1)} reshape(bf16[768,1024]{1,0:T(8,128)(2,1)} %add_convert_fusion) | data formatting | bytes 3145728 | tf_op jit(solution)/shard_map/reshape | solution.py:79
  241.8 4.8 %copy.151 = bf16[64,4,3,1024]{3,1,2,0:T(4,128)(2,1)} copy(bf16[64,4,3,1024]{3,2,0,1:T(4,128)(2,1)} %bitcast.122) | data formatting | bytes 3145728 | tf_op jit(solution)/shard_map/optimization_barrier | solution.py:81
  246.6 6.3 %all-to-all-start.3 = ((bf16[64,4,3,1024]{3,1,2,0:T(4,128)(2,1)}), bf16[64,4,3,1024]{3,1,2,0:T(4,128)(2,1)}, u32[]{:S(2)}, u32[]{:S(2)}) async-start(bf16[64,4,3,1024]{3,1,2,0:T(4,128)(2,1)} %copy.151), calls=%async_computation.3 | async-start | bytes 3145728 | tf_op jit(solution)/shard_map/all_to_all | solution.py:82
  253.3 39.6 %all-to-all-done.3 = bf16[64,4,3,1024]{3,1,2,0:T(4,128)(2,1)} async-done(((bf16[64,4,3,1024]{3,1,2,0:T(4,128)(2,1)}), bf16[64,4,3,1024]{3,1,2,0:T(4,128)(2,1)}, u32[]{:S(2)}, u32[]{:S(2)}) %all-to-all-start.3) | async-done | bytes 1572896 | tf_op jit(solution)/shard_map/all_to_all | solution.py:82
  292.9 3.9 %fusion.8 = bf16[4,128,1024]{2,1,0:T(8,128)(2,1)S(1)} fusion(f32[4,128,1024]{2,1,0:T(8,128)} %convolution_bitcast_fusion, bf16[64,4,3,1024]{3,1,2,0:T(4,128)(2,1)} %all-to-all-done.3, f32[4,128,64,3]{1,0,3,2:T(4,128)S(1)} %bitcast.126), kind=kOutput, calls=%fused_computation.12 | convolution fusion | flops 1209008128 | bytes 5111808 | tf_op jit(solution)/shard_map/rtep,erpf->rtf/dot_general | solution.py:86
  296.8 18.0 %all_to_all.37 = bf16[4,128,1024]{2,1,0:T(8,128)(2,1)} all-to-all(bf16[4,128,1024]{2,1,0:T(8,128)(2,1)S(1)} %fusion.8), channel_id=1, replica_groups=mesh['row'=4,'col'=64] {'row'}, dimensions={0} | all-to-all | bytes 2097152 | tf_op jit(solution)/shard_map/all_to_all | solution.py:91
  314.8 2.3 copy.154
  317.1 2.3 copy.155
  (55 shorter events, 3.1 us)
Async XLA Ops:
  6.5 120.9 %copy-start = (bf16[1,1536,1024]{2,1,0:T(8,128)(2,1)S(1)}, bf16[1,1536,1024]{2,1,0:T(8,128)(2,1)}, u32[]{:S(2)}) copy-start(bf16[1,1536,1024]{2,1,0:T(8,128)(2,1)} %param.11) | copy-start | bytes 9437188
  6.5 107.1 %all-gather.7.cloned.1.call-start = ((), (), s32[]{:S(2)}) async-start(), calls=%async_computation.6 | async-start | bytes 5242880 | tf_op jit(solution)/shard_map/all_gather | solution.py:53
  12.6 43.3 %copy-start.1 = (f32[128,2]{0,1:T(2,128)S(1)}, f32[128,2]{0,1:T(2,128)}, u32[]{:S(2)}) copy-start(f32[128,2]{0,1:T(2,128)} %param.8) | copy-start | bytes 3076
  55.9 136.8 %all-gather.5.cloned.1.call-start = ((), (), s32[]{:S(2)}) async-start(), calls=%async_computation.5 | async-start | bytes 7864320 | tf_op jit(solution)/shard_map/all_gather | solution.py:53
  56.0 11.8 %collective-permute-start = (f32[128,4]{0,1:T(4,128)S(1)}, f32[128,4]{0,1:T(4,128)S(1)}, u32[]{:S(2)}, u32[]{:S(2)}) collective-permute-start(f32[128,4]{0,1:T(4,128)S(1)} %pad_maximum_fusion), channel_id=1, source_target_pairs={{0,192},{64,0},{128,64},{192,128},{1,193},{65,1},{129,65},{193,129... | collective-permute-start | bytes 6152 | tf_op jit(solution)/shard_map/ppermute | solution.py:30
  59.0 8.7 %collective-permute-start.1 = (f32[128,4]{0,1:T(4,128)S(1)}, f32[128,4]{0,1:T(4,128)S(1)}, u32[]{:S(2)}, u32[]{:S(2)}) collective-permute-start(f32[128,4]{0,1:T(4,128)S(1)} %pad_maximum_fusion), channel_id=1, source_target_pairs={{0,128},{64,192},{128,0},{192,64},{1,129},{65,193},{129,1},{193,65... | collective-permute-start | bytes 6152 | tf_op jit(solution)/shard_map/ppermute | solution.py:30
  59.7 8.1 %collective-permute-start.2 = (f32[128,4]{0,1:T(4,128)S(1)}, f32[128,4]{0,1:T(4,128)S(1)}, u32[]{:S(2)}, u32[]{:S(2)}) collective-permute-start(f32[128,4]{0,1:T(4,128)S(1)} %pad_maximum_fusion), channel_id=1, source_target_pairs={{0,64},{64,128},{128,192},{192,0},{1,65},{65,129},{129,193},{193,1... | collective-permute-start | bytes 6152 | tf_op jit(solution)/shard_map/ppermute | solution.py:30
  113.6 5.7 %copy-start.4 = (bf16[256,64,128]{2,1,0:T(8,128)(2,1)S(1)}, bf16[256,64,128]{2,1,0:T(8,128)(2,1)}, u32[]{:S(2)}) copy-start(bf16[256,64,128]{2,1,0:T(8,128)(2,1)} %all-gather.7.cloned.1.call-done) | copy-start | bytes 12582916
  113.6 5.7 %copy-start.5 = (bf16[1,4096,384]{2,1,0:T(8,128)(2,1)S(1)}, bf16[1,4096,384]{2,1,0:T(8,128)(2,1)}, u32[]{:S(2)}) copy-start(bf16[1,4096,384]{2,1,0:T(8,128)(2,1)} %param.10) | copy-start | bytes 9437188
  121.7 22.2 %collective-permute-start.7 = (bf16[512,384]{1,0:T(8,128)(2,1)S(1)}, bf16[512,384]{1,0:T(8,128)(2,1)}, u32[]{:S(2)}, u32[]{:S(2)}) collective-permute-start(bf16[512,384]{1,0:T(8,128)(2,1)S(1)} %fusion.31), channel_id=1, source_target_pairs={{0,128},{64,192},{128,0},{192,64},{1,129},{65,193},{129,1},{193,65... | collective-permute-start | bytes 1179656 | tf_op jit(solution)/shard_map/ppermute | solution.py:76
  124.2 33.1 %collective-permute-start.6 = (bf16[512,384]{1,0:T(8,128)(2,1)S(1)}, bf16[512,384]{1,0:T(8,128)(2,1)S(1)}, u32[]{:S(2)}, u32[]{:S(2)}) collective-permute-start(bf16[512,384]{1,0:T(8,128)(2,1)S(1)} %fusion.31), channel_id=1, source_target_pairs={{0,64},{64,128},{128,192},{192,0},{1,65},{65,129},{129,193},{193,1... | collective-permute-start | bytes 1179656 | tf_op jit(solution)/shard_map/ppermute | solution.py:76
  125.4 32.7 %collective-permute-start.8 = (bf16[512,384]{1,0:T(8,128)(2,1)S(1)}, bf16[512,384]{1,0:T(8,128)(2,1)S(1)}, u32[]{:S(2)}, u32[]{:S(2)}) collective-permute-start(bf16[512,384]{1,0:T(8,128)(2,1)S(1)} %fusion.31), channel_id=1, source_target_pairs={{0,192},{64,0},{128,64},{192,128},{1,193},{65,1},{129,65},{193,129... | collective-permute-start | bytes 1179656 | tf_op jit(solution)/shard_map/ppermute | solution.py:76
  165.5 42.0 %all-to-all-start.2 = ((bf16[64,4,2,1024]{3,2,1,0:T(2,128)(2,1)}), bf16[64,4,2,1024]{3,2,1,0:T(2,128)(2,1)}, u32[]{:S(2)}, u32[]{:S(2)}) async-start(bf16[64,4,2,1024]{3,2,1,0:T(2,128)(2,1)} %bitcast.123), calls=%async_computation.2 | async-start | bytes 2097152 | tf_op jit(solution)/shard_map/all_to_all | solution.py:82
  192.7 6.7 %copy-start.3 = (bf16[256,96,128]{2,1,0:T(8,128)(2,1)S(1)}, bf16[256,96,128]{2,1,0:T(8,128)(2,1)}, u32[]{:S(2)}) copy-start(bf16[256,96,128]{2,1,0:T(8,128)(2,1)} %all-gather.5.cloned.1.call-done) | copy-start | bytes 18874372
  192.7 6.7 %copy-start.6 = (bf16[1,4096,384]{2,1,0:T(8,128)(2,1)S(1)}, bf16[1,4096,384]{2,1,0:T(8,128)(2,1)}, u32[]{:S(2)}) copy-start(bf16[1,4096,384]{2,1,0:T(8,128)(2,1)} %param.10) | copy-start | bytes 9437188
  199.4 6.9 %copy-start.2 = (f32[128]{0:T(128)S(1)}, f32[128]{0:T(128)}, u32[]{:S(2)}) copy-start(f32[128]{0:T(128)} %convert_element_type.56) | copy-start | bytes 1540
  203.8 18.0 %collective-permute-start.4 = (bf16[768,384]{1,0:T(8,128)(2,1)}, bf16[768,384]{1,0:T(8,128)(2,1)}, u32[]{:S(2)}, u32[]{:S(2)}) collective-permute-start(bf16[768,384]{1,0:T(8,128)(2,1)} %fusion.19), channel_id=1, source_target_pairs={{0,128},{64,192},{128,0},{192,64},{1,129},{65,193},{129,1},{193,65... | collective-permute-start | bytes 1769480 | tf_op jit(solution)/shard_map/ppermute | solution.py:76
  212.1 21.3 %collective-permute-start.3 = (bf16[768,384]{1,0:T(8,128)(2,1)}, bf16[768,384]{1,0:T(8,128)(2,1)S(1)}, u32[]{:S(2)}, u32[]{:S(2)}) collective-permute-start(bf16[768,384]{1,0:T(8,128)(2,1)} %fusion.19), channel_id=1, source_target_pairs={{0,64},{64,128},{128,192},{192,0},{1,65},{65,129},{129,193},{193,1... | collective-permute-start | bytes 1769480 | tf_op jit(solution)/shard_map/ppermute | solution.py:76
  212.8 21.6 %collective-permute-start.5 = (bf16[768,384]{1,0:T(8,128)(2,1)}, bf16[768,384]{1,0:T(8,128)(2,1)S(1)}, u32[]{:S(2)}, u32[]{:S(2)}) collective-permute-start(bf16[768,384]{1,0:T(8,128)(2,1)} %fusion.19), channel_id=1, source_target_pairs={{0,192},{64,0},{128,64},{192,128},{1,193},{65,1},{129,65},{193,129... | collective-permute-start | bytes 1769480 | tf_op jit(solution)/shard_map/ppermute | solution.py:76
  246.6 46.3 %all-to-all-start.3 = ((bf16[64,4,3,1024]{3,1,2,0:T(4,128)(2,1)}), bf16[64,4,3,1024]{3,1,2,0:T(4,128)(2,1)}, u32[]{:S(2)}, u32[]{:S(2)}) async-start(bf16[64,4,3,1024]{3,1,2,0:T(4,128)(2,1)} %copy.151), calls=%async_computation.3 | async-start | bytes 3145728 | tf_op jit(solution)/shard_map/all_to_all | solution.py:82
Sparse Core Ops, SparseCore 0:
  56.0 47.4 all-gather.6
  113.7 78.8 all-gather.4

commit v10 on v5

--- a/solution.py
+++ b/solution.py
@@ -85,8 +85,8 @@
             precision=lax.Precision.HIGHEST, preferred_element_type=jnp.float32,
         )
     combined = combined.astype(jnp.bfloat16)
-    home = lax.all_to_all(combined, "row", split_axis=0, concat_axis=2, tiled=True)
-    return home.reshape(token_count, width)
+    home = lax.all_to_all(combined, "row", split_axis=0, concat_axis=0, tiled=True)
+    return jnp.concatenate([home[j] for j in range(groups)], axis=1)
 
 
 def solution(mesh):

time: 326 us -> 322 us (0.988)
  local copies, waits for them, and re-layouts: 29.3 us -> 24.8 us
where the time goes in v10:
time: 322 us; the launch traced here: 321 us
  waiting for transfers between devices  105 us (33%)
  blocking collectives  104 us (32%)
  matrix products  42.4 us (13%)
  starting transfers between devices  27.7 us (9%)
  local copies, waits for them, and re-layouts  24.8 us (8%)
  between operations  13.7 us (4%)
  other arithmetic  3.37 us (1%)
    all_to_all x2, blocking collectives, local(): lax.all_to_all(outgoing, 'col', split_axis=0, concat_axis=0, tiled=True)  86.7 us
    ppermute x6, waiting for transfers between devices, local(): moved = lax.ppermute(hidden, 'row', pairs)  51.1 us
    all_to_all x2, waiting for transfers between devices, local(): lax.all_to_all(result, 'col', split_axis=0, concat_axis=0, tiled=True)  33.7 us
    all_gather x2, waiting for transfers between devices, local(): rows = lax.all_gather(arrived, 'row', axis=0, tiled=False)  20.6 us
    all_to_all x1, blocking collectives, local(): lax.all_to_all(combined, 'row', split_axis=0, concat_axis=0, tiled=True)  17.4 us
    dot_general x2, matrix products, local(): jnp.einsum('npak,aku->npu', rows, gate_w, preferred_element_type=jnp.floa...  12.4 us
    all_to_all x2, starting transfers between devices, local(): lax.all_to_all(result, 'col', split_axis=0, concat_axis=0, tiled=True)  11.9 us
    ppermute x6, starting transfers between devices, local(): moved = lax.ppermute(hidden, 'row', pairs)  11.1 us
  transfers between devices with their start and end apart: 13, of which 6 were waited for; matrix products, arithmetic and copies ran while one was open for 18% of the time, Pallas kernels for 0%

profile of v10, /device:TPU:4, one launch (start us, length us, event | category | flops | bytes accessed | tf_op | source)
XLA Modules:
  0.0 321.4 jit_solution(4089328952477078429)
XLA Ops:
  6.5 0.9 copy.118
  7.8 0.6 reduce-window.6
  8.9 0.7 fusion.78
  10.0 2.6 convolution_convert_fusion.1
  12.6 2.3 reshape.126
  14.9 40.9 %all_to_all.25 = bf16[64,64,128]{2,1,0:T(8,128)(2,1)} all-to-all(bf16[64,64,128]{2,1,0:T(8,128)(2,1)} %reshape.126), channel_id=1, replica_groups=mesh['row'=4,'col'=64] {'col'}, dimensions={0} | all-to-all | bytes 2097152 | tf_op jit(solution)/shard_map/all_to_all | solution.py:51
  56.0 3.1 collective-permute-start
  59.0 0.6 collective-permute-start.1
  59.7 1.0 collective-permute-start.2
  61.0 2.9 convolution_convert_fusion
  63.9 3.8 %reshape.125 = bf16[64,96,128]{2,1,0:T(8,128)(2,1)} reshape(bf16[192,4096]{1,0:T(8,128)(2,1)} %convolution_convert_fusion) | data formatting | bytes 3145728 | tf_op jit(solution)/shard_map/reshape | solution.py:48
  67.8 45.8 %all_to_all.26 = bf16[64,96,128]{2,1,0:T(8,128)(2,1)} all-to-all(bf16[64,96,128]{2,1,0:T(8,128)(2,1)} %reshape.125), channel_id=1, replica_groups=mesh['row'=4,'col'=64] {'col'}, dimensions={0} | all-to-all | bytes 3145728 | tf_op jit(solution)/shard_map/all_to_all | solution.py:51
  113.7 5.6 %fusion.22 = f32[512,384]{1,0:T(8,128)S(1)} fusion(bf16[32,128,384]{2,1,0:T(8,128)(2,1)} %bitcast.142, bf16[512,32,128]{2,1,0:T(8,128)(2,1)} %bitcast.140), kind=kOutput, calls=%fused_computation.19 | convolution fusion | flops 1610612736 | bytes 8126464 | tf_op jit(solution)/shard_map/npak,aku->npu/dot_general | solution.py:57
  119.3 2.4 fusion.31
  121.7 2.0 collective-permute-start.3
  123.7 1.8 collective-permute-start.4
  125.5 1.3 collective-permute-start.5
  126.7 0.7 fusion.54
  127.5 15.7 %collective-permute-done.3 = bf16[512,384]{1,0:T(8,128)(2,1)} collective-permute-done((bf16[512,384]{1,0:T(8,128)(2,1)S(1)}, bf16[512,384]{1,0:T(8,128)(2,1)}, u32[]{:S(2)}, u32[]{:S(2)}) %collective-permute-start.3) | collective-permute-done | bytes 393248 | tf_op jit(solution)/shard_map/ppermute | solution.py:75
  143.2 1.7 fusion.50
  144.9 13.8 %collective-permute-done.4 = bf16[512,384]{1,0:T(8,128)(2,1)S(1)} collective-permute-done((bf16[512,384]{1,0:T(8,128)(2,1)S(1)}, bf16[512,384]{1,0:T(8,128)(2,1)S(1)}, u32[]{:S(2)}, u32[]{:S(2)}) %collective-permute-start.4) | collective-permute-done | bytes 393248 | tf_op jit(solution)/shard_map/ppermute | solution.py:75
  158.7 0.7 fusion.46
  159.4 1.7 add_convert_fusion.1
  161.2 2.3 reshape.128
  163.4 3.4 %copy.183 = bf16[4,64,2,1024]{3,2,0,1:T(2,128)(2,1)} copy(bf16[4,64,2,1024]{3,2,1,0:T(2,128)(2,1)} %reshape.128) | data formatting | bytes 2097152 | tf_op jit(solution)/shard_map/reshape | solution.py:78
  166.8 5.6 %all-to-all-start.1 = ((bf16[64,4,2,1024]{3,2,1,0:T(2,128)(2,1)}), bf16[64,4,2,1024]{3,2,1,0:T(2,128)(2,1)}, u32[]{:S(2)}, u32[]{:S(2)}) async-start(bf16[64,4,2,1024]{3,2,1,0:T(2,128)(2,1)} %bitcast.127), calls=%async_computation.1 | async-start | bytes 2097152 | tf_op jit(solution)/shard_map/all_to_all | solution.py:79
  172.4 20.5 %all-gather.7.cloned.1.call-done = bf16[256,96,128]{2,1,0:T(8,128)(2,1)} async-done(((bf16[64,96,128]{2,1,0:T(8,128)(2,1)}), bf16[256,96,128]{2,1,0:T(8,128)(2,1)}) %all-gather.7.cloned.1.call-update) | async-done | bytes 6291472 | tf_op jit(solution)/shard_map/all_gather | solution.py:53
  192.9 6.7 %fusion.10 = f32[768,384]{1,0:T(8,128)S(1)} fusion(bf16[32,128,384]{2,1,0:T(8,128)(2,1)} %bitcast.143, bf16[768,32,128]{2,1,0:T(8,128)(2,1)} %bitcast.138), kind=kOutput, calls=%fused_computation.15 | convolution fusion | flops 2415919104 | bytes 10616832 | tf_op jit(solution)/shard_map/npak,aku->npu/dot_general | solution.py:57
  199.7 3.6 %fusion.19 = bf16[768,384]{1,0:T(8,128)(2,1)S(1)} fusion(bf16[32,128,384]{2,1,0:T(8,128)(2,1)S(1)} %bitcast.145, bf16[768,32,128]{2,1,0:T(8,128)(2,1)S(1)} %bitcast.139, f32[768,384]{1,0:T(8,128)S(1)} %fusion.10), kind=kOutput, calls=%fused_computation.18 | convolution fusion | flops 2417688576 | bytes 11206656 | tf_op jit(solution)/shard_map/npak,aku->npu/dot_general | solution.py:58
  203.2 2.8 collective-permute-start.7
  206.0 0.9 collective-permute-start.6
  206.8 2.4 collective-permute-start.8
  209.2 1.0 fusion.52
  210.2 10.8 %collective-permute-done.7 = bf16[768,384]{1,0:T(8,128)(2,1)S(1)} collective-permute-done((bf16[768,384]{1,0:T(8,128)(2,1)S(1)}, bf16[768,384]{1,0:T(8,128)(2,1)S(1)}, u32[]{:S(2)}, u32[]{:S(2)}) %collective-permute-start.7) | collective-permute-done | bytes 589856 | tf_op jit(solution)/shard_map/ppermute | solution.py:75
  221.1 1.0 fusion.44
  222.0 10.7 %collective-permute-done.6 = bf16[768,384]{1,0:T(8,128)(2,1)S(1)} collective-permute-done((bf16[768,384]{1,0:T(8,128)(2,1)S(1)}, bf16[768,384]{1,0:T(8,128)(2,1)S(1)}, u32[]{:S(2)}, u32[]{:S(2)}) %collective-permute-start.6) | collective-permute-done | bytes 589856 | tf_op jit(solution)/shard_map/ppermute | solution.py:75
  232.7 1.0 fusion.48
  233.7 2.2 add_convert_fusion
  235.9 5.1 %reshape.130 = bf16[4,64,3,1024]{3,2,1,0:T(4,128)(2,1)} reshape(bf16[768,1024]{1,0:T(8,128)(2,1)} %add_convert_fusion) | data formatting | bytes 3145728 | tf_op jit(solution)/shard_map/reshape | solution.py:78
  241.0 4.8 %copy.143 = bf16[64,4,3,1024]{3,1,2,0:T(4,128)(2,1)} copy(bf16[64,4,3,1024]{3,2,0,1:T(4,128)(2,1)} %bitcast.126) | data formatting | bytes 3145728 | tf_op jit(solution)/shard_map/transpose | solution.py:78
  245.8 6.4 %all-to-all-start.3 = ((bf16[64,4,3,1024]{3,1,2,0:T(4,128)(2,1)}), bf16[64,4,3,1024]{3,1,2,0:T(4,128)(2,1)}, u32[]{:S(2)}, u32[]{:S(2)}) async-start(bf16[64,4,3,1024]{3,1,2,0:T(4,128)(2,1)} %copy.143), calls=%async_computation.3 | async-start | bytes 3145728 | tf_op jit(solution)/shard_map/all_to_all | solution.py:79
  252.2 0.3 select_reduce_fusion.1
  252.6 0.8 copy.132
  253.8 4.6 %fusion.34 = f32[4,128,1024,1]{2,1,3,0:T(8,128)} fusion(bf16[64,4,2,1024]{3,2,1,0:T(2,128)(2,1)} %all-to-all-done.1, f32[4,128,64,2]{1,3,2,0:T(2,128)} %bitcast.129), kind=kOutput, calls=%fused_computation.24 | convolution fusion | flops 805306368 | bytes 3407872 | tf_op jit(solution)/shard_map/rtep,erpf->rtf/dot_general | solution.py:83
  258.5 33.7 %all-to-all-done.3 = bf16[64,4,3,1024]{3,1,2,0:T(4,128)(2,1)} async-done(((bf16[64,4,3,1024]{3,1,2,0:T(4,128)(2,1)}), bf16[64,4,3,1024]{3,1,2,0:T(4,128)(2,1)}, u32[]{:S(2)}, u32[]{:S(2)}) %all-to-all-start.3) | async-done | bytes 1572896 | tf_op jit(solution)/shard_map/all_to_all | solution.py:79
  292.2 3.9 %fusion.8 = bf16[4,128,1024]{2,1,0:T(8,128)(2,1)S(1)} fusion(f32[4,128,1024,1]{2,1,3,0:T(8,128)} %fusion.34, bf16[64,4,3,1024]{3,1,2,0:T(4,128)(2,1)} %all-to-all-done.3, f32[4,128,64,3]{1,0,3,2:T(4,128)S(1)} %bitcast.128), kind=kOutput, calls=%fused_computation.12 | convolution fusion | flops 1209008128 | bytes 5111808 | tf_op jit(solution)/shard_map/rtep,erpf->rtf/dot_general | solution.py:83
  296.1 17.4 %all_to_all.27 = bf16[4,128,1024]{2,1,0:T(8,128)(2,1)S(1)} all-to-all(bf16[4,128,1024]{2,1,0:T(8,128)(2,1)S(1)} %fusion.8), channel_id=1, replica_groups=mesh['row'=4,'col'=64] {'row'}, dimensions={0} | all-to-all | bytes 2097152 | tf_op jit(solution)/shard_map/all_to_all | solution.py:88
  313.5 1.0 pad_maximum_fusion
  (53 shorter events, 2.2 us)
Async XLA Ops:
  6.5 120.2 %copy-start = (bf16[1,1536,1024]{2,1,0:T(8,128)(2,1)S(1)}, bf16[1,1536,1024]{2,1,0:T(8,128)(2,1)}, u32[]{:S(2)}) copy-start(bf16[1,1536,1024]{2,1,0:T(8,128)(2,1)} %param.11) | copy-start | bytes 9437188
  6.5 107.1 %all-gather.5.cloned.1.call-start = ((), (), s32[]{:S(2)}) async-start(), calls=%async_computation.5 | async-start | bytes 5242880 | tf_op jit(solution)/shard_map/all_gather | solution.py:53
  12.6 43.3 %copy-start.1 = (f32[128,2]{0,1:T(2,128)S(1)}, f32[128,2]{0,1:T(2,128)}, u32[]{:S(2)}) copy-start(f32[128,2]{0,1:T(2,128)} %param.8) | copy-start | bytes 3076
  55.9 137.1 %all-gather.7.cloned.1.call-start = ((), (), s32[]{:S(2)}) async-start(), calls=%async_computation.6 | async-start | bytes 7864320 | tf_op jit(solution)/shard_map/all_gather | solution.py:53
  56.0 11.8 %collective-permute-start = (f32[128,4]{0,1:T(4,128)S(1)}, f32[128,4]{0,1:T(4,128)S(1)}, u32[]{:S(2)}, u32[]{:S(2)}) collective-permute-start(f32[128,4]{0,1:T(4,128)S(1)} %pad_maximum_fusion.1), channel_id=1, source_target_pairs={{0,192},{64,0},{128,64},{192,128},{1,193},{65,1},{129,65},{193,129... | collective-permute-start | bytes 6152 | tf_op jit(solution)/shard_map/ppermute | solution.py:30
  59.0 8.7 %collective-permute-start.1 = (f32[128,4]{0,1:T(4,128)S(1)}, f32[128,4]{0,1:T(4,128)S(1)}, u32[]{:S(2)}, u32[]{:S(2)}) collective-permute-start(f32[128,4]{0,1:T(4,128)S(1)} %pad_maximum_fusion.1), channel_id=1, source_target_pairs={{0,128},{64,192},{128,0},{192,64},{1,129},{65,193},{129,1},{193,65... | collective-permute-start | bytes 6152 | tf_op jit(solution)/shard_map/ppermute | solution.py:30
  59.7 8.1 %collective-permute-start.2 = (f32[128,4]{0,1:T(4,128)S(1)}, f32[128,4]{0,1:T(4,128)S(1)}, u32[]{:S(2)}, u32[]{:S(2)}) collective-permute-start(f32[128,4]{0,1:T(4,128)S(1)} %pad_maximum_fusion.1), channel_id=1, source_target_pairs={{0,64},{64,128},{128,192},{192,0},{1,65},{65,129},{129,193},{193,1... | collective-permute-start | bytes 6152 | tf_op jit(solution)/shard_map/ppermute | solution.py:30
  113.6 5.7 %copy-start.3 = (bf16[256,64,128]{2,1,0:T(8,128)(2,1)S(1)}, bf16[256,64,128]{2,1,0:T(8,128)(2,1)}, u32[]{:S(2)}) copy-start(bf16[256,64,128]{2,1,0:T(8,128)(2,1)} %all-gather.5.cloned.1.call-done) | copy-start | bytes 12582916
  113.6 5.7 %copy-start.4 = (bf16[1,4096,384]{2,1,0:T(8,128)(2,1)S(1)}, bf16[1,4096,384]{2,1,0:T(8,128)(2,1)}, u32[]{:S(2)}) copy-start(bf16[1,4096,384]{2,1,0:T(8,128)(2,1)} %param.10) | copy-start | bytes 9437188
  121.7 21.5 %collective-permute-start.3 = (bf16[512,384]{1,0:T(8,128)(2,1)S(1)}, bf16[512,384]{1,0:T(8,128)(2,1)}, u32[]{:S(2)}, u32[]{:S(2)}) collective-permute-start(bf16[512,384]{1,0:T(8,128)(2,1)S(1)} %fusion.31), channel_id=1, source_target_pairs={{0,64},{64,128},{128,192},{192,0},{1,65},{65,129},{129,193},{193,1... | collective-permute-start | bytes 1179656 | tf_op jit(solution)/shard_map/ppermute | solution.py:75
  123.7 35.0 %collective-permute-start.4 = (bf16[512,384]{1,0:T(8,128)(2,1)S(1)}, bf16[512,384]{1,0:T(8,128)(2,1)S(1)}, u32[]{:S(2)}, u32[]{:S(2)}) collective-permute-start(bf16[512,384]{1,0:T(8,128)(2,1)S(1)} %fusion.31), channel_id=1, source_target_pairs={{0,128},{64,192},{128,0},{192,64},{1,129},{65,193},{129,1},{193,65... | collective-permute-start | bytes 1179656 | tf_op jit(solution)/shard_map/ppermute | solution.py:75
  125.5 34.0 %collective-permute-start.5 = (bf16[512,384]{1,0:T(8,128)(2,1)S(1)}, bf16[512,384]{1,0:T(8,128)(2,1)S(1)}, u32[]{:S(2)}, u32[]{:S(2)}) collective-permute-start(bf16[512,384]{1,0:T(8,128)(2,1)S(1)} %fusion.31), channel_id=1, source_target_pairs={{0,192},{64,0},{128,64},{192,128},{1,193},{65,1},{129,65},{193,129... | collective-permute-start | bytes 1179656 | tf_op jit(solution)/shard_map/ppermute | solution.py:75
  166.8 79.0 %all-to-all-start.1 = ((bf16[64,4,2,1024]{3,2,1,0:T(2,128)(2,1)}), bf16[64,4,2,1024]{3,2,1,0:T(2,128)(2,1)}, u32[]{:S(2)}, u32[]{:S(2)}) async-start(bf16[64,4,2,1024]{3,2,1,0:T(2,128)(2,1)} %bitcast.127), calls=%async_computation.1 | async-start | bytes 2097152 | tf_op jit(solution)/shard_map/all_to_all | solution.py:79
  192.9 6.7 %copy-start.2 = (bf16[256,96,128]{2,1,0:T(8,128)(2,1)S(1)}, bf16[256,96,128]{2,1,0:T(8,128)(2,1)}, u32[]{:S(2)}) copy-start(bf16[256,96,128]{2,1,0:T(8,128)(2,1)} %all-gather.7.cloned.1.call-done) | copy-start | bytes 18874372
  192.9 6.7 %copy-start.5 = (bf16[1,4096,384]{2,1,0:T(8,128)(2,1)S(1)}, bf16[1,4096,384]{2,1,0:T(8,128)(2,1)}, u32[]{:S(2)}) copy-start(bf16[1,4096,384]{2,1,0:T(8,128)(2,1)} %param.10) | copy-start | bytes 9437188
  203.2 17.8 %collective-permute-start.7 = (bf16[768,384]{1,0:T(8,128)(2,1)S(1)}, bf16[768,384]{1,0:T(8,128)(2,1)S(1)}, u32[]{:S(2)}, u32[]{:S(2)}) collective-permute-start(bf16[768,384]{1,0:T(8,128)(2,1)S(1)} %fusion.19), channel_id=1, source_target_pairs={{0,128},{64,192},{128,0},{192,64},{1,129},{65,193},{129,1},{193,65... | collective-permute-start | bytes 1769480 | tf_op jit(solution)/shard_map/ppermute | solution.py:75
  206.0 26.7 %collective-permute-start.6 = (bf16[768,384]{1,0:T(8,128)(2,1)S(1)}, bf16[768,384]{1,0:T(8,128)(2,1)S(1)}, u32[]{:S(2)}, u32[]{:S(2)}) collective-permute-start(bf16[768,384]{1,0:T(8,128)(2,1)S(1)} %fusion.19), channel_id=1, source_target_pairs={{0,64},{64,128},{128,192},{192,0},{1,65},{65,129},{129,193},{193,1... | collective-permute-start | bytes 1769480 | tf_op jit(solution)/shard_map/ppermute | solution.py:75
  206.8 26.9 %collective-permute-start.8 = (bf16[768,384]{1,0:T(8,128)(2,1)S(1)}, bf16[768,384]{1,0:T(8,128)(2,1)S(1)}, u32[]{:S(2)}, u32[]{:S(2)}) collective-permute-start(bf16[768,384]{1,0:T(8,128)(2,1)S(1)} %fusion.19), channel_id=1, source_target_pairs={{0,192},{64,0},{128,64},{192,128},{1,193},{65,1},{129,65},{193,129... | collective-permute-start | bytes 1769480 | tf_op jit(solution)/shard_map/ppermute | solution.py:75
  245.8 46.4 %all-to-all-start.3 = ((bf16[64,4,3,1024]{3,1,2,0:T(4,128)(2,1)}), bf16[64,4,3,1024]{3,1,2,0:T(4,128)(2,1)}, u32[]{:S(2)}, u32[]{:S(2)}) async-start(bf16[64,4,3,1024]{3,1,2,0:T(4,128)(2,1)} %copy.143), calls=%async_computation.3 | async-start | bytes 3145728 | tf_op jit(solution)/shard_map/all_to_all | solution.py:79
Sparse Core Ops, SparseCore 0:
  56.0 47.4 all-gather.4
  113.7 79.1 all-gather.6

commit v11 on v10

--- a/solution.py
+++ b/solution.py
@@ -82,7 +82,7 @@
         weights = weights.reshape(groups, token_count, experts, span)
         combined = combined + jnp.einsum(
             "rtep,erpf->rtf", weights, back.astype(jnp.float32),
-            precision=lax.Precision.HIGHEST, preferred_element_type=jnp.float32,
+            precision=lax.Precision.HIGH, preferred_element_type=jnp.float32,
         )
     combined = combined.astype(jnp.bfloat16)
     home = lax.all_to_all(combined, "row", split_axis=0, concat_axis=0, tiled=True)

time: 322 us -> 322 us (level)
  no operation moved by 1% of the time
where the time goes in v11:
time: 322 us; the launch traced here: 321 us
  waiting for transfers between devices  106 us (33%)
  blocking collectives  104 us (32%)
  matrix products  41.8 us (13%)
  starting transfers between devices  27.7 us (9%)
  local copies, waits for them, and re-layouts  24.8 us (8%)
  between operations  13.7 us (4%)
  other arithmetic  3.37 us (1%)
    all_to_all x2, blocking collectives, local(): lax.all_to_all(outgoing, 'col', split_axis=0, concat_axis=0, tiled=True)  86.7 us
    ppermute x6, waiting for transfers between devices, local(): moved = lax.ppermute(hidden, 'row', pairs)  51.1 us
    all_to_all x2, waiting for transfers between devices, local(): lax.all_to_all(result, 'col', split_axis=0, concat_axis=0, tiled=True)  34 us
    all_gather x2, waiting for transfers between devices, local(): rows = lax.all_gather(arrived, 'row', axis=0, tiled=False)  20.6 us
    all_to_all x1, blocking collectives, local(): lax.all_to_all(combined, 'row', split_axis=0, concat_axis=0, tiled=True)  17.4 us
    dot_general x2, matrix products, local(): jnp.einsum('npak,aku->npu', rows, gate_w, preferred_element_type=jnp.floa...  12.4 us
    all_to_all x2, starting transfers between devices, local(): lax.all_to_all(result, 'col', split_axis=0, concat_axis=0, tiled=True)  11.9 us
    ppermute x6, starting transfers between devices, local(): moved = lax.ppermute(hidden, 'row', pairs)  11.1 us
  transfers between devices with their start and end apart: 13, of which 6 were waited for; matrix products, arithmetic and copies ran while one was open for 18% of the time, Pallas kernels for 0%

profile of v11, /device:TPU:4, one launch (start us, length us, event | category | flops | bytes accessed | tf_op | source)
XLA Modules:
  0.0 321.1 jit_solution(12049502986703657002)
XLA Ops:
  6.5 0.9 copy.118
  7.8 0.6 reduce-window.6
  8.9 0.7 fusion.78
  10.0 2.6 convolution_convert_fusion.1
  12.6 2.3 reshape.126
  14.9 40.9 %all_to_all.25 = bf16[64,64,128]{2,1,0:T(8,128)(2,1)} all-to-all(bf16[64,64,128]{2,1,0:T(8,128)(2,1)} %reshape.126), channel_id=1, replica_groups=mesh['row'=4,'col'=64] {'col'}, dimensions={0} | all-to-all | bytes 2097152 | tf_op jit(solution)/shard_map/all_to_all | solution.py:51
  56.0 3.1 collective-permute-start
  59.0 0.6 collective-permute-start.1
  59.7 1.0 collective-permute-start.2
  61.0 2.9 convolution_convert_fusion
  63.9 3.8 %reshape.125 = bf16[64,96,128]{2,1,0:T(8,128)(2,1)} reshape(bf16[192,4096]{1,0:T(8,128)(2,1)} %convolution_convert_fusion) | data formatting | bytes 3145728 | tf_op jit(solution)/shard_map/reshape | solution.py:48
  67.8 45.8 %all_to_all.26 = bf16[64,96,128]{2,1,0:T(8,128)(2,1)} all-to-all(bf16[64,96,128]{2,1,0:T(8,128)(2,1)} %reshape.125), channel_id=1, replica_groups=mesh['row'=4,'col'=64] {'col'}, dimensions={0} | all-to-all | bytes 3145728 | tf_op jit(solution)/shard_map/all_to_all | solution.py:51
  113.7 5.6 %fusion.22 = f32[512,384]{1,0:T(8,128)S(1)} fusion(bf16[32,128,384]{2,1,0:T(8,128)(2,1)} %bitcast.142, bf16[512,32,128]{2,1,0:T(8,128)(2,1)} %bitcast.140), kind=kOutput, calls=%fused_computation.19 | convolution fusion | flops 1610612736 | bytes 8126464 | tf_op jit(solution)/shard_map/npak,aku->npu/dot_general | solution.py:57
  119.3 2.4 fusion.31
  121.7 2.0 collective-permute-start.3
  123.7 1.8 collective-permute-start.4
  125.5 1.3 collective-permute-start.5
  126.7 0.7 fusion.54
  127.5 15.7 %collective-permute-done.3 = bf16[512,384]{1,0:T(8,128)(2,1)} collective-permute-done((bf16[512,384]{1,0:T(8,128)(2,1)S(1)}, bf16[512,384]{1,0:T(8,128)(2,1)}, u32[]{:S(2)}, u32[]{:S(2)}) %collective-permute-start.3) | collective-permute-done | bytes 393248 | tf_op jit(solution)/shard_map/ppermute | solution.py:75
  143.2 1.7 fusion.50
  144.9 13.8 %collective-permute-done.4 = bf16[512,384]{1,0:T(8,128)(2,1)S(1)} collective-permute-done((bf16[512,384]{1,0:T(8,128)(2,1)S(1)}, bf16[512,384]{1,0:T(8,128)(2,1)S(1)}, u32[]{:S(2)}, u32[]{:S(2)}) %collective-permute-start.4) | collective-permute-done | bytes 393248 | tf_op jit(solution)/shard_map/ppermute | solution.py:75
  158.7 0.7 fusion.46
  159.4 1.7 add_convert_fusion.1
  161.2 2.3 reshape.128
  163.4 3.4 %copy.183 = bf16[4,64,2,1024]{3,2,0,1:T(2,128)(2,1)} copy(bf16[4,64,2,1024]{3,2,1,0:T(2,128)(2,1)} %reshape.128) | data formatting | bytes 2097152 | tf_op jit(solution)/shard_map/reshape | solution.py:78
  166.8 5.6 %all-to-all-start.1 = ((bf16[64,4,2,1024]{3,2,1,0:T(2,128)(2,1)}), bf16[64,4,2,1024]{3,2,1,0:T(2,128)(2,1)}, u32[]{:S(2)}, u32[]{:S(2)}) async-start(bf16[64,4,2,1024]{3,2,1,0:T(2,128)(2,1)} %bitcast.127), calls=%async_computation.1 | async-start | bytes 2097152 | tf_op jit(solution)/shard_map/all_to_all | solution.py:79
  172.4 20.5 %all-gather.7.cloned.1.call-done = bf16[256,96,128]{2,1,0:T(8,128)(2,1)} async-done(((bf16[64,96,128]{2,1,0:T(8,128)(2,1)}), bf16[256,96,128]{2,1,0:T(8,128)(2,1)}) %all-gather.7.cloned.1.call-update) | async-done | bytes 6291472 | tf_op jit(solution)/shard_map/all_gather | solution.py:53
  192.9 6.7 %fusion.10 = f32[768,384]{1,0:T(8,128)S(1)} fusion(bf16[32,128,384]{2,1,0:T(8,128)(2,1)} %bitcast.143, bf16[768,32,128]{2,1,0:T(8,128)(2,1)} %bitcast.138), kind=kOutput, calls=%fused_computation.15 | convolution fusion | flops 2415919104 | bytes 10616832 | tf_op jit(solution)/shard_map/npak,aku->npu/dot_general | solution.py:57
  199.7 3.6 %fusion.19 = bf16[768,384]{1,0:T(8,128)(2,1)S(1)} fusion(bf16[32,128,384]{2,1,0:T(8,128)(2,1)S(1)} %bitcast.145, bf16[768,32,128]{2,1,0:T(8,128)(2,1)S(1)} %bitcast.139, f32[768,384]{1,0:T(8,128)S(1)} %fusion.10), kind=kOutput, calls=%fused_computation.18 | convolution fusion | flops 2417688576 | bytes 11206656 | tf_op jit(solution)/shard_map/npak,aku->npu/dot_general | solution.py:58
  203.2 2.8 collective-permute-start.7
  206.0 0.9 collective-permute-start.6
  206.8 2.4 collective-permute-start.8
  209.2 1.0 fusion.52
  210.2 10.8 %collective-permute-done.7 = bf16[768,384]{1,0:T(8,128)(2,1)S(1)} collective-permute-done((bf16[768,384]{1,0:T(8,128)(2,1)S(1)}, bf16[768,384]{1,0:T(8,128)(2,1)S(1)}, u32[]{:S(2)}, u32[]{:S(2)}) %collective-permute-start.7) | collective-permute-done | bytes 589856 | tf_op jit(solution)/shard_map/ppermute | solution.py:75
  221.1 1.0 fusion.44
  222.0 10.7 %collective-permute-done.6 = bf16[768,384]{1,0:T(8,128)(2,1)S(1)} collective-permute-done((bf16[768,384]{1,0:T(8,128)(2,1)S(1)}, bf16[768,384]{1,0:T(8,128)(2,1)S(1)}, u32[]{:S(2)}, u32[]{:S(2)}) %collective-permute-start.6) | collective-permute-done | bytes 589856 | tf_op jit(solution)/shard_map/ppermute | solution.py:75
  232.7 1.0 fusion.48
  233.7 2.2 add_convert_fusion
  235.9 5.1 %reshape.130 = bf16[4,64,3,1024]{3,2,1,0:T(4,128)(2,1)} reshape(bf16[768,1024]{1,0:T(8,128)(2,1)} %add_convert_fusion) | data formatting | bytes 3145728 | tf_op jit(solution)/shard_map/reshape | solution.py:78
  241.0 4.8 %copy.143 = bf16[64,4,3,1024]{3,1,2,0:T(4,128)(2,1)} copy(bf16[64,4,3,1024]{3,2,0,1:T(4,128)(2,1)} %bitcast.126) | data formatting | bytes 3145728 | tf_op jit(solution)/shard_map/transpose | solution.py:78
  245.8 6.4 %all-to-all-start.3 = ((bf16[64,4,3,1024]{3,1,2,0:T(4,128)(2,1)}), bf16[64,4,3,1024]{3,1,2,0:T(4,128)(2,1)}, u32[]{:S(2)}, u32[]{:S(2)}) async-start(bf16[64,4,3,1024]{3,1,2,0:T(4,128)(2,1)} %copy.143), calls=%async_computation.3 | async-start | bytes 3145728 | tf_op jit(solution)/shard_map/all_to_all | solution.py:79
  252.2 0.3 select_reduce_fusion.1
  252.6 0.8 copy.132
  253.8 4.4 %fusion.34 = f32[4,128,1024,1]{2,1,3,0:T(8,128)} fusion(bf16[64,4,2,1024]{3,2,1,0:T(2,128)(2,1)} %all-to-all-done.1, f32[4,128,64,2]{1,3,2,0:T(2,128)} %bitcast.129), kind=kOutput, calls=%fused_computation.24 | convolution fusion | flops 402653184 | bytes 3407872 | tf_op jit(solution)/shard_map/rtep,erpf->rtf/dot_general | solution.py:83
  258.2 34.0 %all-to-all-done.3 = bf16[64,4,3,1024]{3,1,2,0:T(4,128)(2,1)} async-done(((bf16[64,4,3,1024]{3,1,2,0:T(4,128)(2,1)}), bf16[64,4,3,1024]{3,1,2,0:T(4,128)(2,1)}, u32[]{:S(2)}, u32[]{:S(2)}) %all-to-all-start.3) | async-done | bytes 1572896 | tf_op jit(solution)/shard_map/all_to_all | solution.py:79
  292.2 3.6 %fusion.8 = bf16[4,128,1024]{2,1,0:T(8,128)(2,1)S(1)} fusion(f32[4,128,1024,1]{2,1,3,0:T(8,128)} %fusion.34, bf16[64,4,3,1024]{3,1,2,0:T(4,128)(2,1)} %all-to-all-done.3, f32[4,128,64,3]{1,0,3,2:T(4,128)S(1)} %bitcast.128), kind=kOutput, calls=%fused_computation.12 | convolution fusion | flops 605028352 | bytes 5111808 | tf_op jit(solution)/shard_map/rtep,erpf->rtf/dot_general | solution.py:83
  295.8 17.4 %all_to_all.27 = bf16[4,128,1024]{2,1,0:T(8,128)(2,1)S(1)} all-to-all(bf16[4,128,1024]{2,1,0:T(8,128)(2,1)S(1)} %fusion.8), channel_id=1, replica_groups=mesh['row'=4,'col'=64] {'row'}, dimensions={0} | all-to-all | bytes 2097152 | tf_op jit(solution)/shard_map/all_to_all | solution.py:88
  313.3 1.0 pad_maximum_fusion
  (53 shorter events, 2.2 us)
Async XLA Ops:
  6.5 120.2 %copy-start = (bf16[1,1536,1024]{2,1,0:T(8,128)(2,1)S(1)}, bf16[1,1536,1024]{2,1,0:T(8,128)(2,1)}, u32[]{:S(2)}) copy-start(bf16[1,1536,1024]{2,1,0:T(8,128)(2,1)} %param.11) | copy-start | bytes 9437188
  6.5 107.1 %all-gather.5.cloned.1.call-start = ((), (), s32[]{:S(2)}) async-start(), calls=%async_computation.5 | async-start | bytes 5242880 | tf_op jit(solution)/shard_map/all_gather | solution.py:53
  12.6 43.3 %copy-start.1 = (f32[128,2]{0,1:T(2,128)S(1)}, f32[128,2]{0,1:T(2,128)}, u32[]{:S(2)}) copy-start(f32[128,2]{0,1:T(2,128)} %param.8) | copy-start | bytes 3076
  55.9 137.1 %all-gather.7.cloned.1.call-start = ((), (), s32[]{:S(2)}) async-start(), calls=%async_computation.6 | async-start | bytes 7864320 | tf_op jit(solution)/shard_map/all_gather | solution.py:53
  56.0 11.8 %collective-permute-start = (f32[128,4]{0,1:T(4,128)S(1)}, f32[128,4]{0,1:T(4,128)S(1)}, u32[]{:S(2)}, u32[]{:S(2)}) collective-permute-start(f32[128,4]{0,1:T(4,128)S(1)} %pad_maximum_fusion.1), channel_id=1, source_target_pairs={{0,192},{64,0},{128,64},{192,128},{1,193},{65,1},{129,65},{193,129... | collective-permute-start | bytes 6152 | tf_op jit(solution)/shard_map/ppermute | solution.py:30
  59.0 8.7 %collective-permute-start.1 = (f32[128,4]{0,1:T(4,128)S(1)}, f32[128,4]{0,1:T(4,128)S(1)}, u32[]{:S(2)}, u32[]{:S(2)}) collective-permute-start(f32[128,4]{0,1:T(4,128)S(1)} %pad_maximum_fusion.1), channel_id=1, source_target_pairs={{0,128},{64,192},{128,0},{192,64},{1,129},{65,193},{129,1},{193,65... | collective-permute-start | bytes 6152 | tf_op jit(solution)/shard_map/ppermute | solution.py:30
  59.7 8.1 %collective-permute-start.2 = (f32[128,4]{0,1:T(4,128)S(1)}, f32[128,4]{0,1:T(4,128)S(1)}, u32[]{:S(2)}, u32[]{:S(2)}) collective-permute-start(f32[128,4]{0,1:T(4,128)S(1)} %pad_maximum_fusion.1), channel_id=1, source_target_pairs={{0,64},{64,128},{128,192},{192,0},{1,65},{65,129},{129,193},{193,1... | collective-permute-start | bytes 6152 | tf_op jit(solution)/shard_map/ppermute | solution.py:30
  113.6 5.7 %copy-start.3 = (bf16[256,64,128]{2,1,0:T(8,128)(2,1)S(1)}, bf16[256,64,128]{2,1,0:T(8,128)(2,1)}, u32[]{:S(2)}) copy-start(bf16[256,64,128]{2,1,0:T(8,128)(2,1)} %all-gather.5.cloned.1.call-done) | copy-start | bytes 12582916
  113.6 5.7 %copy-start.4 = (bf16[1,4096,384]{2,1,0:T(8,128)(2,1)S(1)}, bf16[1,4096,384]{2,1,0:T(8,128)(2,1)}, u32[]{:S(2)}) copy-start(bf16[1,4096,384]{2,1,0:T(8,128)(2,1)} %param.10) | copy-start | bytes 9437188
  121.7 21.5 %collective-permute-start.3 = (bf16[512,384]{1,0:T(8,128)(2,1)S(1)}, bf16[512,384]{1,0:T(8,128)(2,1)}, u32[]{:S(2)}, u32[]{:S(2)}) collective-permute-start(bf16[512,384]{1,0:T(8,128)(2,1)S(1)} %fusion.31), channel_id=1, source_target_pairs={{0,64},{64,128},{128,192},{192,0},{1,65},{65,129},{129,193},{193,1... | collective-permute-start | bytes 1179656 | tf_op jit(solution)/shard_map/ppermute | solution.py:75
  123.7 35.0 %collective-permute-start.4 = (bf16[512,384]{1,0:T(8,128)(2,1)S(1)}, bf16[512,384]{1,0:T(8,128)(2,1)S(1)}, u32[]{:S(2)}, u32[]{:S(2)}) collective-permute-start(bf16[512,384]{1,0:T(8,128)(2,1)S(1)} %fusion.31), channel_id=1, source_target_pairs={{0,128},{64,192},{128,0},{192,64},{1,129},{65,193},{129,1},{193,65... | collective-permute-start | bytes 1179656 | tf_op jit(solution)/shard_map/ppermute | solution.py:75
  125.5 34.0 %collective-permute-start.5 = (bf16[512,384]{1,0:T(8,128)(2,1)S(1)}, bf16[512,384]{1,0:T(8,128)(2,1)S(1)}, u32[]{:S(2)}, u32[]{:S(2)}) collective-permute-start(bf16[512,384]{1,0:T(8,128)(2,1)S(1)} %fusion.31), channel_id=1, source_target_pairs={{0,192},{64,0},{128,64},{192,128},{1,193},{65,1},{129,65},{193,129... | collective-permute-start | bytes 1179656 | tf_op jit(solution)/shard_map/ppermute | solution.py:75
  166.8 79.0 %all-to-all-start.1 = ((bf16[64,4,2,1024]{3,2,1,0:T(2,128)(2,1)}), bf16[64,4,2,1024]{3,2,1,0:T(2,128)(2,1)}, u32[]{:S(2)}, u32[]{:S(2)}) async-start(bf16[64,4,2,1024]{3,2,1,0:T(2,128)(2,1)} %bitcast.127), calls=%async_computation.1 | async-start | bytes 2097152 | tf_op jit(solution)/shard_map/all_to_all | solution.py:79
  192.9 6.7 %copy-start.2 = (bf16[256,96,128]{2,1,0:T(8,128)(2,1)S(1)}, bf16[256,96,128]{2,1,0:T(8,128)(2,1)}, u32[]{:S(2)}) copy-start(bf16[256,96,128]{2,1,0:T(8,128)(2,1)} %all-gather.7.cloned.1.call-done) | copy-start | bytes 18874372
  192.9 6.7 %copy-start.5 = (bf16[1,4096,384]{2,1,0:T(8,128)(2,1)S(1)}, bf16[1,4096,384]{2,1,0:T(8,128)(2,1)}, u32[]{:S(2)}) copy-start(bf16[1,4096,384]{2,1,0:T(8,128)(2,1)} %param.10) | copy-start | bytes 9437188
  203.2 17.8 %collective-permute-start.7 = (bf16[768,384]{1,0:T(8,128)(2,1)S(1)}, bf16[768,384]{1,0:T(8,128)(2,1)S(1)}, u32[]{:S(2)}, u32[]{:S(2)}) collective-permute-start(bf16[768,384]{1,0:T(8,128)(2,1)S(1)} %fusion.19), channel_id=1, source_target_pairs={{0,128},{64,192},{128,0},{192,64},{1,129},{65,193},{129,1},{193,65... | collective-permute-start | bytes 1769480 | tf_op jit(solution)/shard_map/ppermute | solution.py:75
  206.0 26.7 %collective-permute-start.6 = (bf16[768,384]{1,0:T(8,128)(2,1)S(1)}, bf16[768,384]{1,0:T(8,128)(2,1)S(1)}, u32[]{:S(2)}, u32[]{:S(2)}) collective-permute-start(bf16[768,384]{1,0:T(8,128)(2,1)S(1)} %fusion.19), channel_id=1, source_target_pairs={{0,64},{64,128},{128,192},{192,0},{1,65},{65,129},{129,193},{193,1... | collective-permute-start | bytes 1769480 | tf_op jit(solution)/shard_map/ppermute | solution.py:75
  206.8 26.9 %collective-permute-start.8 = (bf16[768,384]{1,0:T(8,128)(2,1)S(1)}, bf16[768,384]{1,0:T(8,128)(2,1)S(1)}, u32[]{:S(2)}, u32[]{:S(2)}) collective-permute-start(bf16[768,384]{1,0:T(8,128)(2,1)S(1)} %fusion.19), channel_id=1, source_target_pairs={{0,192},{64,0},{128,64},{192,128},{1,193},{65,1},{129,65},{193,129... | collective-permute-start | bytes 1769480 | tf_op jit(solution)/shard_map/ppermute | solution.py:75
  245.8 46.4 %all-to-all-start.3 = ((bf16[64,4,3,1024]{3,1,2,0:T(4,128)(2,1)}), bf16[64,4,3,1024]{3,1,2,0:T(4,128)(2,1)}, u32[]{:S(2)}, u32[]{:S(2)}) async-start(bf16[64,4,3,1024]{3,1,2,0:T(4,128)(2,1)} %copy.143), calls=%async_computation.3 | async-start | bytes 3145728 | tf_op jit(solution)/shard_map/all_to_all | solution.py:79
Sparse Core Ops, SparseCore 0:
  56.0 47.4 all-gather.4
  113.7 79.1 all-gather.6
